TPU v7x, 128 devices: a whole 4x4x4 slice. The times are simulated.
128 devices in a mesh: req: 16 (over y, x), kv: 8 (over z, core).
Axes of the slice: x: 4, y: 4, z: 4, core: 2. Of those that a mesh axis runs over, the one named last changes fastest.
Arguments:
- residual: bfloat16 [16384, 2560], P(('req', 'kv')), may hold values from -6 to 6
- queries: bfloat16 [16384, 2560], P(('req', 'kv')), may hold values from -180 to 180
- suffix_kv: bfloat16 [16384, 1280], P(('req', 'kv')), may hold values from -6 to 6
- prefix_kv: bfloat16 [64, 128, 1280], P('kv'), may hold values from -6 to 6
- page_table: int32 [64], P('kv'), may hold values from 0 to 63, each once
- suffix_lens: int32 [16, 4], P('req'), may hold values from 1 to 512, 1024 in all within a row
- w_out: bfloat16 [2560, 2560], replicated, may hold values from -0.125 to 0.125
- norm_gain: float32 [2560], replicated, may hold values from 0.1 to 1.9
- w_gate: bfloat16 [2560, 7168], P(None, 'req'), may hold values from -0.125 to 0.125
- w_up: bfloat16 [2560, 7168], P(None, 'req'), may hold values from -0.125 to 0.125
- w_down: bfloat16 [7168, 2560], P('req'), may hold values from -0.0625 to 0.0625
Outputs:
- attended: bfloat16 [16384, 2560], P(('req', 'kv'))
- layer_out: bfloat16 [16384, 2560], P(('req', 'kv'))
Inputs may be any that keep to these rules, and one draw needn't show every extreme that they name: `page_table`: each logical page number appears once. `suffix_lens`: each group's lengths sum to 1024.
All inputs are finite; a program needn't handle non-finite values.
Results may differ from a plain program's by a relative error of at most 0.02.
Values may be sent and summed in bfloat16 or wider, within the bound.
No kernel may reach another device: no remote copies, remote signals or barrier semaphores. Data moves between devices by JAX's collectives and lax.ppermute only.
A program may use at most 192 MiB of HBM per device.

v0:
```python
import math

import jax
import jax.numpy as jnp
from jax import lax
from jax.sharding import PartitionSpec as P

QH = 32
KVH = 8
HD = 80
PREFIX = 8192


THETA = 1000000.0
NEG = -1e30


def rotate(values, positions):
    half_dim = values.shape[-1] // 2
    exponent = jnp.arange(half_dim, dtype=jnp.float32) * (2.0 / values.shape[-1])
    inverse = jnp.exp(-exponent * math.log(THETA))
    angles = positions.astype(jnp.float32)[:, None] * inverse[None, :]
    cosine = jnp.cos(angles)[:, None, :]
    sine_part = jnp.sin(angles)[:, None, :]
    first_half = values[..., :half_dim]
    second = values[..., half_dim:]
    return jnp.concatenate(
        [first_half * cosine - second * sine_part, second * cosine + first_half * sine_part],
        axis=-1,
    )


def request_info(request_lens, tok_index):
    request_ends = jnp.cumsum(request_lens)
    passed = tok_index[:, None] >= request_ends[None, :]
    request_of = jnp.sum(passed.astype(jnp.int32), axis=1)
    request_start = jnp.sum(jnp.where(passed, request_lens[None, :], 0), axis=1)
    return (request_of, request_start)


def initial_state(tok_count, kv_heads, per_group, head_dim):
    return (
        jnp.full((tok_count, kv_heads, per_group), NEG, jnp.float32),
        jnp.zeros((tok_count, kv_heads, per_group), jnp.float32),
        jnp.zeros((tok_count, kv_heads, per_group, head_dim), jnp.float32),
    )


def absorb(running, rotated_q, key_rows, value_rows, key_mask):
    running_max, denom, accumulated = running
    score_scale = rotated_q.shape[-1] ** (-0.5)
    scores = (
        jnp.einsum("tkgd,nkd->tkgn", rotated_q, key_rows, preferred_element_type=jnp.float32)
        * score_scale
    )
    if key_mask is not None:
        scores = jnp.where(key_mask[:, None, None, :], scores, NEG)
    new_max = jnp.maximum(running_max, jnp.max(scores, axis=-1))
    weights = jnp.exp(scores - new_max[..., None])
    if key_mask is not None:
        weights = jnp.where(key_mask[:, None, None, :], weights, 0.0)
    factor = jnp.exp(running_max - new_max)
    denom = denom * factor + jnp.sum(weights, axis=-1)
    accumulated = accumulated * factor[..., None] + jnp.einsum(
        "tkgn,nkd->tkgd",
        weights.astype(jnp.bfloat16),
        value_rows,
        preferred_element_type=jnp.float32,
    )
    return (new_max, denom, accumulated)


def sweep_keys(running, rotated_q, key_rows, value_rows, mask_maker):
    key_count = key_rows.shape[0]
    block_len = math.gcd(key_count, 1024)
    block_count = key_count // block_len
    if block_count == 1:
        key_mask = mask_maker(0, key_count)
        return absorb(running, rotated_q, key_rows, value_rows, key_mask)
    key_blocks = key_rows.reshape((block_count, block_len) + key_rows.shape[1:])
    value_blocks = value_rows.reshape((block_count, block_len) + value_rows.shape[1:])
    offsets = jnp.arange(block_count, dtype=jnp.int32) * block_len

    def scan_step(carried, inputs):
        key_part, value_part, offset = inputs
        key_mask = None
        return (absorb(carried, rotated_q, key_part, value_part, key_mask), None)

    running, unused = lax.scan(scan_step, running, (key_blocks, value_blocks, offsets))
    return running


def body(
    residual,
    queries,
    suffix_kv,
    prefix_kv,
    page_table,
    suffix_lens,
    w_out,
    norm_gain,
    w_gate,
    w_up,
    w_down,
):
    tok_rows = queries.shape[0]
    kv_width = KVH * HD
    per_group = QH // KVH
    tok_index = lax.axis_index("kv") * tok_rows + jnp.arange(tok_rows, dtype=jnp.int32)
    request_lens = suffix_lens[0]
    request_of, request_start = request_info(request_lens, tok_index)
    positions = PREFIX + tok_index - request_start
    rotated_q = rotate(queries.astype(jnp.float32).reshape(tok_rows, QH, HD), positions).astype(
        jnp.bfloat16
    )
    rotated_q = rotated_q.reshape(tok_rows, KVH, per_group, HD)
    suf_keys = rotate(
        suffix_kv[:, :kv_width].astype(jnp.float32).reshape(tok_rows, KVH, HD), positions
    ).astype(jnp.bfloat16)
    local_kv = jnp.concatenate(
        [suf_keys.reshape(tok_rows, kv_width), suffix_kv[:, kv_width:]], axis=1
    )
    page_count = prefix_kv.shape[0]
    page_size = prefix_kv.shape[1]
    page_pos = (
        page_table[:, None] * page_size + jnp.arange(page_size, dtype=jnp.int32)[None, :]
    ).reshape(-1)
    page_keys = rotate(
        prefix_kv[:, :, :kv_width].astype(jnp.float32).reshape(page_count * page_size, KVH, HD),
        page_pos,
    ).astype(jnp.bfloat16)
    page_block = jnp.concatenate(
        [page_keys.reshape(page_count, page_size, kv_width), prefix_kv[:, :, kv_width:]], axis=2
    )

    def suffix_step(running, shard_piece):
        key_count = shard_piece.shape[0]
        key_index = jnp.arange(key_count, dtype=jnp.int32)
        key_request, unused = request_info(request_lens, key_index)

        def mask_maker(offset, span_len):
            return (key_request[None, :] == request_of[:, None]) & (
                key_index[None, :] <= tok_index[:, None]
            )

        return sweep_keys(
            running,
            rotated_q,
            shard_piece[:, :kv_width].reshape(key_count, KVH, HD),
            shard_piece[:, kv_width:].reshape(key_count, KVH, HD),
            mask_maker,
        )

    running = suffix_step(
        initial_state(tok_rows, KVH, per_group, HD),
        lax.all_gather(local_kv, "kv", axis=0, tiled=True),
    )
    shard_piece = lax.all_gather(page_block, "kv", axis=0, tiled=True)
    key_count = shard_piece.shape[0] * shard_piece.shape[1]
    flat_rows = shard_piece.reshape(key_count, 2 * kv_width)
    running = sweep_keys(
        running,
        rotated_q,
        flat_rows[:, :kv_width].reshape(key_count, KVH, HD),
        flat_rows[:, kv_width:].reshape(key_count, KVH, HD),
        None,
    )
    final_max, denom, accumulated = running
    attended = (accumulated / denom[..., None]).astype(jnp.bfloat16).reshape(tok_rows, QH * HD)
    mixed_sum = residual.astype(jnp.float32) + jnp.dot(
        attended, w_out, preferred_element_type=jnp.float32
    )
    stream_wide = mixed_sum.astype(jnp.bfloat16).astype(jnp.float32)
    normed = (
        stream_wide
        * lax.rsqrt(jnp.mean(stream_wide * stream_wide, axis=1, keepdims=True) + 1e-05)
        * norm_gain
    ).astype(jnp.bfloat16)
    shard_piece = lax.all_gather(normed, "req", axis=0, tiled=True)
    gate_proj = jnp.dot(shard_piece, w_gate, preferred_element_type=jnp.float32)
    up_proj = jnp.dot(shard_piece, w_up, preferred_element_type=jnp.float32)
    activated = (jax.nn.silu(gate_proj) * up_proj).astype(jnp.bfloat16)
    summed = lax.psum_scatter(
        jnp.dot(activated, w_down, preferred_element_type=jnp.float32).astype(jnp.bfloat16),
        "req",
        scatter_dimension=0,
        tiled=True,
    ).astype(jnp.float32)
    layer_out = (stream_wide + summed).astype(jnp.bfloat16)
    return (attended, layer_out)


def solution(mesh):
    in_specs = (
        P(("req", "kv"), None),
        P(("req", "kv"), None),
        P(("req", "kv"), None),
        P("kv", None, None),
        P("kv"),
        P("req", None),
        P(),
        P(),
        P(None, "req"),
        P(None, "req"),
        P("req", None),
    )
    out_specs = (P(("req", "kv"), None), P(("req", "kv"), None))
    return jax.shard_map(body, mesh=mesh, in_specs=in_specs, out_specs=out_specs, check_vma=False)
```

profile of v0, /device:TPU:0, one launch (start us, length us, event | category | flops | bytes accessed | tf_op | source)
XLA Modules:
  0.0 702.2 jit_solution(10777696697320531535)
XLA Ops:
  7.3 1.0 reduce-window.8
  8.2 0.7 fusion.37
  9.0 1.0 fusion.47
  10.6 0.7 pad_maximum_fusion.3
  11.4 4.0 slice_convert_fusion
  15.5 3.4 copy.37
  18.9 3.8 reshape.275
  22.7 0.6 multiply_cosine_fusion
  23.4 2.3 subtract_convert_fusion
  25.8 1.4 copy.51
  27.2 2.8 copy.50
  30.1 4.0 pad_maximum_fusion
  34.1 0.3 all-gather.8.cloned.1.call-start
  34.4 1.4 copy.35
  36.0 0.2 subtract_convert_fusion.1
  36.2 0.7 copy-done.2
  37.0 0.2 fusion.36
  37.2 5.9 all-gather.4.cloned.1.call-done
  43.2 2.0 fusion.46
  45.2 2.6 fusion.21
  47.8 4.1 fusion.23
  51.9 4.7 fusion.33
  56.6 97.1 %all-gather.6.cloned.1.call-done = bf16[64,128,1280]{1,0,2:T(8,128)(2,1)} async-done(((bf16[8,128,1280]{1,0,2:T(8,128)(2,1)}), bf16[64,128,1280]{1,0,2:T(8,128)(2,1)}) %all-gather.6.cloned.1.call-update) | async-done | bytes 20971536 | tf_op jit(solution)/shard_map/all_gather | solution.py:158
  153.7 22.1 %copy.56 = bf16[160,8,64,128]{3,1,2,0:T(8,128)(2,1)S(1)} copy(bf16[160,8,64,128]{3,2,1,0:T(8,128)(2,1)} %bitcast.144) | data formatting | bytes 41943040
  175.8 8.1 %fusion.45 = (bf16[8192,640]{0,1:T(8,128)(2,1)}, bf16[8192,640]{0,1:T(8,128)(2,1)}) fusion(bf16[8192,1280]{0,1:T(8,128)(2,1)S(1)} %bitcast.139), kind=kLoop, calls=%fused_computation.78 | loop fusion | bytes 41943040 | tf_op jit(solution)/shard_map/slice | solution.py:165
  184.0 20.3 %copy.53 = bf16[80,8,8,1024]{3,2,1,0:T(8,128)(2,1)} copy(bf16[80,8,8,1024]{3,1,2,0:T(8,128)(2,1)} %bitcast.141) | data formatting | bytes 20971520
  204.2 13.9 %copy.39 = bf16[8,1024,8,80]{1,3,2,0:T(8,128)(2,1)} copy(bf16[8,1024,8,80]{1,0,3,2:T(8,128)(2,1)} %bitcast.142) | data formatting | bytes 20971520 | tf_op jit(solution)/shard_map/while | solution.py:89
  218.1 20.3 %copy.54 = bf16[80,8,8,1024]{3,2,1,0:T(8,128)(2,1)} copy(bf16[80,8,8,1024]{3,1,2,0:T(8,128)(2,1)} %bitcast.140) | data formatting | bytes 20971520
  238.4 14.2 %copy.40 = bf16[8,1024,8,80]{1,3,2,0:T(8,128)(2,1)} copy(bf16[8,1024,8,80]{1,0,3,2:T(8,128)(2,1)} %bitcast.143) | data formatting | bytes 20971520 | tf_op jit(solution)/shard_map/while | solution.py:89
  252.6 230.2 %while.14 = (s32[]{:T(128)}, f32[128,8,4]{0,2,1:T(4,128)S(1)}, f32[128,8,4]{0,2,1:T(4,128)S(1)}, f32[128,8,4,80]{0,3,2,1:T(8,128)}, bf16[8,1024,8,80]{1,3,2,0:T(...) while((s32[]{:T(128)}, f32[128,8,4]{0,2,1:T(4,128)S(1)}, ...), condition=%wide.region_9.10_spmd, body=%wide.region_6.9_spmd.sunk | while | flops 1376395264 | bytes 56493140 | solution.py:89
  252.6 9.5 %bitcast_reduce_fusion.2 = (f32[128,8,4]{0,2,1:T(4,128)S(1)}, f32[8,1024,128,4]{2,1,3,0:T(8,128)}) fusion(bf16[128,8,4,80]{0,3,2,1:T(8,128)(2,1)S(1)} %get-tuple-element.180, bf16[8,1024,8,80]{1,3,2,0:T(8,128)(2,1)} %get-tuple-element.179, s32[]{:T(128)} %get-tuple-element.167), kind=kOutput, calls=%fused_computation.1.clone.1 | convolution fusion | flops 679473152 | bytes 18760192 | tf_op jit(solution)/shard_map/while/body/eval_jaxpr/tkgd,nkd->tkgn/dot_general | solution.py:53
  262.2 8.7 %fusion.67 = f32[128,8,4]{0,2,1:T(4,128)S(1)} fusion(f32[8,1024,128,4]{2,1,3,0:T(8,128)} %get-tuple-element.156, f32[128,8,4]{0,2,1:T(4,128)S(1)} %max.4), kind=kLoop, calls=%fused_computation.4.clone.1 | loop fusion | flops 12578816 | bytes 16809984 | tf_op jit(solution)/shard_map/while/body/eval_jaxpr/reduce_sum | solution.py:63
  270.9 10.5 %fusion.68 = f32[128,8,4,80]{0,3,2,1:T(8,128)} fusion(f32[8,1024,128,4]{2,1,3,0:T(8,128)} %get-tuple-element.156, f32[128,8,4]{0,2,1:T(4,128)S(1)} %max.4, bf16[8,1024,8,80]{1,3,2,0:T(8,128)(2,1)} %get-tuple-element.181, s32[]{:T(128)} %get-tuple-element.167, f32[128,8,4,80]{0,3,2,1:T(8,128)} %get-tuple-element.170, f32[128,8,4]{0,2,1:T(4,128)S(1)} %bitcast.157), kind=kOutput, calls=%fused_computation.9.clone.1 | convolution fusion | flops 684326912 | bytes 20742656 | tf_op jit(solution)/shard_map/while/body/eval_jaxpr/tkgn,nkd->tkgd/dot_general | solution.py:64
  281.4 9.5 %bitcast_reduce_fusion.2 = (f32[128,8,4]{0,2,1:T(4,128)S(1)}, f32[8,1024,128,4]{2,1,3,0:T(8,128)}) fusion(bf16[128,8,4,80]{0,3,2,1:T(8,128)(2,1)S(1)} %get-tuple-element.180, bf16[8,1024,8,80]{1,3,2,0:T(8,128)(2,1)} %get-tuple-element.179, s32[]{:T(128)} %get-tuple-element.167), kind=kOutput, calls=%fused_computation.1.clone.1 | convolution fusion | flops 679473152 | bytes 18760192 | tf_op jit(solution)/shard_map/while/body/eval_jaxpr/tkgd,nkd->tkgn/dot_general | solution.py:53
  290.9 8.7 %fusion.67 = f32[128,8,4]{0,2,1:T(4,128)S(1)} fusion(f32[8,1024,128,4]{2,1,3,0:T(8,128)} %get-tuple-element.156, f32[128,8,4]{0,2,1:T(4,128)S(1)} %max.4), kind=kLoop, calls=%fused_computation.4.clone.1 | loop fusion | flops 12578816 | bytes 16809984 | tf_op jit(solution)/shard_map/while/body/eval_jaxpr/reduce_sum | solution.py:63
  299.7 10.5 %fusion.68 = f32[128,8,4,80]{0,3,2,1:T(8,128)} fusion(f32[8,1024,128,4]{2,1,3,0:T(8,128)} %get-tuple-element.156, f32[128,8,4]{0,2,1:T(4,128)S(1)} %max.4, bf16[8,1024,8,80]{1,3,2,0:T(8,128)(2,1)} %get-tuple-element.181, s32[]{:T(128)} %get-tuple-element.167, f32[128,8,4,80]{0,3,2,1:T(8,128)} %get-tuple-element.170, f32[128,8,4]{0,2,1:T(4,128)S(1)} %bitcast.157), kind=kOutput, calls=%fused_computation.9.clone.1 | convolution fusion | flops 684326912 | bytes 20742656 | tf_op jit(solution)/shard_map/while/body/eval_jaxpr/tkgn,nkd->tkgd/dot_general | solution.py:64
  310.1 9.5 %bitcast_reduce_fusion.2 = (f32[128,8,4]{0,2,1:T(4,128)S(1)}, f32[8,1024,128,4]{2,1,3,0:T(8,128)}) fusion(bf16[128,8,4,80]{0,3,2,1:T(8,128)(2,1)S(1)} %get-tuple-element.180, bf16[8,1024,8,80]{1,3,2,0:T(8,128)(2,1)} %get-tuple-element.179, s32[]{:T(128)} %get-tuple-element.167), kind=kOutput, calls=%fused_computation.1.clone.1 | convolution fusion | flops 679473152 | bytes 18760192 | tf_op jit(solution)/shard_map/while/body/eval_jaxpr/tkgd,nkd->tkgn/dot_general | solution.py:53
  319.7 8.7 %fusion.67 = f32[128,8,4]{0,2,1:T(4,128)S(1)} fusion(f32[8,1024,128,4]{2,1,3,0:T(8,128)} %get-tuple-element.156, f32[128,8,4]{0,2,1:T(4,128)S(1)} %max.4), kind=kLoop, calls=%fused_computation.4.clone.1 | loop fusion | flops 12578816 | bytes 16809984 | tf_op jit(solution)/shard_map/while/body/eval_jaxpr/reduce_sum | solution.py:63
  328.4 10.5 %fusion.68 = f32[128,8,4,80]{0,3,2,1:T(8,128)} fusion(f32[8,1024,128,4]{2,1,3,0:T(8,128)} %get-tuple-element.156, f32[128,8,4]{0,2,1:T(4,128)S(1)} %max.4, bf16[8,1024,8,80]{1,3,2,0:T(8,128)(2,1)} %get-tuple-element.181, s32[]{:T(128)} %get-tuple-element.167, f32[128,8,4,80]{0,3,2,1:T(8,128)} %get-tuple-element.170, f32[128,8,4]{0,2,1:T(4,128)S(1)} %bitcast.157), kind=kOutput, calls=%fused_computation.9.clone.1 | convolution fusion | flops 684326912 | bytes 20742656 | tf_op jit(solution)/shard_map/while/body/eval_jaxpr/tkgn,nkd->tkgd/dot_general | solution.py:64
  338.9 9.5 %bitcast_reduce_fusion.2 = (f32[128,8,4]{0,2,1:T(4,128)S(1)}, f32[8,1024,128,4]{2,1,3,0:T(8,128)}) fusion(bf16[128,8,4,80]{0,3,2,1:T(8,128)(2,1)S(1)} %get-tuple-element.180, bf16[8,1024,8,80]{1,3,2,0:T(8,128)(2,1)} %get-tuple-element.179, s32[]{:T(128)} %get-tuple-element.167), kind=kOutput, calls=%fused_computation.1.clone.1 | convolution fusion | flops 679473152 | bytes 18760192 | tf_op jit(solution)/shard_map/while/body/eval_jaxpr/tkgd,nkd->tkgn/dot_general | solution.py:53
  348.5 8.7 %fusion.67 = f32[128,8,4]{0,2,1:T(4,128)S(1)} fusion(f32[8,1024,128,4]{2,1,3,0:T(8,128)} %get-tuple-element.156, f32[128,8,4]{0,2,1:T(4,128)S(1)} %max.4), kind=kLoop, calls=%fused_computation.4.clone.1 | loop fusion | flops 12578816 | bytes 16809984 | tf_op jit(solution)/shard_map/while/body/eval_jaxpr/reduce_sum | solution.py:63
  357.2 10.5 %fusion.68 = f32[128,8,4,80]{0,3,2,1:T(8,128)} fusion(f32[8,1024,128,4]{2,1,3,0:T(8,128)} %get-tuple-element.156, f32[128,8,4]{0,2,1:T(4,128)S(1)} %max.4, bf16[8,1024,8,80]{1,3,2,0:T(8,128)(2,1)} %get-tuple-element.181, s32[]{:T(128)} %get-tuple-element.167, f32[128,8,4,80]{0,3,2,1:T(8,128)} %get-tuple-element.170, f32[128,8,4]{0,2,1:T(4,128)S(1)} %bitcast.157), kind=kOutput, calls=%fused_computation.9.clone.1 | convolution fusion | flops 684326912 | bytes 20742656 | tf_op jit(solution)/shard_map/while/body/eval_jaxpr/tkgn,nkd->tkgd/dot_general | solution.py:64
  367.7 9.5 %bitcast_reduce_fusion.2 = (f32[128,8,4]{0,2,1:T(4,128)S(1)}, f32[8,1024,128,4]{2,1,3,0:T(8,128)}) fusion(bf16[128,8,4,80]{0,3,2,1:T(8,128)(2,1)S(1)} %get-tuple-element.180, bf16[8,1024,8,80]{1,3,2,0:T(8,128)(2,1)} %get-tuple-element.179, s32[]{:T(128)} %get-tuple-element.167), kind=kOutput, calls=%fused_computation.1.clone.1 | convolution fusion | flops 679473152 | bytes 18760192 | tf_op jit(solution)/shard_map/while/body/eval_jaxpr/tkgd,nkd->tkgn/dot_general | solution.py:53
  377.2 8.7 %fusion.67 = f32[128,8,4]{0,2,1:T(4,128)S(1)} fusion(f32[8,1024,128,4]{2,1,3,0:T(8,128)} %get-tuple-element.156, f32[128,8,4]{0,2,1:T(4,128)S(1)} %max.4), kind=kLoop, calls=%fused_computation.4.clone.1 | loop fusion | flops 12578816 | bytes 16809984 | tf_op jit(solution)/shard_map/while/body/eval_jaxpr/reduce_sum | solution.py:63
  385.9 10.5 %fusion.68 = f32[128,8,4,80]{0,3,2,1:T(8,128)} fusion(f32[8,1024,128,4]{2,1,3,0:T(8,128)} %get-tuple-element.156, f32[128,8,4]{0,2,1:T(4,128)S(1)} %max.4, bf16[8,1024,8,80]{1,3,2,0:T(8,128)(2,1)} %get-tuple-element.181, s32[]{:T(128)} %get-tuple-element.167, f32[128,8,4,80]{0,3,2,1:T(8,128)} %get-tuple-element.170, f32[128,8,4]{0,2,1:T(4,128)S(1)} %bitcast.157), kind=kOutput, calls=%fused_computation.9.clone.1 | convolution fusion | flops 684326912 | bytes 20742656 | tf_op jit(solution)/shard_map/while/body/eval_jaxpr/tkgn,nkd->tkgd/dot_general | solution.py:64
  396.4 9.5 %bitcast_reduce_fusion.2 = (f32[128,8,4]{0,2,1:T(4,128)S(1)}, f32[8,1024,128,4]{2,1,3,0:T(8,128)}) fusion(bf16[128,8,4,80]{0,3,2,1:T(8,128)(2,1)S(1)} %get-tuple-element.180, bf16[8,1024,8,80]{1,3,2,0:T(8,128)(2,1)} %get-tuple-element.179, s32[]{:T(128)} %get-tuple-element.167), kind=kOutput, calls=%fused_computation.1.clone.1 | convolution fusion | flops 679473152 | bytes 18760192 | tf_op jit(solution)/shard_map/while/body/eval_jaxpr/tkgd,nkd->tkgn/dot_general | solution.py:53
  406.0 8.7 %fusion.67 = f32[128,8,4]{0,2,1:T(4,128)S(1)} fusion(f32[8,1024,128,4]{2,1,3,0:T(8,128)} %get-tuple-element.156, f32[128,8,4]{0,2,1:T(4,128)S(1)} %max.4), kind=kLoop, calls=%fused_computation.4.clone.1 | loop fusion | flops 12578816 | bytes 16809984 | tf_op jit(solution)/shard_map/while/body/eval_jaxpr/reduce_sum | solution.py:63
  414.7 10.5 %fusion.68 = f32[128,8,4,80]{0,3,2,1:T(8,128)} fusion(f32[8,1024,128,4]{2,1,3,0:T(8,128)} %get-tuple-element.156, f32[128,8,4]{0,2,1:T(4,128)S(1)} %max.4, bf16[8,1024,8,80]{1,3,2,0:T(8,128)(2,1)} %get-tuple-element.181, s32[]{:T(128)} %get-tuple-element.167, f32[128,8,4,80]{0,3,2,1:T(8,128)} %get-tuple-element.170, f32[128,8,4]{0,2,1:T(4,128)S(1)} %bitcast.157), kind=kOutput, calls=%fused_computation.9.clone.1 | convolution fusion | flops 684326912 | bytes 20742656 | tf_op jit(solution)/shard_map/while/body/eval_jaxpr/tkgn,nkd->tkgd/dot_general | solution.py:64
  425.2 9.5 %bitcast_reduce_fusion.2 = (f32[128,8,4]{0,2,1:T(4,128)S(1)}, f32[8,1024,128,4]{2,1,3,0:T(8,128)}) fusion(bf16[128,8,4,80]{0,3,2,1:T(8,128)(2,1)S(1)} %get-tuple-element.180, bf16[8,1024,8,80]{1,3,2,0:T(8,128)(2,1)} %get-tuple-element.179, s32[]{:T(128)} %get-tuple-element.167), kind=kOutput, calls=%fused_computation.1.clone.1 | convolution fusion | flops 679473152 | bytes 18760192 | tf_op jit(solution)/shard_map/while/body/eval_jaxpr/tkgd,nkd->tkgn/dot_general | solution.py:53
  434.7 8.7 %fusion.67 = f32[128,8,4]{0,2,1:T(4,128)S(1)} fusion(f32[8,1024,128,4]{2,1,3,0:T(8,128)} %get-tuple-element.156, f32[128,8,4]{0,2,1:T(4,128)S(1)} %max.4), kind=kLoop, calls=%fused_computation.4.clone.1 | loop fusion | flops 12578816 | bytes 16809984 | tf_op jit(solution)/shard_map/while/body/eval_jaxpr/reduce_sum | solution.py:63
  443.5 10.5 %fusion.68 = f32[128,8,4,80]{0,3,2,1:T(8,128)} fusion(f32[8,1024,128,4]{2,1,3,0:T(8,128)} %get-tuple-element.156, f32[128,8,4]{0,2,1:T(4,128)S(1)} %max.4, bf16[8,1024,8,80]{1,3,2,0:T(8,128)(2,1)} %get-tuple-element.181, s32[]{:T(128)} %get-tuple-element.167, f32[128,8,4,80]{0,3,2,1:T(8,128)} %get-tuple-element.170, f32[128,8,4]{0,2,1:T(4,128)S(1)} %bitcast.157), kind=kOutput, calls=%fused_computation.9.clone.1 | convolution fusion | flops 684326912 | bytes 20742656 | tf_op jit(solution)/shard_map/while/body/eval_jaxpr/tkgn,nkd->tkgd/dot_general | solution.py:64
  453.9 9.5 %bitcast_reduce_fusion.2 = (f32[128,8,4]{0,2,1:T(4,128)S(1)}, f32[8,1024,128,4]{2,1,3,0:T(8,128)}) fusion(bf16[128,8,4,80]{0,3,2,1:T(8,128)(2,1)S(1)} %get-tuple-element.180, bf16[8,1024,8,80]{1,3,2,0:T(8,128)(2,1)} %get-tuple-element.179, s32[]{:T(128)} %get-tuple-element.167), kind=kOutput, calls=%fused_computation.1.clone.1 | convolution fusion | flops 679473152 | bytes 18760192 | tf_op jit(solution)/shard_map/while/body/eval_jaxpr/tkgd,nkd->tkgn/dot_general | solution.py:53
  463.5 8.7 %fusion.67 = f32[128,8,4]{0,2,1:T(4,128)S(1)} fusion(f32[8,1024,128,4]{2,1,3,0:T(8,128)} %get-tuple-element.156, f32[128,8,4]{0,2,1:T(4,128)S(1)} %max.4), kind=kLoop, calls=%fused_computation.4.clone.1 | loop fusion | flops 12578816 | bytes 16809984 | tf_op jit(solution)/shard_map/while/body/eval_jaxpr/reduce_sum | solution.py:63
  472.2 10.5 %fusion.68 = f32[128,8,4,80]{0,3,2,1:T(8,128)} fusion(f32[8,1024,128,4]{2,1,3,0:T(8,128)} %get-tuple-element.156, f32[128,8,4]{0,2,1:T(4,128)S(1)} %max.4, bf16[8,1024,8,80]{1,3,2,0:T(8,128)(2,1)} %get-tuple-element.181, s32[]{:T(128)} %get-tuple-element.167, f32[128,8,4,80]{0,3,2,1:T(8,128)} %get-tuple-element.170, f32[128,8,4]{0,2,1:T(4,128)S(1)} %bitcast.157), kind=kOutput, calls=%fused_computation.9.clone.1 | convolution fusion | flops 684326912 | bytes 20742656 | tf_op jit(solution)/shard_map/while/body/eval_jaxpr/tkgn,nkd->tkgd/dot_general | solution.py:64
  482.8 1.4 divide_convert_fusion
  484.3 6.8 multiply_reduce_fusion
  491.1 1.1 copy-done.1
  492.2 1.0 multiply_convert_fusion.1
  493.3 81.3 %all-gather.8.cloned.1.call-done = bf16[2048,2560]{1,0:T(8,128)(2,1)} async-done(((bf16[128,2560]{1,0:T(8,128)(2,1)}), bf16[2048,2560]{1,0:T(8,128)(2,1)}) %all-gather.8.cloned.1.call-update) | async-done | bytes 10485776 | tf_op jit(solution)/shard_map/all_gather | solution.py:179
  574.6 11.4 %fusion.48 = f32[2048,448]{0,1:T(8,128)} fusion(bf16[2048,2560]{1,0:T(8,128)(2,1)} %all-gather.8.cloned.1.call-done, bf16[2560,448]{0,1:T(8,128)(2,1)} %param.21), kind=kOutput, calls=%fused_computation.81 | convolution fusion | flops 4697620480 | bytes 16449536 | tf_op jit(solution)/shard_map/dot_general | solution.py:180
  586.0 16.9 %convolution_convert_fusion = bf16[2048,2560]{1,0:T(8,128)(2,1)} fusion(bf16[448,2560]{1,0:T(8,128)(2,1)S(1)} %copy-done, f32[2048,448]{0,1:T(8,128)} %fusion.48, bf16[2048,2560]{1,0:T(8,128)(2,1)} %all-gather.8.cloned.1.call-done, bf16[2560,448]{0,1:T(8,128)(2,1)} %param.22), kind=kOutput, calls=%fused_computation.26 | convolution fusion | flops 9405988864 | bytes 29229056 | tf_op jit(solution)/shard_map/dot_general | solution.py:184
  602.9 1.1 copy.41
  604.0 89.1 %reduce-scatter.2.cloned.1.call-done = bf16[128,2560]{1,0:T(8,128)(2,1)} async-done(((bf16[2048,2560]{1,0:T(8,128)(2,1)}), bf16[128,2560]{1,0:T(8,128)(2,1)}) %reduce-scatter.2.cloned.1.call-update) | async-done | bytes 655376 | tf_op jit(solution)/shard_map/reduce_scatter | solution.py:183
  693.1 2.4 add_convert_fusion
  (59 shorter events, 1.4 us)
Async XLA Ops:
  7.2 578.9 %copy-start = (bf16[448,2560]{1,0:T(8,128)(2,1)S(1)}, bf16[448,2560]{1,0:T(8,128)(2,1)}, u32[]{:S(2)}) copy-start(bf16[448,2560]{1,0:T(8,128)(2,1)} %param.23) | copy-start | bytes 6881284
  7.2 36.0 %all-gather.4.cloned.1.call-start = ((), (), s32[]{:S(2)}) async-start(), calls=%async_computation.1 | async-start | bytes 2949120 | tf_op jit(solution)/shard_map/all_gather | solution.py:156
  11.4 142.3 %all-gather.6.cloned.1.call-start = ((), (), s32[]{:S(2)}) async-start(), calls=%async_computation.2 | async-start | bytes 23592960 | tf_op jit(solution)/shard_map/all_gather | solution.py:158
  18.9 3.8 copy-start.5
  34.1 540.5 %all-gather.8.cloned.1.call-start = ((), (), s32[]{:S(2)}) async-start(), calls=%async_computation.3 | async-start | bytes 11141120 | tf_op jit(solution)/shard_map/all_gather | solution.py:179
  36.2 0.7 copy-start.2
  43.2 2.0 copy-start.3
  484.3 7.9 %copy-start.4 = (f32[2560]{0:T(1024)S(1)}, f32[2560]{0:T(1024)}, u32[]{:S(2)}) copy-start(f32[2560]{0:T(1024)} %param.20) | copy-start | bytes 30724
  491.1 1.1 copy-start.1
  493.2 199.9 %reduce-scatter.2.cloned.1.call-start = ((), (), s32[]{:S(2)}) async-start(), calls=%async_computation.4 | async-start | bytes 11141120 | tf_op jit(solution)/shard_map/reduce_scatter | solution.py:183
Sparse Core Ops, SparseCore 0:
  11.5 31.6 all-gather.3
  44.8 108.7 all-gather.5
  493.3 81.2 all-gather.7
  603.0 90.0 reduce-scatter.1
where the time goes:
time: 707 us; the launch traced here: 702 us
  waiting for transfers between devices  273 us (39%)
  matrix products  202 us (29%)
  local copies, waits for them, and re-layouts  118 us (17%)
  other arithmetic  93.4 us (13%)
  between operations  14.2 us (2%)
    all_gather x1, waiting for transfers between devices, body(): shard_piece = lax.all_gather(page_block, 'kv', axis=0, tiled=True)  97.1 us
    reduce_scatter x1, waiting for transfers between devices, body(): lax.psum_scatter(jnp.dot(activated, w_down, preferred_element_type=jnp.fl...  89.1 us
    dot_general x9, matrix products, absorb(): jnp.einsum('tkgn,nkd->tkgd', weights.astype(jnp.bfloat16), value_rows, pr...  88.4 us
    all_gather x1, waiting for transfers between devices, body(): shard_piece = lax.all_gather(normed, 'req', axis=0, tiled=True)  81.3 us
    dot_general x9, matrix products, absorb(): jnp.einsum('tkgd,nkd->tkgn', rotated_q, key_rows, preferred_element_type=...  78.9 us
    reduce_sum x9, other arithmetic, absorb(): denom = denom * factor + jnp.sum(weights, axis=-1)  73.9 us
    unnamed x21, local copies, waits for them, and re-layouts  71.6 us
    while x2, local copies, waits for them, and re-layouts, sweep_keys(): lax.scan(scan_step, running, (key_blocks, value_blocks, offsets))  28.1 us
  transfers between devices with their start and end apart: 4, of which 4 were waited for; matrix products, arithmetic and copies ran while one was open for 6% of the time, Pallas kernels for 0%

commit v1 on v0

v1 whole, which is shorter than its diff:
```python
import math

import jax
import jax.numpy as jnp
from jax import lax
from jax.experimental import pallas as pl
from jax.experimental.pallas import tpu as pltpu
from jax.sharding import PartitionSpec as P

QH = 32
KVH = 8
HD = 80
PREFIX = 8192


THETA = 1000000.0
NEG = -1e30


def rotate(values, positions):
    half_dim = values.shape[-1] // 2
    exponent = jnp.arange(half_dim, dtype=jnp.float32) * (2.0 / values.shape[-1])
    inverse = jnp.exp(-exponent * math.log(THETA))
    angles = positions.astype(jnp.float32)[:, None] * inverse[None, :]
    cosine = jnp.cos(angles)[:, None, :]
    sine_part = jnp.sin(angles)[:, None, :]
    first_half = values[..., :half_dim]
    second = values[..., half_dim:]
    return jnp.concatenate(
        [first_half * cosine - second * sine_part, second * cosine + first_half * sine_part],
        axis=-1,
    )


def request_info(request_lens, tok_index):
    request_ends = jnp.cumsum(request_lens)
    passed = tok_index[:, None] >= request_ends[None, :]
    request_of = jnp.sum(passed.astype(jnp.int32), axis=1)
    request_start = jnp.sum(jnp.where(passed, request_lens[None, :], 0), axis=1)
    return (request_of, request_start)


def attn_kernel(q_ref, k_ref, v_ref, qi_ref, qs_ref, o_ref, *, chunks, pre_len, suf_len):
    rows = q_ref.shape[0]
    scale = HD ** (-0.5)
    q = q_ref[...]
    qi = qi_ref[...]
    qs = qs_ref[...]

    def step(j, carry):
        m, l, acc = carry
        kt = k_ref[j]
        vt = v_ref[j]
        s = jnp.dot(q, kt, preferred_element_type=jnp.float32) * scale
        kidx = j * suf_len + lax.broadcasted_iota(jnp.int32, (rows, suf_len), 1)
        mask = (kidx >= qs) & (kidx <= qi)
        s_pre = s[:, :pre_len]
        s_suf = jnp.where(mask, s[:, pre_len:], NEG)
        m_new = jnp.maximum(
            m,
            jnp.maximum(
                jnp.max(s_pre, axis=1, keepdims=True), jnp.max(s_suf, axis=1, keepdims=True)
            ),
        )
        alpha = jnp.exp(m - m_new)
        p_pre = jnp.exp(s_pre - m_new)
        p_suf = jnp.where(mask, jnp.exp(s_suf - m_new), 0.0)
        l_new = alpha * l + (
            jnp.sum(p_pre, axis=1, keepdims=True) + jnp.sum(p_suf, axis=1, keepdims=True)
        )
        p = jnp.concatenate([p_pre, p_suf], axis=1).astype(jnp.bfloat16)
        pv = lax.dot_general(
            p, vt, (((1,), (1,)), ((), ())), preferred_element_type=jnp.float32
        )
        return (m_new, l_new, alpha * acc + pv)

    init = (
        jnp.full((rows, 1), NEG, jnp.float32),
        jnp.zeros((rows, 1), jnp.float32),
        jnp.zeros((rows, HD), jnp.float32),
    )
    m, l, acc = lax.fori_loop(0, chunks, step, init)
    o_ref[...] = (acc / l).astype(o_ref.dtype)


def attention(q_heads, kv_t, qidx, qstart, pre_len, suf_len):
    heads, rows, _ = q_heads.shape
    chunks = kv_t.shape[0]
    width = kv_t.shape[2]
    kernel = lambda *refs: attn_kernel(*refs, chunks=chunks, pre_len=pre_len, suf_len=suf_len)
    return pl.pallas_call(
        kernel,
        grid=(heads,),
        in_specs=[
            pl.BlockSpec((None, rows, HD), lambda h: (h, 0, 0)),
            pl.BlockSpec((chunks, HD, width), lambda h: (0, h, 0)),
            pl.BlockSpec((chunks, HD, width), lambda h: (0, heads + h, 0)),
            pl.BlockSpec((rows, 1), lambda h: (0, 0)),
            pl.BlockSpec((rows, 1), lambda h: (0, 0)),
        ],
        out_specs=pl.BlockSpec((None, rows, HD), lambda h: (h, 0, 0)),
        out_shape=jax.ShapeDtypeStruct((heads, rows, HD), jnp.bfloat16),
        compiler_params=pltpu.CompilerParams(
            dimension_semantics=("arbitrary",), vmem_limit_bytes=48 * 1024 * 1024
        ),
    )(q_heads, kv_t, kv_t, qidx, qstart)


def body(
    residual,
    queries,
    suffix_kv,
    prefix_kv,
    page_table,
    suffix_lens,
    w_out,
    norm_gain,
    w_gate,
    w_up,
    w_down,
):
    tok_rows = queries.shape[0]
    kv_width = KVH * HD
    per_group = QH // KVH
    tok_index = lax.axis_index("kv") * tok_rows + jnp.arange(tok_rows, dtype=jnp.int32)
    request_lens = suffix_lens[0]
    request_of, request_start = request_info(request_lens, tok_index)
    positions = PREFIX + tok_index - request_start
    rotated_q = rotate(queries.astype(jnp.float32).reshape(tok_rows, QH, HD), positions).astype(
        jnp.bfloat16
    )
    q_heads = (
        rotated_q.reshape(tok_rows, KVH, per_group, HD)
        .transpose(1, 2, 0, 3)
        .reshape(KVH, per_group * tok_rows, HD)
    )
    suf_keys = rotate(
        suffix_kv[:, :kv_width].astype(jnp.float32).reshape(tok_rows, KVH, HD), positions
    ).astype(jnp.bfloat16)
    page_count = prefix_kv.shape[0]
    page_size = prefix_kv.shape[1]
    pre_len = page_count * page_size
    page_pos = (
        page_table[:, None] * page_size + jnp.arange(page_size, dtype=jnp.int32)[None, :]
    ).reshape(-1)
    page_keys = rotate(
        prefix_kv[:, :, :kv_width].astype(jnp.float32).reshape(pre_len, KVH, HD),
        page_pos,
    ).astype(jnp.bfloat16)
    keys_all = jnp.concatenate(
        [page_keys.reshape(pre_len, kv_width), suf_keys.reshape(tok_rows, kv_width)], axis=0
    )
    values_all = jnp.concatenate(
        [prefix_kv[:, :, kv_width:].reshape(pre_len, kv_width), suffix_kv[:, kv_width:]], axis=0
    )
    local_t = jnp.concatenate([keys_all, values_all], axis=1).T
    kv_t = lax.all_gather(local_t[None], "kv", axis=0, tiled=True)
    qidx = jnp.tile(tok_index, per_group)[:, None]
    qstart = jnp.tile(request_start, per_group)[:, None]
    out_heads = attention(q_heads, kv_t, qidx, qstart, pre_len, tok_rows)
    attended = (
        out_heads.reshape(KVH, per_group, tok_rows, HD)
        .transpose(2, 0, 1, 3)
        .reshape(tok_rows, QH * HD)
    )
    mixed_sum = residual.astype(jnp.float32) + jnp.dot(
        attended, w_out, preferred_element_type=jnp.float32
    )
    stream_wide = mixed_sum.astype(jnp.bfloat16).astype(jnp.float32)
    normed = (
        stream_wide
        * lax.rsqrt(jnp.mean(stream_wide * stream_wide, axis=1, keepdims=True) + 1e-05)
        * norm_gain
    ).astype(jnp.bfloat16)
    shard_piece = lax.all_gather(normed, "req", axis=0, tiled=True)
    gate_proj = jnp.dot(shard_piece, w_gate, preferred_element_type=jnp.float32)
    up_proj = jnp.dot(shard_piece, w_up, preferred_element_type=jnp.float32)
    activated = (jax.nn.silu(gate_proj) * up_proj).astype(jnp.bfloat16)
    summed = lax.psum_scatter(
        jnp.dot(activated, w_down, preferred_element_type=jnp.float32).astype(jnp.bfloat16),
        "req",
        scatter_dimension=0,
        tiled=True,
    ).astype(jnp.float32)
    layer_out = (stream_wide + summed).astype(jnp.bfloat16)
    return (attended, layer_out)


def solution(mesh):
    in_specs = (
        P(("req", "kv"), None),
        P(("req", "kv"), None),
        P(("req", "kv"), None),
        P("kv", None, None),
        P("kv"),
        P("req", None),
        P(),
        P(),
        P(None, "req"),
        P(None, "req"),
        P("req", None),
    )
    out_specs = (P(("req", "kv"), None), P(("req", "kv"), None))
    return jax.shard_map(body, mesh=mesh, in_specs=in_specs, out_specs=out_specs, check_vma=False)
```

time: 707 us -> 490 us (0.69)
  matrix products: 202 us -> 35 us
  Pallas kernels: 0 us -> 116 us
  local copies, waits for them, and re-layouts: 118 us -> 24.6 us
  other arithmetic: 93.4 us -> 21.5 us
    dot_general x18 -> x0, matrix products: 167 us -> none  [the longest x9 88.4 us: absorb(): jnp.einsum('tkgn,nkd->tkgd', weights.astype(jnp.bfloat16), value_rows, pr...]
    pallas_call x0 -> x1, Pallas kernels: none -> 116 us  [attention(): pl.pallas_call(kernel, grid=(heads,), in_specs=[pl.BlockSpec((None, rows,...]
    reduce_sum x11 -> x1, other arithmetic: 74.7 us -> 0.74 us  [request_info(): request_start = jnp.sum(jnp.where(passed, request_lens[None, :], 0), axis=1)]
    unnamed x21 -> x17, local copies, waits for them, and re-layouts: 71.6 us -> 7.84 us
    while x10 -> x0, local copies, waits for them, and re-layouts: 28.1 us -> none  [the longest x2 28.1 us: sweep_keys(): lax.scan(scan_step, running, (key_blocks, value_blocks, offsets))]
    slice x2 -> x1, local copies, waits for them, and re-layouts: 10.1 us -> 0.16 us  [body(): suffix_kv[:, kv_width:]]
    all_gather x2 -> x1, waiting for transfers between devices: 103 us -> 108 us  [body(): kv_t = lax.all_gather(local_t[None], 'kv', axis=0, tiled=True)]
  transfers between devices with their start and end apart: 4 -> 3, of which waited for: 4 -> 3; matrix products, arithmetic and copies ran while one was open for 6% -> 2% of each run, Pallas kernels for 0% -> 0%
where the time goes in v1:
time: 490 us; the launch traced here: 489 us
  waiting for transfers between devices  278 us (57%)
  Pallas kernels  116 us (24%)
  matrix products  35 us (7%)
  local copies, waits for them, and re-layouts  24.6 us (5%)
  other arithmetic  21.5 us (4%)
  between operations  13.9 us (3%)
    pallas_call x1, Pallas kernels, attention(): pl.pallas_call(kernel, grid=(heads,), in_specs=[pl.BlockSpec((None, rows,...  116 us
    all_gather x1, waiting for transfers between devices, body(): kv_t = lax.all_gather(local_t[None], 'kv', axis=0, tiled=True)  108 us
    reduce_scatter x1, waiting for transfers between devices, body(): lax.psum_scatter(jnp.dot(activated, w_down, preferred_element_type=jnp.fl...  88.8 us
    all_gather x1, waiting for transfers between devices, body(): shard_piece = lax.all_gather(normed, 'req', axis=0, tiled=True)  81 us
    dot_general x1, matrix products, body(): jnp.dot(activated, w_down, preferred_element_type=jnp.float32)  16.8 us
    dot_general x1, matrix products, body(): gate_proj = jnp.dot(shard_piece, w_gate, preferred_element_type=jnp.float32)  11.3 us
  transfers between devices with their start and end apart: 3, of which 3 were waited for; matrix products, arithmetic and copies ran while one was open for 2% of the time, Pallas kernels for 0%

profile of v1, /device:TPU:0, one launch (start us, length us, event | category | flops | bytes accessed | tf_op | source)
XLA Modules:
  0.0 489.0 jit_solution(8543033824855667537)
XLA Ops:
  7.2 0.0 copy-start
  7.2 0.0 all-gather.6.cloned.1.call-start
  7.3 1.0 reduce-window.8
  8.2 0.7 select_reduce_fusion
  9.0 1.0 fusion.4
  10.0 0.2 copy.42
  10.2 0.7 broadcast_multiply_fusion
  10.9 0.1 convert_bitcast_fusion
  10.9 0.2 multiply_cosine_fusion.1
  11.1 0.6 multiply_cosine_fusion
  11.8 3.9 slice_convert_fusion
  15.7 3.4 copy.34
  19.1 3.8 reshape.227
  22.8 2.4 copy.36
  25.3 0.2 copy.37
  25.5 0.1 subtract_convert_fusion.2
  25.5 2.1 subtract_convert_fusion
  27.7 0.0 copy-start.5
  27.7 0.1 pad_maximum_fusion
  27.8 1.2 copy-done.5
  29.0 6.1 %maximum_bitcast_fusion = bf16[1280,1152]{1,0:T(8,128)(2,1)} fusion(bf16[128,640]{0,1:T(8,128)(2,1)S(1)} %copy.37, bf16[1024,640]{0,1:T(8,128)(2,1)S(1)} %copy-done.5, bf16[128,640]{0,1:T(8,128)(2,1)S(1)} %bitcast.46, bf16[1024,640]{0,1:T(8,128)(2,1)S(1)} %bitcast.42), kind=kLoop, calls=%fused_computation.5 | loop fusion | flops 11796480 | bytes 5898240 | tf_op jit(solution)/shard_map/transpose | solution.py:156
  35.1 0.0 all-gather.6.cloned.1.call-update
  35.1 0.0 all-gather.4.cloned.1.call-start
  35.2 1.4 copy.31
  36.6 0.1 convert.29
  36.7 0.2 subtract_convert_fusion.1
  36.9 1.3 copy.32
  38.2 1.3 copy.33
  39.6 0.9 copy.39.refs_4_
  40.5 0.9 copy.38.refs_3_
  41.3 2.1 pad_maximum_fusion.1
  43.4 108.1 %all-gather.6.cloned.1.call-done = bf16[10240,1152]{1,0:T(8,128)(2,1)} async-done(((bf16[1280,1152]{1,0:T(8,128)(2,1)}), bf16[10240,1152]{1,0:T(8,128)(2,1)}) %all-gather.6.cloned.1.call-update) | async-done | bytes 23592976 | tf_op jit(solution)/shard_map/all_gather | solution.py:157
  151.5 0.0 copy-start.2
  151.5 0.9 copy-done.2
  152.5 0.0 copy-start.3
  152.5 0.9 copy-done.3
  153.4 115.8 %shard_map.122 = bf16[8,512,80]{2,1,0:T(8,128)(2,1)S(1)} custom-call(bf16[8,512,80]{2,1,0:T(8,128)(2,1)S(1)} %bitcast.35, bf16[8,1280,1152]{2,1,0:T(8,128)(2,1)} %bitcast.37, bf16[8,1280,1152]{2,1,0:T(8,128)(2,1)} %bitcast.38, s32[512,1]{1,0:T(8,128)S(1)} %copy-done.3, s32[512,1]{1,0:T(8,128)S(1)} %copy-done.2), custom_call_target="tpu_custom_call" | custom-call | tf_op jit(solution)/shard_map/pallas_call | solution.py:91
  269.2 0.0 copy-start.1
  269.2 1.0 copy-done.1
  270.2 1.5 copy.40
  271.7 0.0 copy-start.6
  271.7 6.8 %multiply_reduce_fusion = (f32[128]{0:T(128)S(1)}, f32[128,2560]{1,0:T(8,128)S(1)}) fusion(bf16[128,2560]{0,1:T(8,128)(2,1)S(1)} %bitcast.39, bf16[2560,2560]{1,0:T(8,128)(2,1)} %param.17, bf16[128,2560]{1,0:T(8,128)(2,1)} %param.11), kind=kOutput, calls=%fused_computation.10 | convolution fusion | flops 1679687552 | bytes 15729152 | tf_op jit(solution)/shard_map/dot_general | solution.py:166
  278.5 0.0 copy-start.4
  278.6 1.1 copy-done.4
  279.7 0.0 copy-done.6
  279.7 1.0 multiply_convert_fusion.1
  280.7 0.0 all-gather.4.cloned.1.call-update
  280.7 0.2 reduce-scatter.2.cloned.1.call-start
  281.0 81.0 %all-gather.4.cloned.1.call-done = bf16[2048,2560]{1,0:T(8,128)(2,1)} async-done(((bf16[128,2560]{1,0:T(8,128)(2,1)}), bf16[2048,2560]{1,0:T(8,128)(2,1)}) %all-gather.4.cloned.1.call-update) | async-done | bytes 10485776 | tf_op jit(solution)/shard_map/all_gather | solution.py:175
  361.9 11.3 %fusion.5 = f32[2048,448]{0,1:T(8,128)} fusion(bf16[2048,2560]{1,0:T(8,128)(2,1)} %all-gather.4.cloned.1.call-done, bf16[2560,448]{0,1:T(8,128)(2,1)} %param.19), kind=kOutput, calls=%fused_computation.33 | convolution fusion | flops 4697620480 | bytes 16449536 | tf_op jit(solution)/shard_map/dot_general | solution.py:176
  373.3 0.0 copy-done
  373.3 16.8 %convolution_convert_fusion = bf16[2048,2560]{1,0:T(8,128)(2,1)} fusion(bf16[448,2560]{1,0:T(8,128)(2,1)S(1)} %copy-done, f32[2048,448]{0,1:T(8,128)} %fusion.5, bf16[2048,2560]{1,0:T(8,128)(2,1)} %all-gather.4.cloned.1.call-done, bf16[2560,448]{0,1:T(8,128)(2,1)} %param.20), kind=kOutput, calls=%fused_computation | convolution fusion | flops 9405988864 | bytes 29229056 | tf_op jit(solution)/shard_map/dot_general | solution.py:180
  390.1 0.0 reduce-scatter.2.cloned.1.call-update
  390.1 1.1 copy.41
  391.2 88.8 %reduce-scatter.2.cloned.1.call-done = bf16[128,2560]{1,0:T(8,128)(2,1)} async-done(((bf16[2048,2560]{1,0:T(8,128)(2,1)}), bf16[128,2560]{1,0:T(8,128)(2,1)}) %reduce-scatter.2.cloned.1.call-update) | async-done | bytes 655376 | tf_op jit(solution)/shard_map/reduce_scatter | solution.py:179
  480.0 2.4 add_convert_fusion
  (8 shorter events, 0.1 us)
Async XLA Ops:
  7.2 366.1 %copy-start = (bf16[448,2560]{1,0:T(8,128)(2,1)S(1)}, bf16[448,2560]{1,0:T(8,128)(2,1)}, u32[]{:S(2)}) copy-start(bf16[448,2560]{1,0:T(8,128)(2,1)} %param.21) | copy-start | bytes 6881284
  7.2 144.4 %all-gather.6.cloned.1.call-start = ((), (), s32[]{:S(2)}) async-start(), calls=%async_computation.3 | async-start | bytes 26542080 | tf_op jit(solution)/shard_map/all_gather | solution.py:157
  27.7 1.3 copy-start.5
  35.1 326.8 %all-gather.4.cloned.1.call-start = ((), (), s32[]{:S(2)}) async-start(), calls=%async_computation.1 | async-start | bytes 11141120 | tf_op jit(solution)/shard_map/all_gather | solution.py:175
  151.5 0.9 copy-start.2
  152.5 0.9 copy-start.3
  269.2 1.0 copy-start.1
  271.7 8.0 %copy-start.6 = (f32[2560]{0:T(1024)S(1)}, f32[2560]{0:T(1024)}, u32[]{:S(2)}) copy-start(f32[2560]{0:T(1024)} %param.18) | copy-start | bytes 30724
  278.5 1.1 copy-start.4
  280.7 199.3 %reduce-scatter.2.cloned.1.call-start = ((), (), s32[]{:S(2)}) async-start(), calls=%async_computation.2 | async-start | bytes 11141120 | tf_op jit(solution)/shard_map/reduce_scatter | solution.py:179
Sparse Core Ops, SparseCore 0:
  35.3 116.2 all-gather.5
  280.8 81.0 all-gather.3
  390.3 89.6 reduce-scatter.1

commit v2 on v1

--- a/solution.py
+++ b/solution.py
@@ -51,11 +51,11 @@
         m, l, acc = carry
         kt = k_ref[j]
         vt = v_ref[j]
-        s = jnp.dot(q, kt, preferred_element_type=jnp.float32) * scale
+        s_pre = jnp.dot(q, kt[:, :pre_len], preferred_element_type=jnp.float32) * scale
+        s_suf = jnp.dot(q, kt[:, pre_len:], preferred_element_type=jnp.float32) * scale
         kidx = j * suf_len + lax.broadcasted_iota(jnp.int32, (rows, suf_len), 1)
         mask = (kidx >= qs) & (kidx <= qi)
-        s_pre = s[:, :pre_len]
-        s_suf = jnp.where(mask, s[:, pre_len:], NEG)
+        s_suf = jnp.where(mask, s_suf, NEG)
         m_new = jnp.maximum(
             m,
             jnp.maximum(
@@ -68,9 +68,11 @@
         l_new = alpha * l + (
             jnp.sum(p_pre, axis=1, keepdims=True) + jnp.sum(p_suf, axis=1, keepdims=True)
         )
-        p = jnp.concatenate([p_pre, p_suf], axis=1).astype(jnp.bfloat16)
+        nt = (((1,), (1,)), ((), ()))
         pv = lax.dot_general(
-            p, vt, (((1,), (1,)), ((), ())), preferred_element_type=jnp.float32
+            p_pre.astype(jnp.bfloat16), vt[:, :pre_len], nt, preferred_element_type=jnp.float32
+        ) + lax.dot_general(
+            p_suf.astype(jnp.bfloat16), vt[:, pre_len:], nt, preferred_element_type=jnp.float32
         )
         return (m_new, l_new, alpha * acc + pv)
 
@@ -153,11 +155,23 @@
     values_all = jnp.concatenate(
         [prefix_kv[:, :, kv_width:].reshape(pre_len, kv_width), suffix_kv[:, kv_width:]], axis=0
     )
-    local_t = jnp.concatenate([keys_all, values_all], axis=1).T
-    kv_t = lax.all_gather(local_t[None], "kv", axis=0, tiled=True)
+    n_chunks = 4
+    chunk_heads = KVH // n_chunks
+    chunk_rows = chunk_heads * HD
+    keys_t = keys_all.T.reshape(n_chunks, chunk_rows, pre_len + tok_rows)
+    values_t = values_all.T.reshape(n_chunks, chunk_rows, pre_len + tok_rows)
+    local_t = jnp.concatenate([keys_t, values_t], axis=1)
     qidx = jnp.tile(tok_index, per_group)[:, None]
     qstart = jnp.tile(request_start, per_group)[:, None]
-    out_heads = attention(q_heads, kv_t, qidx, qstart, pre_len, tok_rows)
+    outs = []
+    for c in range(n_chunks):
+        kv_t = lax.all_gather(local_t[c][None], "kv", axis=0, tiled=True)
+        outs.append(
+            attention(
+                q_heads[c * chunk_heads:(c + 1) * chunk_heads], kv_t, qidx, qstart, pre_len, tok_rows
+            )
+        )
+    out_heads = jnp.concatenate(outs, axis=0)
     attended = (
         out_heads.reshape(KVH, per_group, tok_rows, HD)
         .transpose(2, 0, 1, 3)

time: 490 us -> 441 us (0.900)
  waiting for transfers between devices: 278 us -> 247 us
  Pallas kernels: 116 us -> 99.5 us
    all_gather x1 -> x4, waiting for transfers between devices: 108 us -> 76 us  [body(): kv_t = lax.all_gather(local_t[c][None], 'kv', axis=0, tiled=True)]
    pallas_call x1 -> x4, Pallas kernels: 116 us -> 99.5 us  [attention(): pl.pallas_call(kernel, grid=(heads,), in_specs=[pl.BlockSpec((None, rows,...]
  transfers between devices with their start and end apart: 3 -> 6, of which waited for: 3 -> 6; matrix products, arithmetic and copies ran while one was open for 2% -> 2% of each run, Pallas kernels for 0% -> 17%
where the time goes in v2:
time: 441 us; the launch traced here: 440 us
  waiting for transfers between devices  247 us (56%)
  Pallas kernels  99.5 us (23%)
  matrix products  35.1 us (8%)
  local copies, waits for them, and re-layouts  25.4 us (6%)
  other arithmetic  18.5 us (4%)
  between operations  14.4 us (3%)
    pallas_call x4, Pallas kernels, attention(): pl.pallas_call(kernel, grid=(heads,), in_specs=[pl.BlockSpec((None, rows,...  99.5 us
    reduce_scatter x1, waiting for transfers between devices, body(): lax.psum_scatter(jnp.dot(activated, w_down, preferred_element_type=jnp.fl...  88.7 us
    all_gather x1, waiting for transfers between devices, body(): shard_piece = lax.all_gather(normed, 'req', axis=0, tiled=True)  80 us
    all_gather x4, waiting for transfers between devices, body(): kv_t = lax.all_gather(local_t[c][None], 'kv', axis=0, tiled=True)  76 us
    dot_general x1, matrix products, body(): jnp.dot(activated, w_down, preferred_element_type=jnp.float32)  16.9 us
    dot_general x1, matrix products, body(): gate_proj = jnp.dot(shard_piece, w_gate, preferred_element_type=jnp.float32)  11.4 us
    unnamed x25, local copies, waits for them, and re-layouts  9.13 us
  transfers between devices with their start and end apart: 6, of which 6 were waited for; matrix products, arithmetic and copies ran while one was open for 2% of the time, Pallas kernels for 17%

profile of v2, /device:TPU:0, one launch (start us, length us, event | category | flops | bytes accessed | tf_op | source)
XLA Modules:
  0.0 440.2 jit_solution(3726516134436969041)
XLA Ops:
  7.2 0.0 all-gather.6.cloned.1.call-start
  7.3 0.8 broadcast_multiply_fusion
  8.1 0.8 reduce-window.8
  8.9 0.7 select_reduce_fusion
  9.6 0.1 convert_bitcast_fusion
  9.7 0.2 multiply_cosine_fusion.1
  9.9 0.6 multiply_cosine_fusion
  10.5 1.0 fusion.8
  11.5 0.2 copy.71
  11.7 0.2 copy.60
  11.9 4.0 slice_convert_fusion
  15.9 3.4 copy.57
  19.3 3.7 reshape.236
  23.1 2.4 copy.59
  25.6 2.1 subtract_convert_fusion
  27.7 0.1 pad_maximum_fusion.2
  27.8 0.1 pad_maximum_fusion
  28.0 1.0 copy-done.9
  29.0 0.1 pad_maximum_fusion.1
  29.1 1.6 fusion.4
  30.8 0.0 all-gather.6.cloned.1.call-update
  30.8 0.0 all-gather.8.cloned.1.call-start
  30.8 0.7 all-gather.8.cloned.1.call-update
  31.5 0.0 all-gather.12.cloned.1.call-start
  31.6 0.7 all-gather.12.cloned.1.call-update
  32.3 0.0 all-gather.10.cloned.1.call-start
  32.3 0.5 all-gather.10.cloned.1.call-update
  32.9 0.2 all-gather.14.cloned.1.call-start
  33.1 0.1 copy.61.refs_3_
  33.3 0.1 copy.62.refs_4_
  33.4 1.4 copy.54
  34.8 0.1 convert.29
  34.9 0.2 subtract_convert_fusion.1
  35.1 1.3 copy.56
  36.4 1.4 copy.55
  37.8 2.1 maximum_bitcast_fusion
  40.0 0.9 fusion.7
  40.9 32.0 %all-gather.6.cloned.1.call-done.refs_1_.refs_2_ = bf16[8,320,1152]{2,1,0:T(8,128)(2,1)} async-done(((bf16[1,320,1152]{2,1,0:T(8,128)(2,1)}), bf16[8,320,1152]{2,1,0:T(8,128)(2,1)}) %all-gather.6.cloned.1.call-update) | async-done | bytes 5898256 | tf_op jit(solution)/shard_map/all_gather | solution.py:168
  72.8 0.9 copy-done.7
  73.8 24.9 %shard_map.122 = bf16[2,512,80]{2,1,0:T(8,128)(2,1)S(1)} custom-call(bf16[2,512,80]{2,1,0:T(8,128)(2,1)S(1)} %bitcast.44, bf16[8,320,1152]{2,1,0:T(8,128)(2,1)} %all-gather.6.cloned.1.call-done.refs_1_.refs_2_, bf16[8,320,1152]{2,1,0:T(8,128)(2,1)} %all-gather.6.cloned.1.call-done.refs_1_.refs_2_, s32[512,1]{1,0:T(8,128)S(1)} %copy.61.refs_3_, ...), custom_call_target="tpu_custom_call" | custom-call | tf_op jit(solution)/shard_map/pallas_call | solution.py:93
  98.7 15.2 %all-gather.8.cloned.1.call-done.refs_1_.refs_2_ = bf16[8,320,1152]{2,1,0:T(8,128)(2,1)} async-done(((bf16[1,320,1152]{2,1,0:T(8,128)(2,1)}), bf16[8,320,1152]{2,1,0:T(8,128)(2,1)}) %all-gather.8.cloned.1.call-update) | async-done | bytes 5898256 | tf_op jit(solution)/shard_map/all_gather | solution.py:168
  113.9 0.9 copy-done.4
  114.8 24.9 %shard_map.123 = bf16[2,512,80]{2,1,0:T(8,128)(2,1)S(1)} custom-call(bf16[2,512,80]{2,1,0:T(8,128)(2,1)S(1)} %bitcast.43, bf16[8,320,1152]{2,1,0:T(8,128)(2,1)} %all-gather.8.cloned.1.call-done.refs_1_.refs_2_, bf16[8,320,1152]{2,1,0:T(8,128)(2,1)} %all-gather.8.cloned.1.call-done.refs_1_.refs_2_, s32[512,1]{1,0:T(8,128)S(1)} %copy.61.refs_3_, ...), custom_call_target="tpu_custom_call" | custom-call | tf_op jit(solution)/shard_map/pallas_call | solution.py:93
  139.7 0.7 copy-done.2
  140.4 14.5 %all-gather.12.cloned.1.call-done.refs_1_.refs_2_ = bf16[8,320,1152]{2,1,0:T(8,128)(2,1)} async-done(((bf16[1,320,1152]{2,1,0:T(8,128)(2,1)}), bf16[8,320,1152]{2,1,0:T(8,128)(2,1)}) %all-gather.12.cloned.1.call-update) | async-done | bytes 5898256 | tf_op jit(solution)/shard_map/all_gather | solution.py:168
  154.9 0.9 copy-done.1
  155.9 24.9 %shard_map.125 = bf16[2,512,80]{2,1,0:T(8,128)(2,1)S(1)} custom-call(bf16[2,512,80]{2,1,0:T(8,128)(2,1)S(1)} %bitcast.42, bf16[8,320,1152]{2,1,0:T(8,128)(2,1)} %all-gather.12.cloned.1.call-done.refs_1_.refs_2_, bf16[8,320,1152]{2,1,0:T(8,128)(2,1)} %all-gather.12.cloned.1.call-done.refs_1_.refs_2_, s32[512,1]{1,0:T(8,128)S(1)} %copy.61.refs_3_, ...), custom_call_target="tpu_custom_call" | custom-call | tf_op jit(solution)/shard_map/pallas_call | solution.py:93
  180.7 0.7 copy-done.5
  181.4 14.4 %all-gather.10.cloned.1.call-done.refs_1_.refs_2_ = bf16[8,320,1152]{2,1,0:T(8,128)(2,1)} async-done(((bf16[1,320,1152]{2,1,0:T(8,128)(2,1)}), bf16[8,320,1152]{2,1,0:T(8,128)(2,1)}) %all-gather.10.cloned.1.call-update) | async-done | bytes 5898256 | tf_op jit(solution)/shard_map/all_gather | solution.py:168
  195.8 24.9 %shard_map.124 = bf16[2,512,80]{2,1,0:T(8,128)(2,1)S(1)} custom-call(bf16[2,512,80]{2,1,0:T(8,128)(2,1)S(1)} %bitcast.41, bf16[8,320,1152]{2,1,0:T(8,128)(2,1)} %all-gather.10.cloned.1.call-done.refs_1_.refs_2_, bf16[8,320,1152]{2,1,0:T(8,128)(2,1)} %all-gather.10.cloned.1.call-done.refs_1_.refs_2_, s32[512,1]{1,0:T(8,128)S(1)} %copy.61.refs_3_, ...), custom_call_target="tpu_custom_call" | custom-call | tf_op jit(solution)/shard_map/pallas_call | solution.py:93
  220.8 1.3 pad_maximum_fusion.3
  222.0 1.5 copy.69
  223.5 6.8 %multiply_reduce_fusion = (f32[128]{0:T(128)S(1)}, f32[128,2560]{1,0:T(8,128)S(1)}) fusion(bf16[128,2560]{0,1:T(8,128)(2,1)S(1)} %bitcast.45, bf16[2560,2560]{1,0:T(8,128)(2,1)} %param.17, bf16[128,2560]{1,0:T(8,128)(2,1)} %param.11), kind=kOutput, calls=%fused_computation.17 | convolution fusion | flops 1679687552 | bytes 15729152 | tf_op jit(solution)/shard_map/dot_general | solution.py:180
  230.4 1.2 copy-done.8
  231.5 1.0 multiply_convert_fusion.1
  232.5 0.0 all-gather.14.cloned.1.call-update
  232.6 0.3 reduce-scatter.2.cloned.1.call-start
  232.8 80.0 %all-gather.14.cloned.1.call-done = bf16[2048,2560]{1,0:T(8,128)(2,1)} async-done(((bf16[128,2560]{1,0:T(8,128)(2,1)}), bf16[2048,2560]{1,0:T(8,128)(2,1)}) %all-gather.14.cloned.1.call-update) | async-done | bytes 10485776 | tf_op jit(solution)/shard_map/all_gather | solution.py:189
  312.9 11.4 %fusion.9 = f32[2048,448]{0,1:T(8,128)} fusion(bf16[2048,2560]{1,0:T(8,128)(2,1)} %all-gather.14.cloned.1.call-done, bf16[2560,448]{0,1:T(8,128)(2,1)} %param.19), kind=kOutput, calls=%fused_computation.46 | convolution fusion | flops 4697620480 | bytes 16449536 | tf_op jit(solution)/shard_map/dot_general | solution.py:190
  324.2 16.9 %convolution_convert_fusion = bf16[2048,2560]{1,0:T(8,128)(2,1)} fusion(bf16[448,2560]{1,0:T(8,128)(2,1)S(1)} %copy-done, f32[2048,448]{0,1:T(8,128)} %fusion.9, bf16[2048,2560]{1,0:T(8,128)(2,1)} %all-gather.14.cloned.1.call-done, bf16[2560,448]{0,1:T(8,128)(2,1)} %param.20), kind=kOutput, calls=%fused_computation | convolution fusion | flops 9405988864 | bytes 29229056 | tf_op jit(solution)/shard_map/dot_general | solution.py:194
  341.1 0.0 reduce-scatter.2.cloned.1.call-update
  341.1 1.1 copy.70
  342.2 88.7 %reduce-scatter.2.cloned.1.call-done = bf16[128,2560]{1,0:T(8,128)(2,1)} async-done(((bf16[2048,2560]{1,0:T(8,128)(2,1)}), bf16[128,2560]{1,0:T(8,128)(2,1)}) %reduce-scatter.2.cloned.1.call-update) | async-done | bytes 655376 | tf_op jit(solution)/shard_map/reduce_scatter | solution.py:193
  430.9 2.4 add_convert_fusion
  (24 shorter events, 0.2 us)
Async XLA Ops:
  7.2 317.1 %copy-start = (bf16[448,2560]{1,0:T(8,128)(2,1)S(1)}, bf16[448,2560]{1,0:T(8,128)(2,1)}, u32[]{:S(2)}) copy-start(bf16[448,2560]{1,0:T(8,128)(2,1)} %param.21) | copy-start | bytes 6881284
  7.2 65.7 %all-gather.6.cloned.1.call-start = ((), (), s32[]{:S(2)}) async-start(), calls=%async_computation.1 | async-start | bytes 6635520 | tf_op jit(solution)/shard_map/all_gather | solution.py:168
  27.7 1.3 copy-start.9
  30.8 83.1 %all-gather.8.cloned.1.call-start = ((), (), s32[]{:S(2)}) async-start(), calls=%async_computation.2 | async-start | bytes 6635520 | tf_op jit(solution)/shard_map/all_gather | solution.py:168
  31.5 123.4 %all-gather.12.cloned.1.call-start = ((), (), s32[]{:S(2)}) async-start(), calls=%async_computation.4 | async-start | bytes 6635520 | tf_op jit(solution)/shard_map/all_gather | solution.py:168
  32.3 163.5 %all-gather.10.cloned.1.call-start = ((), (), s32[]{:S(2)}) async-start(), calls=%async_computation.3 | async-start | bytes 6635520 | tf_op jit(solution)/shard_map/all_gather | solution.py:168
  32.9 280.0 %all-gather.14.cloned.1.call-start = ((), (), s32[]{:S(2)}) async-start(), calls=%async_computation.5 | async-start | bytes 11141120 | tf_op jit(solution)/shard_map/all_gather | solution.py:189
  72.8 0.9 copy-start.7
  113.9 0.9 copy-start.4
  139.7 0.7 copy-start.2
  154.9 0.9 copy-start.1
  180.7 0.7 copy-start.5
  195.8 24.9 %copy-start.3 = (bf16[2,512,80]{2,1,0:T(8,128)(2,1)S(1)}, bf16[2,512,80]{2,1,0:T(8,128)(2,1)}, u32[]{:S(2)}) copy-start(bf16[2,512,80]{2,1,0:T(8,128)(2,1)} %copy-done.2) | copy-start | bytes 491524
  195.8 25.0 %copy-start.6 = (bf16[2,512,80]{2,1,0:T(8,128)(2,1)S(1)}, bf16[2,512,80]{2,1,0:T(8,128)(2,1)}, u32[]{:S(2)}) copy-start(bf16[2,512,80]{2,1,0:T(8,128)(2,1)} %copy-done.5) | copy-start | bytes 491524
  223.5 8.0 %copy-start.10 = (f32[2560]{0:T(1024)S(1)}, f32[2560]{0:T(1024)}, u32[]{:S(2)}) copy-start(f32[2560]{0:T(1024)} %param.18) | copy-start | bytes 30724
  230.4 1.2 copy-start.8
  232.6 198.3 %reduce-scatter.2.cloned.1.call-start = ((), (), s32[]{:S(2)}) async-start(), calls=%async_computation.6 | async-start | bytes 11141120 | tf_op jit(solution)/shard_map/reduce_scatter | solution.py:193
Sparse Core Ops, SparseCore 0:
  30.9 41.8 all-gather.5
  74.5 39.2 all-gather.7
  115.6 39.2 all-gather.11
  156.5 39.2 all-gather.9
  232.7 80.1 all-gather.13
  341.3 89.5 reduce-scatter.1

commit v3 on v2

--- a/solution.py
+++ b/solution.py
@@ -136,50 +136,61 @@
         .transpose(1, 2, 0, 3)
         .reshape(KVH, per_group * tok_rows, HD)
     )
-    suf_keys = rotate(
-        suffix_kv[:, :kv_width].astype(jnp.float32).reshape(tok_rows, KVH, HD), positions
-    ).astype(jnp.bfloat16)
     page_count = prefix_kv.shape[0]
     page_size = prefix_kv.shape[1]
     pre_len = page_count * page_size
+    key_count = pre_len + tok_rows
     page_pos = (
         page_table[:, None] * page_size + jnp.arange(page_size, dtype=jnp.int32)[None, :]
     ).reshape(-1)
-    page_keys = rotate(
-        prefix_kv[:, :, :kv_width].astype(jnp.float32).reshape(pre_len, KVH, HD),
-        page_pos,
+    key_pos = jnp.concatenate([page_pos, positions]).astype(jnp.float32)
+    raw_t = jnp.concatenate(
+        [prefix_kv.reshape(pre_len, 2 * kv_width), suffix_kv], axis=0
+    ).T
+    half_dim = HD // 2
+    exponent = jnp.arange(half_dim, dtype=jnp.float32) * (2.0 / HD)
+    inverse = jnp.exp(-exponent * math.log(THETA))
+    angles = inverse[:, None] * key_pos[None, :]
+    cosine = jnp.cos(angles)[None]
+    sine_part = jnp.sin(angles)[None]
+    halves = raw_t[:kv_width].astype(jnp.float32).reshape(KVH, 2, half_dim, key_count)
+    first_half = halves[:, 0]
+    second = halves[:, 1]
+    keys_t = jnp.stack(
+        [first_half * cosine - second * sine_part, second * cosine + first_half * sine_part],
+        axis=1,
     ).astype(jnp.bfloat16)
-    keys_all = jnp.concatenate(
-        [page_keys.reshape(pre_len, kv_width), suf_keys.reshape(tok_rows, kv_width)], axis=0
-    )
-    values_all = jnp.concatenate(
-        [prefix_kv[:, :, kv_width:].reshape(pre_len, kv_width), suffix_kv[:, kv_width:]], axis=0
-    )
+    values_t = raw_t[kv_width:]
     n_chunks = 4
     chunk_heads = KVH // n_chunks
     chunk_rows = chunk_heads * HD
-    keys_t = keys_all.T.reshape(n_chunks, chunk_rows, pre_len + tok_rows)
-    values_t = values_all.T.reshape(n_chunks, chunk_rows, pre_len + tok_rows)
-    local_t = jnp.concatenate([keys_t, values_t], axis=1)
+    local_t = jnp.concatenate(
+        [
+            keys_t.reshape(n_chunks, chunk_rows, key_count),
+            values_t.reshape(n_chunks, chunk_rows, key_count),
+        ],
+        axis=1,
+    )
     qidx = jnp.tile(tok_index, per_group)[:, None]
     qstart = jnp.tile(request_start, per_group)[:, None]
-    outs = []
+    pieces = []
+    mixed_sum = residual.astype(jnp.float32)
     for c in range(n_chunks):
         kv_t = lax.all_gather(local_t[c][None], "kv", axis=0, tiled=True)
-        outs.append(
-            attention(
-                q_heads[c * chunk_heads:(c + 1) * chunk_heads], kv_t, qidx, qstart, pre_len, tok_rows
-            )
-        )
-    out_heads = jnp.concatenate(outs, axis=0)
-    attended = (
-        out_heads.reshape(KVH, per_group, tok_rows, HD)
-        .transpose(2, 0, 1, 3)
-        .reshape(tok_rows, QH * HD)
-    )
-    mixed_sum = residual.astype(jnp.float32) + jnp.dot(
-        attended, w_out, preferred_element_type=jnp.float32
-    )
+        out_c = attention(
+            q_heads[c * chunk_heads:(c + 1) * chunk_heads], kv_t, qidx, qstart, pre_len, tok_rows
+        )
+        piece = (
+            out_c.reshape(chunk_heads, per_group, tok_rows, HD)
+            .transpose(2, 0, 1, 3)
+            .reshape(tok_rows, chunk_heads * per_group * HD)
+        )
+        width = piece.shape[1]
+        mixed_sum = mixed_sum + jnp.dot(
+            piece, w_out[c * width:(c + 1) * width], preferred_element_type=jnp.float32
+        )
+        pieces.append(piece)
+    attended = jnp.concatenate(pieces, axis=1)
     stream_wide = mixed_sum.astype(jnp.bfloat16).astype(jnp.float32)
     normed = (
         stream_wide

time: 441 us -> 432 us (0.980)
  local copies, waits for them, and re-layouts: 25.4 us -> 19.2 us
    reshape x4 -> x5, local copies, waits for them, and re-layouts: 11.1 us -> 6.38 us  [the longest x1 4.51 us: body(): prefix_kv.reshape(pre_len, 2 * kv_width)]
    dot_general x1 -> x4, matrix products: 6.81 us -> 10.9 us  [body(): jnp.dot(piece, w_out[c * width:(c + 1) * width], preferred_element_type=j...]
    unnamed x25 -> x21, local copies, waits for them, and re-layouts: 9.13 us -> 8.6 us
  transfers between devices with their start and end apart: 6 -> 6, of which waited for: 6 -> 6; matrix products, arithmetic and copies ran while one was open for 2% -> 3% of each run, Pallas kernels for 17% -> 17%
where the time goes in v3:
time: 432 us
  waiting for transfers between devices  244 us (56%)
  Pallas kernels  99.5 us (23%)
  matrix products  39.1 us (9%)
  local copies, waits for them, and re-layouts  19.2 us (4%)
  other arithmetic  14.6 us (3%)
  between operations  14.4 us (3%)
    pallas_call x4, Pallas kernels, attention(): pl.pallas_call(kernel, grid=(heads,), in_specs=[pl.BlockSpec((None, rows,...  99.5 us
    reduce_scatter x1, waiting for transfers between devices, body(): lax.psum_scatter(jnp.dot(activated, w_down, preferred_element_type=jnp.fl...  86.7 us
    all_gather x1, waiting for transfers between devices, body(): shard_piece = lax.all_gather(normed, 'req', axis=0, tiled=True)  80 us
    all_gather x4, waiting for transfers between devices, body(): kv_t = lax.all_gather(local_t[c][None], 'kv', axis=0, tiled=True)  75.5 us
    dot_general x1, matrix products, body(): jnp.dot(activated, w_down, preferred_element_type=jnp.float32)  16.9 us
    dot_general x1, matrix products, body(): gate_proj = jnp.dot(shard_piece, w_gate, preferred_element_type=jnp.float32)  11.3 us
    dot_general x4, matrix products, body(): jnp.dot(piece, w_out[c * width:(c + 1) * width], preferred_element_type=j...  10.9 us
  transfers between devices with their start and end apart: 6, of which 6 were waited for; matrix products, arithmetic and copies ran while one was open for 3% of the time, Pallas kernels for 17%

profile of v3, /device:TPU:0, one launch (start us, length us, event | category | flops | bytes accessed | tf_op | source)
XLA Modules:
  0.0 431.6 jit_solution(3202110469307806519)
XLA Ops:
  7.2 0.0 all-gather.6.cloned.1.call-start
  7.3 0.8 broadcast_multiply_fusion
  8.1 0.8 reduce-window.8
  8.9 0.7 select_reduce_fusion
  9.6 0.1 add_bitcast_fusion
  9.7 1.2 copy.61
  10.9 4.5 %copy.60 = bf16[1024,1280]{0,1:T(8,128)(2,1)} copy(bf16[1024,1280]{1,0:T(8,128)(2,1)} %bitcast.60) | data formatting | bytes 5242880 | tf_op jit(solution)/shard_map/reshape | solution.py:148
  15.4 2.0 maximum_bitcast_fusion
  17.4 0.2 fusion.12
  17.7 0.2 convert.21
  17.9 0.7 multiply_cosine_fusion
  18.6 0.4 subtract_convert_fusion
  19.0 0.1 pad_maximum_fusion
  19.2 1.6 fusion.8
  20.8 0.0 all-gather.6.cloned.1.call-update
  20.9 0.0 all-gather.8.cloned.1.call-start
  20.9 0.7 all-gather.8.cloned.1.call-update
  21.6 0.0 all-gather.12.cloned.1.call-start
  21.7 0.7 all-gather.12.cloned.1.call-update
  22.4 0.0 all-gather.10.cloned.1.call-start
  22.4 0.5 all-gather.10.cloned.1.call-update
  22.9 0.2 all-gather.14.cloned.1.call-start
  23.2 0.1 copy.62.refs_3_
  23.3 0.1 copy.63.refs_4_
  23.5 1.4 copy.57
  24.9 0.1 convert.20
  25.0 0.2 multiply_cosine_fusion.1
  25.2 0.2 subtract_convert_fusion.1
  25.3 1.3 copy.59
  26.7 1.4 copy.58
  28.1 2.1 maximum_bitcast_fusion.1
  30.2 0.9 fusion.13
  31.1 31.8 %all-gather.6.cloned.1.call-done.refs_1_.refs_2_ = bf16[8,320,1152]{2,1,0:T(8,128)(2,1)} async-done(((bf16[1,320,1152]{2,1,0:T(8,128)(2,1)}), bf16[8,320,1152]{2,1,0:T(8,128)(2,1)}) %all-gather.6.cloned.1.call-update) | async-done | bytes 5898256 | tf_op jit(solution)/shard_map/all_gather | solution.py:179
  62.9 0.9 copy-done.3
  63.9 24.9 %shard_map.122 = bf16[2,512,80]{2,1,0:T(8,128)(2,1)S(1)} custom-call(bf16[2,512,80]{2,1,0:T(8,128)(2,1)S(1)} %bitcast.56, bf16[8,320,1152]{2,1,0:T(8,128)(2,1)} %all-gather.6.cloned.1.call-done.refs_1_.refs_2_, bf16[8,320,1152]{2,1,0:T(8,128)(2,1)} %all-gather.6.cloned.1.call-done.refs_1_.refs_2_, s32[512,1]{1,0:T(8,128)S(1)} %copy.62.refs_3_, ...), custom_call_target="tpu_custom_call" | custom-call | tf_op jit(solution)/shard_map/pallas_call | solution.py:93
  88.8 0.8 copy.64
  89.6 14.4 %all-gather.8.cloned.1.call-done.refs_1_.refs_2_ = bf16[8,320,1152]{2,1,0:T(8,128)(2,1)} async-done(((bf16[1,320,1152]{2,1,0:T(8,128)(2,1)}), bf16[8,320,1152]{2,1,0:T(8,128)(2,1)}) %all-gather.8.cloned.1.call-update) | async-done | bytes 5898256 | tf_op jit(solution)/shard_map/all_gather | solution.py:179
  104.0 0.9 copy-done.2
  104.9 24.9 %shard_map.123 = bf16[2,512,80]{2,1,0:T(8,128)(2,1)S(1)} custom-call(bf16[2,512,80]{2,1,0:T(8,128)(2,1)S(1)} %bitcast.55, bf16[8,320,1152]{2,1,0:T(8,128)(2,1)} %all-gather.8.cloned.1.call-done.refs_1_.refs_2_, bf16[8,320,1152]{2,1,0:T(8,128)(2,1)} %all-gather.8.cloned.1.call-done.refs_1_.refs_2_, s32[512,1]{1,0:T(8,128)S(1)} %copy.62.refs_3_, ...), custom_call_target="tpu_custom_call" | custom-call | tf_op jit(solution)/shard_map/pallas_call | solution.py:93
  129.8 0.1 copy.67
  129.9 15.1 %all-gather.12.cloned.1.call-done.refs_1_.refs_2_ = bf16[8,320,1152]{2,1,0:T(8,128)(2,1)} async-done(((bf16[1,320,1152]{2,1,0:T(8,128)(2,1)}), bf16[8,320,1152]{2,1,0:T(8,128)(2,1)}) %all-gather.12.cloned.1.call-update) | async-done | bytes 5898256 | tf_op jit(solution)/shard_map/all_gather | solution.py:179
  145.0 0.9 copy-done.1
  145.9 24.9 %shard_map.125 = bf16[2,512,80]{2,1,0:T(8,128)(2,1)S(1)} custom-call(bf16[2,512,80]{2,1,0:T(8,128)(2,1)S(1)} %bitcast.54, bf16[8,320,1152]{2,1,0:T(8,128)(2,1)} %all-gather.12.cloned.1.call-done.refs_1_.refs_2_, bf16[8,320,1152]{2,1,0:T(8,128)(2,1)} %all-gather.12.cloned.1.call-done.refs_1_.refs_2_, s32[512,1]{1,0:T(8,128)S(1)} %copy.62.refs_3_, ...), custom_call_target="tpu_custom_call" | custom-call | tf_op jit(solution)/shard_map/pallas_call | solution.py:93
  170.8 0.8 copy.73
  171.6 14.2 %all-gather.10.cloned.1.call-done.refs_1_.refs_2_ = bf16[8,320,1152]{2,1,0:T(8,128)(2,1)} async-done(((bf16[1,320,1152]{2,1,0:T(8,128)(2,1)}), bf16[8,320,1152]{2,1,0:T(8,128)(2,1)}) %all-gather.10.cloned.1.call-update) | async-done | bytes 5898256 | tf_op jit(solution)/shard_map/all_gather | solution.py:179
  185.9 24.9 %shard_map.124 = bf16[2,512,80]{2,1,0:T(8,128)(2,1)S(1)} custom-call(bf16[2,512,80]{2,1,0:T(8,128)(2,1)S(1)} %bitcast.53, bf16[8,320,1152]{2,1,0:T(8,128)(2,1)} %all-gather.10.cloned.1.call-done.refs_1_.refs_2_, bf16[8,320,1152]{2,1,0:T(8,128)(2,1)} %all-gather.10.cloned.1.call-done.refs_1_.refs_2_, s32[512,1]{1,0:T(8,128)S(1)} %copy.62.refs_3_, ...), custom_call_target="tpu_custom_call" | custom-call | tf_op jit(solution)/shard_map/pallas_call | solution.py:93
  210.8 0.1 copy.70
  210.9 2.9 convolution_add_fusion.3
  213.8 2.6 convolution_add_fusion.2
  216.5 2.7 convolution_add_fusion.1
  219.2 2.7 multiply_reduce_fusion
  221.9 1.1 copy-done.4
  223.1 1.0 multiply_convert_fusion.1
  224.1 0.0 all-gather.14.cloned.1.call-update
  224.1 0.3 reduce-scatter.2.cloned.1.call-start
  224.4 80.0 %all-gather.14.cloned.1.call-done = bf16[2048,2560]{1,0:T(8,128)(2,1)} async-done(((bf16[128,2560]{1,0:T(8,128)(2,1)}), bf16[2048,2560]{1,0:T(8,128)(2,1)}) %all-gather.14.cloned.1.call-update) | async-done | bytes 10485776 | tf_op jit(solution)/shard_map/all_gather | solution.py:200
  304.4 11.3 %fusion.14 = f32[2048,448]{0,1:T(8,128)} fusion(bf16[2048,2560]{1,0:T(8,128)(2,1)} %all-gather.14.cloned.1.call-done, bf16[2560,448]{0,1:T(8,128)(2,1)} %param.19), kind=kOutput, calls=%fused_computation.50 | convolution fusion | flops 4697620480 | bytes 16449536 | tf_op jit(solution)/shard_map/dot_general | solution.py:201
  315.8 16.9 %convolution_convert_fusion = bf16[2048,2560]{1,0:T(8,128)(2,1)} fusion(bf16[448,2560]{1,0:T(8,128)(2,1)S(1)} %copy-done, f32[2048,448]{0,1:T(8,128)} %fusion.14, bf16[2048,2560]{1,0:T(8,128)(2,1)} %all-gather.14.cloned.1.call-done, bf16[2560,448]{0,1:T(8,128)(2,1)} %param.20), kind=kOutput, calls=%fused_computation | convolution fusion | flops 9405988864 | bytes 29229056 | tf_op jit(solution)/shard_map/dot_general | solution.py:205
  332.6 0.0 reduce-scatter.2.cloned.1.call-update
  332.7 0.9 copy-done.7
  333.5 1.0 pad_maximum_fusion.2
  334.5 1.1 copy.74
  335.6 86.7 %reduce-scatter.2.cloned.1.call-done = bf16[128,2560]{1,0:T(8,128)(2,1)} async-done(((bf16[2048,2560]{1,0:T(8,128)(2,1)}), bf16[128,2560]{1,0:T(8,128)(2,1)}) %reduce-scatter.2.cloned.1.call-update) | async-done | bytes 655376 | tf_op jit(solution)/shard_map/reduce_scatter | solution.py:204
  422.3 2.4 add_convert_fusion.1
  (20 shorter events, 0.1 us)
Async XLA Ops:
  7.2 308.6 %copy-start = (bf16[448,2560]{1,0:T(8,128)(2,1)S(1)}, bf16[448,2560]{1,0:T(8,128)(2,1)}, u32[]{:S(2)}) copy-start(bf16[448,2560]{1,0:T(8,128)(2,1)} %param.21) | copy-start | bytes 6881284
  7.2 55.8 %all-gather.6.cloned.1.call-start = ((), (), s32[]{:S(2)}) async-start(), calls=%async_computation.1 | async-start | bytes 6635520 | tf_op jit(solution)/shard_map/all_gather | solution.py:179
  20.9 83.1 %all-gather.8.cloned.1.call-start = ((), (), s32[]{:S(2)}) async-start(), calls=%async_computation.2 | async-start | bytes 6635520 | tf_op jit(solution)/shard_map/all_gather | solution.py:179
  21.6 123.4 %all-gather.12.cloned.1.call-start = ((), (), s32[]{:S(2)}) async-start(), calls=%async_computation.4 | async-start | bytes 6635520 | tf_op jit(solution)/shard_map/all_gather | solution.py:179
  22.4 163.5 %all-gather.10.cloned.1.call-start = ((), (), s32[]{:S(2)}) async-start(), calls=%async_computation.3 | async-start | bytes 6635520 | tf_op jit(solution)/shard_map/all_gather | solution.py:179
  22.9 281.5 %all-gather.14.cloned.1.call-start = ((), (), s32[]{:S(2)}) async-start(), calls=%async_computation.5 | async-start | bytes 11141120 | tf_op jit(solution)/shard_map/all_gather | solution.py:200
  62.9 0.9 copy-start.3
  104.0 0.9 copy-start.2
  145.0 0.9 copy-start.1
  210.9 5.5 %copy-start.6 = (bf16[2,4,128,80]{2,3,1,0:T(8,128)(2,1)}, bf16[2,4,128,80]{2,3,1,0:T(8,128)(2,1)S(1)}, u32[]{:S(2)}) copy-start(bf16[2,4,128,80]{2,3,1,0:T(8,128)(2,1)S(1)} %copy.70) | copy-start | bytes 491524
  216.5 2.7 copy-start.5
  219.2 3.9 copy-start.8
  221.9 1.2 copy-start.4
  224.1 198.2 %reduce-scatter.2.cloned.1.call-start = ((), (), s32[]{:S(2)}) async-start(), calls=%async_computation.6 | async-start | bytes 11141120 | tf_op jit(solution)/shard_map/reduce_scatter | solution.py:204
  332.6 0.9 copy-start.7
Sparse Core Ops, SparseCore 0:
  21.0 41.8 all-gather.5
  64.6 39.2 all-gather.7
  105.7 39.2 all-gather.11
  146.5 39.2 all-gather.9
  224.2 80.1 all-gather.13
  332.8 89.4 reduce-scatter.1

commit v4 on v1

--- a/solution.py
+++ b/solution.py
@@ -40,70 +40,76 @@
     return (request_of, request_start)
 
 
-def attn_kernel(q_ref, k_ref, v_ref, qi_ref, qs_ref, o_ref, *, chunks, pre_len, suf_len):
+def attn_kernel(q_ref, k_ref, v_ref, qi_ref, qs_ref, m_in, l_in, acc_in, m_ref, l_ref, acc_ref, *, pre_len):
     rows = q_ref.shape[0]
+    suf_len = k_ref.shape[1] - pre_len
     scale = HD ** (-0.5)
     q = q_ref[...]
-    qi = qi_ref[...]
-    qs = qs_ref[...]
-
-    def step(j, carry):
-        m, l, acc = carry
-        kt = k_ref[j]
-        vt = v_ref[j]
-        s = jnp.dot(q, kt, preferred_element_type=jnp.float32) * scale
-        kidx = j * suf_len + lax.broadcasted_iota(jnp.int32, (rows, suf_len), 1)
-        mask = (kidx >= qs) & (kidx <= qi)
-        s_pre = s[:, :pre_len]
-        s_suf = jnp.where(mask, s[:, pre_len:], NEG)
-        m_new = jnp.maximum(
-            m,
-            jnp.maximum(
-                jnp.max(s_pre, axis=1, keepdims=True), jnp.max(s_suf, axis=1, keepdims=True)
-            ),
-        )
-        alpha = jnp.exp(m - m_new)
-        p_pre = jnp.exp(s_pre - m_new)
-        p_suf = jnp.where(mask, jnp.exp(s_suf - m_new), 0.0)
-        l_new = alpha * l + (
-            jnp.sum(p_pre, axis=1, keepdims=True) + jnp.sum(p_suf, axis=1, keepdims=True)
-        )
-        p = jnp.concatenate([p_pre, p_suf], axis=1).astype(jnp.bfloat16)
-        pv = lax.dot_general(
-            p, vt, (((1,), (1,)), ((), ())), preferred_element_type=jnp.float32
-        )
-        return (m_new, l_new, alpha * acc + pv)
-
-    init = (
-        jnp.full((rows, 1), NEG, jnp.float32),
-        jnp.zeros((rows, 1), jnp.float32),
-        jnp.zeros((rows, HD), jnp.float32),
-    )
-    m, l, acc = lax.fori_loop(0, chunks, step, init)
-    o_ref[...] = (acc / l).astype(o_ref.dtype)
-
-
-def attention(q_heads, kv_t, qidx, qstart, pre_len, suf_len):
+    kt = k_ref[...]
+    vt = v_ref[...]
+    m = m_in[...]
+    l = l_in[...]
+    s_pre = jnp.dot(q, kt[:, :pre_len], preferred_element_type=jnp.float32) * scale
+    s_suf = jnp.dot(q, kt[:, pre_len:], preferred_element_type=jnp.float32) * scale
+    kidx = lax.broadcasted_iota(jnp.int32, (rows, suf_len), 1)
+    mask = (kidx >= qs_ref[...]) & (kidx <= qi_ref[...])
+    s_suf = jnp.where(mask, s_suf, NEG)
+    m_new = jnp.maximum(
+        m,
+        jnp.maximum(jnp.max(s_pre, axis=1, keepdims=True), jnp.max(s_suf, axis=1, keepdims=True)),
+    )
+    alpha = jnp.exp(m - m_new)
+    p_pre = jnp.exp(s_pre - m_new)
+    p_suf = jnp.where(mask, jnp.exp(s_suf - m_new), 0.0)
+    l_ref[...] = alpha * l + (
+        jnp.sum(p_pre, axis=1, keepdims=True) + jnp.sum(p_suf, axis=1, keepdims=True)
+    )
+    nt = (((1,), (1,)), ((), ()))
+    pv = lax.dot_general(
+        p_pre.astype(jnp.bfloat16), vt[:, :pre_len], nt, preferred_element_type=jnp.float32
+    ) + lax.dot_general(
+        p_suf.astype(jnp.bfloat16), vt[:, pre_len:], nt, preferred_element_type=jnp.float32
+    )
+    acc_ref[...] = alpha * acc_in[...] + pv
+    m_ref[...] = m_new
+
+
+def attention_block(q_heads, kv_blk, qi_rel, qs_rel, state, pre_len):
     heads, rows, _ = q_heads.shape
-    chunks = kv_t.shape[0]
-    width = kv_t.shape[2]
-    kernel = lambda *refs: attn_kernel(*refs, chunks=chunks, pre_len=pre_len, suf_len=suf_len)
+    width = kv_blk.shape[1]
+    m, l, acc = state
+    kernel = lambda *refs: attn_kernel(*refs, pre_len=pre_len)
+    stat_spec = pl.BlockSpec((None, rows, 1), lambda h: (h, 0, 0))
+    acc_spec = pl.BlockSpec((None, rows, HD), lambda h: (h, 0, 0))
     return pl.pallas_call(
         kernel,
         grid=(heads,),
         in_specs=[
             pl.BlockSpec((None, rows, HD), lambda h: (h, 0, 0)),
-            pl.BlockSpec((chunks, HD, width), lambda h: (0, h, 0)),
-            pl.BlockSpec((chunks, HD, width), lambda h: (0, heads + h, 0)),
+            pl.BlockSpec((HD, width), lambda h: (h, 0)),
+            pl.BlockSpec((HD, width), lambda h: (heads + h, 0)),
             pl.BlockSpec((rows, 1), lambda h: (0, 0)),
             pl.BlockSpec((rows, 1), lambda h: (0, 0)),
+            stat_spec,
+            stat_spec,
+            acc_spec,
         ],
-        out_specs=pl.BlockSpec((None, rows, HD), lambda h: (h, 0, 0)),
-        out_shape=jax.ShapeDtypeStruct((heads, rows, HD), jnp.bfloat16),
+        out_specs=[stat_spec, stat_spec, acc_spec],
+        out_shape=[
+            jax.ShapeDtypeStruct(m.shape, jnp.float32),
+            jax.ShapeDtypeStruct(l.shape, jnp.float32),
+            jax.ShapeDtypeStruct(acc.shape, jnp.float32),
+        ],
+        input_output_aliases={5: 0, 6: 1, 7: 2},
+        cost_estimate=pl.CostEstimate(
+            flops=4 * heads * rows * width * HD,
+            transcendentals=heads * rows * width,
+            bytes_accessed=2 * kv_blk.size + 4 * acc.size,
+        ),
         compiler_params=pltpu.CompilerParams(
             dimension_semantics=("arbitrary",), vmem_limit_bytes=48 * 1024 * 1024
         ),
-    )(q_heads, kv_t, kv_t, qidx, qstart)
+    )(q_heads, kv_blk, kv_blk, qi_rel, qs_rel, m, l, acc)
 
 
 def body(
@@ -134,30 +140,66 @@
         .transpose(1, 2, 0, 3)
         .reshape(KVH, per_group * tok_rows, HD)
     )
-    suf_keys = rotate(
-        suffix_kv[:, :kv_width].astype(jnp.float32).reshape(tok_rows, KVH, HD), positions
-    ).astype(jnp.bfloat16)
     page_count = prefix_kv.shape[0]
     page_size = prefix_kv.shape[1]
     pre_len = page_count * page_size
+    key_count = pre_len + tok_rows
     page_pos = (
         page_table[:, None] * page_size + jnp.arange(page_size, dtype=jnp.int32)[None, :]
     ).reshape(-1)
-    page_keys = rotate(
-        prefix_kv[:, :, :kv_width].astype(jnp.float32).reshape(pre_len, KVH, HD),
-        page_pos,
+    key_pos = jnp.concatenate([page_pos, positions]).astype(jnp.float32)
+    raw_t = jnp.concatenate(
+        [prefix_kv.reshape(pre_len, 2 * kv_width), suffix_kv], axis=0
+    ).T
+    half_dim = HD // 2
+    exponent = jnp.arange(half_dim, dtype=jnp.float32) * (2.0 / HD)
+    inverse = jnp.exp(-exponent * math.log(THETA))
+    angles = inverse[:, None] * key_pos[None, :]
+    cosine = jnp.cos(angles)[None]
+    sine_part = jnp.sin(angles)[None]
+    halves = raw_t[:kv_width].astype(jnp.float32).reshape(KVH, 2, half_dim, key_count)
+    first_half = halves[:, 0]
+    second = halves[:, 1]
+    keys_t = jnp.stack(
+        [first_half * cosine - second * sine_part, second * cosine + first_half * sine_part],
+        axis=1,
     ).astype(jnp.bfloat16)
-    keys_all = jnp.concatenate(
-        [page_keys.reshape(pre_len, kv_width), suf_keys.reshape(tok_rows, kv_width)], axis=0
-    )
-    values_all = jnp.concatenate(
-        [prefix_kv[:, :, kv_width:].reshape(pre_len, kv_width), suffix_kv[:, kv_width:]], axis=0
-    )
-    local_t = jnp.concatenate([keys_all, values_all], axis=1).T
-    kv_t = lax.all_gather(local_t[None], "kv", axis=0, tiled=True)
+    values_t = raw_t[kv_width:]
+    local_t = jnp.concatenate([keys_t.reshape(kv_width, key_count), values_t], axis=0)
     qidx = jnp.tile(tok_index, per_group)[:, None]
     qstart = jnp.tile(request_start, per_group)[:, None]
-    out_heads = attention(q_heads, kv_t, qidx, qstart, pre_len, tok_rows)
+    rows = per_group * tok_rows
+    state = (
+        jnp.full((KVH, rows, 1), NEG, jnp.float32),
+        jnp.zeros((KVH, rows, 1), jnp.float32),
+        jnp.zeros((KVH, rows, HD), jnp.float32),
+    )
+    n_kv = lax.axis_size("kv")
+    me = lax.axis_index("kv")
+
+    def absorb_block(state, blk, owner):
+        return attention_block(
+            q_heads, blk, qidx - owner * tok_rows, qstart - owner * tok_rows, state, pre_len
+        )
+
+    cw_pairs = [(i, (i + 1) % n_kv) for i in range(n_kv)]
+    ccw_pairs = [(i, (i - 1) % n_kv) for i in range(n_kv)]
+    prev_state = state
+    state = absorb_block(state, local_t, me)
+    cw_blk = local_t
+    ccw_blk = local_t
+    for step in range(1, n_kv // 2 + 1):
+        if step > 1:
+            (cw_blk, ccw_blk), unused = lax.optimization_barrier(((cw_blk, ccw_blk), prev_state))
+        prev_state = state
+        cw_blk = lax.ppermute(cw_blk, "kv", cw_pairs)
+        if step < n_kv - step:
+            ccw_blk = lax.ppermute(ccw_blk, "kv", ccw_pairs)
+        state = absorb_block(state, cw_blk, (me - step) % n_kv)
+        if step < n_kv - step:
+            state = absorb_block(state, ccw_blk, (me + step) % n_kv)
+    final_max, denom, accumulated = state
+    out_heads = (accumulated / denom).astype(jnp.bfloat16)
     attended = (
         out_heads.reshape(KVH, per_group, tok_rows, HD)
         .transpose(2, 0, 1, 3)

time: 490 us -> 419 us (0.86)
  waiting for transfers between devices: 278 us -> 177 us
  local copies, waits for them, and re-layouts: 24.6 us -> 53.5 us
  starting transfers between devices: 0.3 us -> 9.8 us
  Pallas kernels: 116 us -> 110 us
    all_gather x1 -> x0, waiting for transfers between devices: 108 us -> none  [body(): kv_t = lax.all_gather(local_t[None], 'kv', axis=0, tiled=True)]
    unnamed x17 -> x71, local copies, waits for them, and re-layouts: 7.84 us -> 28.8 us
    sub x0 -> x16, local copies, waits for them, and re-layouts: none -> 13.8 us  [the longest x8 6.95 us: absorb_block(): qidx - owner * tok_rows]
    ppermute x0 -> x7, starting transfers between devices: none -> 9.5 us  [the longest x3 9.2 us: body(): ccw_blk = lax.ppermute(ccw_blk, 'kv', ccw_pairs)]
    ppermute x0 -> x7, waiting for transfers between devices: none -> 6.51 us  [the longest x4 6.51 us: body(): cw_blk = lax.ppermute(cw_blk, 'kv', cw_pairs)]
    pallas_call x1 -> x8, Pallas kernels: 116 us -> 110 us  [attention_block(): pl.pallas_call(kernel, grid=(heads,), in_specs=[pl.BlockSpec((None, rows,...]
    reshape x3 -> x1, local copies, waits for them, and re-layouts: 9.61 us -> 4.58 us  [body(): prefix_kv.reshape(pre_len, 2 * kv_width)]
  transfers between devices with their start and end apart: 3 -> 9, of which waited for: 3 -> 3; matrix products, arithmetic and copies ran while one was open for 2% -> 6% of each run, Pallas kernels for 0% -> 23%
where the time goes in v4:
time: 419 us; the launch traced here: 418 us
  waiting for transfers between devices  177 us (42%)
  Pallas kernels  110 us (26%)
  local copies, waits for them, and re-layouts  53.5 us (13%)
  matrix products  35.1 us (8%)
  other arithmetic  18.1 us (4%)
  between operations  14.4 us (3%)
  starting transfers between devices  9.8 us (2%)
    pallas_call x8, Pallas kernels, attention_block(): pl.pallas_call(kernel, grid=(heads,), in_specs=[pl.BlockSpec((None, rows,...  110 us
    reduce_scatter x1, waiting for transfers between devices, body(): lax.psum_scatter(jnp.dot(activated, w_down, preferred_element_type=jnp.fl...  88.7 us
    all_gather x1, waiting for transfers between devices, body(): shard_piece = lax.all_gather(normed, 'req', axis=0, tiled=True)  81.4 us
    unnamed x71, local copies, waits for them, and re-layouts  28.8 us
    dot_general x1, matrix products, body(): jnp.dot(activated, w_down, preferred_element_type=jnp.float32)  16.9 us
    dot_general x1, matrix products, body(): gate_proj = jnp.dot(shard_piece, w_gate, preferred_element_type=jnp.float32)  11.4 us
    ppermute x3, starting transfers between devices, body(): ccw_blk = lax.ppermute(ccw_blk, 'kv', ccw_pairs)  9.2 us
  transfers between devices with their start and end apart: 9, of which 3 were waited for; matrix products, arithmetic and copies ran while one was open for 6% of the time, Pallas kernels for 23%

profile of v4, /device:TPU:0, one launch (start us, length us, event | category | flops | bytes accessed | tf_op | source)
XLA Modules:
  0.0 417.9 jit_solution(1777411315395958593)
XLA Ops:
  7.3 1.0 reduce-window.8
  9.0 4.6 %copy.114 = bf16[1024,1280]{0,1:T(8,128)(2,1)} copy(bf16[1024,1280]{1,0:T(8,128)(2,1)} %bitcast.58) | data formatting | bytes 5242880 | tf_op jit(solution)/shard_map/reshape | solution.py:152
  13.8 2.0 maximum_bitcast_fusion
  18.1 1.8 pad_maximum_fusion.refs_1_.refs_2_
  20.0 3.6 collective-permute-start.1
  23.6 1.4 copy.88
  25.4 1.4 copy.89
  26.9 1.3 copy.90
  28.2 0.9 copy.97.refs_4_
  29.0 0.9 copy.96.refs_3_
  29.9 2.1 pad_maximum_fusion.2
  32.3 1.5 broadcast_in_dim.42.clone.refs_7_
  33.8 13.7 %shard_map.122 = (f32[8,512,1]{2,1,0:T(8,128)S(1)}, f32[8,512,1]{2,1,0:T(8,128)S(1)}, f32[8,512,80]{2,1,0:T(8,128)}) custom-call(bf16[8,512,80]{2,1,0:T(8,128)(2,1)S(1)} %bitcast.45, bf16[1280,1152]{1,0:T(8,128)(2,1)} %pad_maximum_fusion.refs_1_.refs_2_, ...), custom_call_target="tpu_custom_call", output_to_operand_aliasing={{0}: (5, {}), {1}: (6, {}), {2}: (7, {})} | custom-call | flops 1509949440 | bytes 4259840 | tf_op jit(solution)/shard_map/pallas_call | solution.py:84
  47.6 1.3 copy-done.1
  48.9 1.3 copy-done.8
  50.2 6.5 %collective-permute-done.refs_1_.refs_2_ = bf16[1280,1152]{1,0:T(8,128)(2,1)} collective-permute-done((bf16[1280,1152]{1,0:T(8,128)(2,1)}, bf16[1280,1152]{1,0:T(8,128)(2,1)}, u32[]{:S(2)}, u32[]{:S(2)}) %collective-permute-start) | collective-permute-done | bytes 2949152 | tf_op jit(solution)/shard_map/ppermute | solution.py:195
  57.0 2.7 collective-permute-start.3
  60.6 0.9 copy.98.refs_3_
  61.5 0.9 copy.101.refs_4_
  62.3 0.9 copy.100.refs_3_
  63.2 1.6 copy-done.2
  64.8 1.6 copy-done.9
  66.4 0.9 copy-done.20
  67.3 0.9 copy-done.24
  68.3 13.8 %shard_map.123 = (f32[8,512,1]{2,1,0:T(8,128)S(1)}, f32[8,512,1]{2,1,0:T(8,128)S(1)}, f32[8,512,80]{2,1,0:T(8,128)}) custom-call(bf16[8,512,80]{2,1,0:T(8,128)(2,1)S(1)} %bitcast.46, bf16[1280,1152]{1,0:T(8,128)(2,1)} %collective-permute-done.refs_1_.refs_2_, ...), custom_call_target="tpu_custom_call", output_to_operand_aliasing={{0}: (5, {}), {1}: (6, {}), {2}: (7, {})} | custom-call | flops 1509949440 | bytes 4259840 | tf_op jit(solution)/shard_map/pallas_call | solution.py:84
  82.0 13.8 %shard_map.124 = (f32[8,512,1]{2,1,0:T(8,128)S(1)}, f32[8,512,1]{2,1,0:T(8,128)S(1)}, f32[8,512,80]{2,1,0:T(8,128)}) custom-call(bf16[8,512,80]{2,1,0:T(8,128)(2,1)S(1)} %bitcast.47, bf16[1280,1152]{1,0:T(8,128)(2,1)} %collective-permute-done.1.refs_1_.refs_2_, ...), custom_call_target="tpu_custom_call", output_to_operand_aliasing={{0}: (5, {}), {1}: (6, {}), {2}: (7, {})} | custom-call | flops 1509949440 | bytes 4259840 | tf_op jit(solution)/shard_map/pallas_call | solution.py:84
  95.8 1.3 copy-done.3
  97.1 1.3 copy-done.10
  98.4 2.9 collective-permute-start.5
  102.3 0.9 copy.102.refs_3_
  103.2 0.9 copy.105.refs_4_
  104.0 0.9 copy.104.refs_3_
  104.9 1.6 copy-done.4
  106.5 1.6 copy-done.11
  108.1 0.9 copy-done.21
  109.0 0.9 copy-done.25
  110.0 13.8 %shard_map.125 = (f32[8,512,1]{2,1,0:T(8,128)S(1)}, f32[8,512,1]{2,1,0:T(8,128)S(1)}, f32[8,512,80]{2,1,0:T(8,128)}) custom-call(bf16[8,512,80]{2,1,0:T(8,128)(2,1)S(1)} %bitcast.48, bf16[1280,1152]{1,0:T(8,128)(2,1)} %collective-permute-done.2.refs_1_.refs_2_, ...), custom_call_target="tpu_custom_call", output_to_operand_aliasing={{0}: (5, {}), {1}: (6, {}), {2}: (7, {})} | custom-call | flops 1509949440 | bytes 4259840 | tf_op jit(solution)/shard_map/pallas_call | solution.py:84
  123.8 13.9 %shard_map.126 = (f32[8,512,1]{2,1,0:T(8,128)S(1)}, f32[8,512,1]{2,1,0:T(8,128)S(1)}, f32[8,512,80]{2,1,0:T(8,128)}) custom-call(bf16[8,512,80]{2,1,0:T(8,128)(2,1)S(1)} %bitcast.49, bf16[1280,1152]{1,0:T(8,128)(2,1)} %collective-permute-done.3.refs_1_.refs_2_, ...), custom_call_target="tpu_custom_call", output_to_operand_aliasing={{0}: (5, {}), {1}: (6, {}), {2}: (7, {})} | custom-call | flops 1509949440 | bytes 4259840 | tf_op jit(solution)/shard_map/pallas_call | solution.py:84
  137.7 1.3 copy-done.5
  139.0 1.3 copy-done.12
  141.2 0.9 copy.106.refs_3_
  142.1 0.9 copy.109.refs_4_
  143.8 0.9 copy.111.refs_4_
  144.7 0.9 copy.110.refs_3_
  145.5 1.6 copy-done.6
  147.1 1.6 copy-done.13
  148.7 0.9 copy-done.14
  149.7 0.9 copy-done.17
  150.6 13.8 %shard_map.127 = (f32[8,512,1]{2,1,0:T(8,128)S(1)}, f32[8,512,1]{2,1,0:T(8,128)S(1)}, f32[8,512,80]{2,1,0:T(8,128)}) custom-call(bf16[8,512,80]{2,1,0:T(8,128)(2,1)S(1)} %bitcast.50, bf16[1280,1152]{1,0:T(8,128)(2,1)} %collective-permute-done.4.refs_1_.refs_2_, ...), custom_call_target="tpu_custom_call", output_to_operand_aliasing={{0}: (5, {}), {1}: (6, {}), {2}: (7, {})} | custom-call | flops 1509949440 | bytes 4259840 | tf_op jit(solution)/shard_map/pallas_call | solution.py:84
  164.4 13.8 %shard_map.128 = (f32[8,512,1]{2,1,0:T(8,128)S(1)}, f32[8,512,1]{2,1,0:T(8,128)S(1)}, f32[8,512,80]{2,1,0:T(8,128)}) custom-call(bf16[8,512,80]{2,1,0:T(8,128)(2,1)S(1)} %bitcast.51, bf16[1280,1152]{1,0:T(8,128)(2,1)} %collective-permute-done.5.refs_1_.refs_2_, ...), custom_call_target="tpu_custom_call", output_to_operand_aliasing={{0}: (5, {}), {1}: (6, {}), {2}: (7, {})} | custom-call | flops 1509949440 | bytes 4259840 | tf_op jit(solution)/shard_map/pallas_call | solution.py:84
  178.2 13.8 %shard_map.129 = (f32[8,512,1]{2,1,0:T(8,128)S(1)}, f32[8,512,1]{2,1,0:T(8,128)S(1)}, f32[8,512,80]{2,1,0:T(8,128)}) custom-call(bf16[8,512,80]{2,1,0:T(8,128)(2,1)S(1)} %bitcast.52, bf16[1280,1152]{1,0:T(8,128)(2,1)} %collective-permute-done.6.refs_1_.refs_2_, ...), custom_call_target="tpu_custom_call", output_to_operand_aliasing={{0}: (5, {}), {1}: (6, {}), {2}: (7, {})} | custom-call | flops 1509949440 | bytes 4259840 | tf_op jit(solution)/shard_map/pallas_call | solution.py:84
  192.0 1.3 copy-done.7
  193.3 2.2 reduce
  195.6 2.8 divide_convert_fusion
  198.3 1.5 copy.112
  199.8 6.8 %multiply_reduce_fusion = (f32[128]{0:T(128)S(1)}, f32[128,2560]{1,0:T(8,128)S(1)}) fusion(bf16[128,2560]{0,1:T(8,128)(2,1)S(1)} %bitcast.53, bf16[2560,2560]{1,0:T(8,128)(2,1)} %param.17, bf16[128,2560]{1,0:T(8,128)(2,1)} %param.11), kind=kOutput, calls=%fused_computation.14 | convolution fusion | flops 1679687552 | bytes 15729152 | tf_op jit(solution)/shard_map/dot_general | solution.py:208
  206.7 1.1 copy-done.30
  207.8 1.0 multiply_convert_fusion.1
  209.1 81.4 %all-gather.2.cloned.1.call-done = bf16[2048,2560]{1,0:T(8,128)(2,1)} async-done(((bf16[128,2560]{1,0:T(8,128)(2,1)}), bf16[2048,2560]{1,0:T(8,128)(2,1)}) %all-gather.2.cloned.1.call-update) | async-done | bytes 10485776 | tf_op jit(solution)/shard_map/all_gather | solution.py:217
  290.5 11.4 %fusion.6 = f32[2048,448]{0,1:T(8,128)} fusion(bf16[2048,2560]{1,0:T(8,128)(2,1)} %all-gather.2.cloned.1.call-done, bf16[2560,448]{0,1:T(8,128)(2,1)} %param.19), kind=kOutput, calls=%fused_computation.48 | convolution fusion | flops 4697620480 | bytes 16449536 | tf_op jit(solution)/shard_map/dot_general | solution.py:218
  301.9 16.9 %convolution_convert_fusion = bf16[2048,2560]{1,0:T(8,128)(2,1)} fusion(bf16[448,2560]{1,0:T(8,128)(2,1)S(1)} %copy-done, f32[2048,448]{0,1:T(8,128)} %fusion.6, bf16[2048,2560]{1,0:T(8,128)(2,1)} %all-gather.2.cloned.1.call-done, bf16[2560,448]{0,1:T(8,128)(2,1)} %param.20), kind=kOutput, calls=%fused_computation | convolution fusion | flops 9405988864 | bytes 29229056 | tf_op jit(solution)/shard_map/dot_general | solution.py:222
  318.8 1.1 copy.113
  319.9 88.7 %reduce-scatter.2.cloned.1.call-done = bf16[128,2560]{1,0:T(8,128)(2,1)} async-done(((bf16[2048,2560]{1,0:T(8,128)(2,1)}), bf16[128,2560]{1,0:T(8,128)(2,1)}) %reduce-scatter.2.cloned.1.call-update) | async-done | bytes 655376 | tf_op jit(solution)/shard_map/reduce_scatter | solution.py:221
  408.6 2.4 add_convert_fusion.1
  (104 shorter events, 8.1 us)
Async XLA Ops:
  7.2 294.8 %copy-start = (bf16[448,2560]{1,0:T(8,128)(2,1)S(1)}, bf16[448,2560]{1,0:T(8,128)(2,1)}, u32[]{:S(2)}) copy-start(bf16[448,2560]{1,0:T(8,128)(2,1)} %param.21) | copy-start | bytes 6881284
  7.2 283.4 %all-gather.2.cloned.1.call-start = ((), (), s32[]{:S(2)}) async-start(), calls=%async_computation.1 | async-start | bytes 11141120 | tf_op jit(solution)/shard_map/all_gather | solution.py:217
  9.0 4.6 %copy-start.31 = (bf16[128,1280]{1,0:T(8,128)(2,1)S(1)}, bf16[128,1280]{1,0:T(8,128)(2,1)}, u32[]{:S(2)}) copy-start(bf16[128,1280]{1,0:T(8,128)(2,1)} %param.13) | copy-start | bytes 983044
  16.1 0.7 copy-start.33
  20.0 36.7 %collective-permute-start = (bf16[1280,1152]{1,0:T(8,128)(2,1)}, bf16[1280,1152]{1,0:T(8,128)(2,1)}, u32[]{:S(2)}, u32[]{:S(2)}) collective-permute-start(bf16[1280,1152]{1,0:T(8,128)(2,1)} %pad_maximum_fusion.refs_1_.refs_2_), channel_id=1, source_target_pairs={{0,1},{1,2},{2,3},{3,4},{4,5},{5,6},{6,7},{7,0},{8,9},{9,10},{10,1... | collective-permute-start | bytes 8847368 | tf_op jit(solution)/shard_map/ppermute | solution.py:195
  20.0 36.7 %collective-permute-start.1 = (bf16[1280,1152]{1,0:T(8,128)(2,1)}, bf16[1280,1152]{1,0:T(8,128)(2,1)}, u32[]{:S(2)}, u32[]{:S(2)}) collective-permute-start(bf16[1280,1152]{1,0:T(8,128)(2,1)} %pad_maximum_fusion.refs_1_.refs_2_), channel_id=1, source_target_pairs={{0,7},{1,0},{2,1},{3,2},{4,3},{5,4},{6,5},{7,6},{8,15},{9,8},{10,9... | collective-permute-start | bytes 8847368 | tf_op jit(solution)/shard_map/ppermute | solution.py:197
  32.2 1.7 copy-start.26
  32.2 1.7 copy-start.29
  47.6 1.3 copy-start.1
  48.9 1.3 copy-start.8
  56.7 41.7 %collective-permute-start.2 = (bf16[1280,1152]{1,0:T(8,128)(2,1)}, bf16[1280,1152]{1,0:T(8,128)(2,1)}, u32[]{:S(2)}, u32[]{:S(2)}) collective-permute-start(bf16[1280,1152]{1,0:T(8,128)(2,1)} %collective-permute-done.refs_1_.refs_2_), channel_id=1, source_target_pairs={{0,1},{1,2},{2,3},{3,4},{4,5},{5,6},{6,7},{7,0},{8,9},{9,10},{10,1... | collective-permute-start | bytes 8847368 | tf_op jit(solution)/shard_map/ppermute | solution.py:195
  57.0 41.4 %collective-permute-start.3 = (bf16[1280,1152]{1,0:T(8,128)(2,1)}, bf16[1280,1152]{1,0:T(8,128)(2,1)}, u32[]{:S(2)}, u32[]{:S(2)}) collective-permute-start(bf16[1280,1152]{1,0:T(8,128)(2,1)} %collective-permute-done.1.refs_1_.refs_2_), channel_id=1, source_target_pairs={{0,7},{1,0},{2,1},{3,2},{4,3},{5,4},{6,5},{7,6},{8,15},{9,8},{10,9... | collective-permute-start | bytes 8847368 | tf_op jit(solution)/shard_map/ppermute | solution.py:197
  63.2 1.6 copy-start.2
  64.8 1.6 copy-start.9
  66.4 0.9 copy-start.20
  67.3 0.9 copy-start.24
  68.3 13.8 %copy-start.22 = (s32[512,1]{1,0:T(8,128)S(1)}, s32[512,1]{1,0:T(8,128)}, u32[]{:S(2)}) copy-start(s32[512,1]{1,0:T(8,128)} %copy.101.refs_4_) | copy-start | bytes 6148
  68.3 13.8 %copy-start.27 = (s32[512,1]{1,0:T(8,128)S(1)}, s32[512,1]{1,0:T(8,128)}, u32[]{:S(2)}) copy-start(s32[512,1]{1,0:T(8,128)} %copy.100.refs_3_) | copy-start | bytes 6148
  95.8 1.3 copy-start.3
  97.1 1.3 copy-start.10
  98.4 41.9 %collective-permute-start.4 = (bf16[1280,1152]{1,0:T(8,128)(2,1)}, bf16[1280,1152]{1,0:T(8,128)(2,1)}, u32[]{:S(2)}, u32[]{:S(2)}) collective-permute-start(bf16[1280,1152]{1,0:T(8,128)(2,1)} %collective-permute-done.2.refs_1_.refs_2_), channel_id=1, source_target_pairs={{0,1},{1,2},{2,3},{3,4},{4,5},{5,6},{6,7},{7,0},{8,9},{9,10},{10,1... | collective-permute-start | bytes 8847368 | tf_op jit(solution)/shard_map/ppermute | solution.py:195
  98.4 41.9 %collective-permute-start.5 = (bf16[1280,1152]{1,0:T(8,128)(2,1)}, bf16[1280,1152]{1,0:T(8,128)(2,1)}, u32[]{:S(2)}, u32[]{:S(2)}) collective-permute-start(bf16[1280,1152]{1,0:T(8,128)(2,1)} %collective-permute-done.3.refs_1_.refs_2_), channel_id=1, source_target_pairs={{0,7},{1,0},{2,1},{3,2},{4,3},{5,4},{6,5},{7,6},{8,15},{9,8},{10,9... | collective-permute-start | bytes 8847368 | tf_op jit(solution)/shard_map/ppermute | solution.py:197
  104.9 1.6 copy-start.4
  106.5 1.6 copy-start.11
  108.1 0.9 copy-start.21
  109.0 0.9 copy-start.25
  110.0 13.8 %copy-start.23 = (s32[512,1]{1,0:T(8,128)S(1)}, s32[512,1]{1,0:T(8,128)}, u32[]{:S(2)}) copy-start(s32[512,1]{1,0:T(8,128)} %copy.105.refs_4_) | copy-start | bytes 6148
  110.0 13.8 %copy-start.28 = (s32[512,1]{1,0:T(8,128)S(1)}, s32[512,1]{1,0:T(8,128)}, u32[]{:S(2)}) copy-start(s32[512,1]{1,0:T(8,128)} %copy.104.refs_3_) | copy-start | bytes 6148
  137.7 1.3 copy-start.5
  139.0 1.3 copy-start.12
  140.3 37.9 %collective-permute-start.6 = (bf16[1280,1152]{1,0:T(8,128)(2,1)}, bf16[1280,1152]{1,0:T(8,128)(2,1)}, u32[]{:S(2)}, u32[]{:S(2)}) collective-permute-start(bf16[1280,1152]{1,0:T(8,128)(2,1)} %collective-permute-done.4.refs_1_.refs_2_), channel_id=1, source_target_pairs={{0,1},{1,2},{2,3},{3,4},{4,5},{5,6},{6,7},{7,0},{8,9},{9,10},{10,1... | collective-permute-start | bytes 8847368 | tf_op jit(solution)/shard_map/ppermute | solution.py:195
  145.5 1.6 copy-start.6
  147.1 1.6 copy-start.13
  148.7 0.9 copy-start.14
  149.7 0.9 copy-start.17
  150.6 13.8 %copy-start.16 = (s32[512,1]{1,0:T(8,128)S(1)}, s32[512,1]{1,0:T(8,128)}, u32[]{:S(2)}) copy-start(s32[512,1]{1,0:T(8,128)} %copy.109.refs_4_) | copy-start | bytes 6148
  150.6 13.8 %copy-start.19 = (s32[512,1]{1,0:T(8,128)S(1)}, s32[512,1]{1,0:T(8,128)}, u32[]{:S(2)}) copy-start(s32[512,1]{1,0:T(8,128)} %copy.108.refs_3_) | copy-start | bytes 6148
  164.4 13.8 %copy-start.15 = (s32[512,1]{1,0:T(8,128)S(1)}, s32[512,1]{1,0:T(8,128)}, u32[]{:S(2)}) copy-start(s32[512,1]{1,0:T(8,128)} %copy.111.refs_4_) | copy-start | bytes 6148
  164.4 13.8 %copy-start.18 = (s32[512,1]{1,0:T(8,128)S(1)}, s32[512,1]{1,0:T(8,128)}, u32[]{:S(2)}) copy-start(s32[512,1]{1,0:T(8,128)} %copy.110.refs_3_) | copy-start | bytes 6148
  192.0 1.3 copy-start.7
  199.8 8.0 %copy-start.32 = (f32[2560]{0:T(1024)S(1)}, f32[2560]{0:T(1024)}, u32[]{:S(2)}) copy-start(f32[2560]{0:T(1024)} %param.18) | copy-start | bytes 30724
  206.6 1.2 copy-start.30
  208.8 199.8 %reduce-scatter.2.cloned.1.call-start = ((), (), s32[]{:S(2)}) async-start(), calls=%async_computation.2 | async-start | bytes 11141120 | tf_op jit(solution)/shard_map/reduce_scatter | solution.py:221
Sparse Core Ops, SparseCore 0:
  209.0 81.5 all-gather.1
  319.0 89.6 reduce-scatter.1

commit v5 on v4

--- a/solution.py
+++ b/solution.py
@@ -40,19 +40,25 @@
     return (request_of, request_start)
 
 
-def attn_kernel(q_ref, k_ref, v_ref, qi_ref, qs_ref, m_in, l_in, acc_in, m_ref, l_ref, acc_ref, *, pre_len):
+def attn_kernel(sc_ref, q_ref, k_ref, v_ref, st_in, st_ref, *, pre_len):
     rows = q_ref.shape[0]
     suf_len = k_ref.shape[1] - pre_len
     scale = HD ** (-0.5)
     q = q_ref[...]
     kt = k_ref[...]
     vt = v_ref[...]
-    m = m_in[...]
-    l = l_in[...]
+    st = st_in[...]
+    acc = st[:, :HD]
+    l = st[:, HD:HD + 1]
+    m = st[:, HD + 1:HD + 2]
     s_pre = jnp.dot(q, kt[:, :pre_len], preferred_element_type=jnp.float32) * scale
     s_suf = jnp.dot(q, kt[:, pre_len:], preferred_element_type=jnp.float32) * scale
-    kidx = lax.broadcasted_iota(jnp.int32, (rows, suf_len), 1)
-    mask = (kidx >= qs_ref[...]) & (kidx <= qi_ref[...])
+    qi = sc_ref[1] + lax.broadcasted_iota(jnp.int32, (rows, 1), 0) % suf_len
+    qs = jnp.zeros((rows, 1), jnp.int32)
+    for j in range(3):
+        qs = qs + jnp.where(qi >= sc_ref[2 + 2 * j], sc_ref[3 + 2 * j], 0)
+    kidx = sc_ref[0] + lax.broadcasted_iota(jnp.int32, (rows, suf_len), 1)
+    mask = (kidx >= qs) & (kidx <= qi)
     s_suf = jnp.where(mask, s_suf, NEG)
     m_new = jnp.maximum(
         m,
@@ -61,7 +67,7 @@
     alpha = jnp.exp(m - m_new)
     p_pre = jnp.exp(s_pre - m_new)
     p_suf = jnp.where(mask, jnp.exp(s_suf - m_new), 0.0)
-    l_ref[...] = alpha * l + (
+    l_new = alpha * l + (
         jnp.sum(p_pre, axis=1, keepdims=True) + jnp.sum(p_suf, axis=1, keepdims=True)
     )
     nt = (((1,), (1,)), ((), ()))
@@ -70,46 +76,38 @@
     ) + lax.dot_general(
         p_suf.astype(jnp.bfloat16), vt[:, pre_len:], nt, preferred_element_type=jnp.float32
     )
-    acc_ref[...] = alpha * acc_in[...] + pv
-    m_ref[...] = m_new
-
-
-def attention_block(q_heads, kv_blk, qi_rel, qs_rel, state, pre_len):
+    st_ref[:, :HD] = alpha * acc + pv
+    st_ref[:, HD:HD + 1] = l_new
+    st_ref[:, HD + 1:HD + 2] = m_new
+
+
+def attention_block(q_heads, kv_blk, scalars, state, pre_len):
     heads, rows, _ = q_heads.shape
     width = kv_blk.shape[1]
-    m, l, acc = state
     kernel = lambda *refs: attn_kernel(*refs, pre_len=pre_len)
-    stat_spec = pl.BlockSpec((None, rows, 1), lambda h: (h, 0, 0))
-    acc_spec = pl.BlockSpec((None, rows, HD), lambda h: (h, 0, 0))
+    st_spec = pl.BlockSpec((None, rows, state.shape[2]), lambda h: (h, 0, 0))
     return pl.pallas_call(
         kernel,
         grid=(heads,),
         in_specs=[
+            pl.BlockSpec(memory_space=pltpu.SMEM),
             pl.BlockSpec((None, rows, HD), lambda h: (h, 0, 0)),
             pl.BlockSpec((HD, width), lambda h: (h, 0)),
             pl.BlockSpec((HD, width), lambda h: (heads + h, 0)),
-            pl.BlockSpec((rows, 1), lambda h: (0, 0)),
-            pl.BlockSpec((rows, 1), lambda h: (0, 0)),
-            stat_spec,
-            stat_spec,
-            acc_spec,
+            st_spec,
         ],
-        out_specs=[stat_spec, stat_spec, acc_spec],
-        out_shape=[
-            jax.ShapeDtypeStruct(m.shape, jnp.float32),
-            jax.ShapeDtypeStruct(l.shape, jnp.float32),
-            jax.ShapeDtypeStruct(acc.shape, jnp.float32),
-        ],
-        input_output_aliases={5: 0, 6: 1, 7: 2},
+        out_specs=st_spec,
+        out_shape=jax.ShapeDtypeStruct(state.shape, jnp.float32),
+        input_output_aliases={4: 0},
         cost_estimate=pl.CostEstimate(
             flops=4 * heads * rows * width * HD,
             transcendentals=heads * rows * width,
-            bytes_accessed=2 * kv_blk.size + 4 * acc.size,
+            bytes_accessed=2 * kv_blk.size + 8 * state.size,
         ),
         compiler_params=pltpu.CompilerParams(
             dimension_semantics=("arbitrary",), vmem_limit_bytes=48 * 1024 * 1024
         ),
-    )(q_heads, kv_blk, kv_blk, qi_rel, qs_rel, m, l, acc)
+    )(scalars, q_heads, kv_blk, kv_blk, state)
 
 
 def body(
@@ -166,21 +164,19 @@
     ).astype(jnp.bfloat16)
     values_t = raw_t[kv_width:]
     local_t = jnp.concatenate([keys_t.reshape(kv_width, key_count), values_t], axis=0)
-    qidx = jnp.tile(tok_index, per_group)[:, None]
-    qstart = jnp.tile(request_start, per_group)[:, None]
+    request_ends = jnp.cumsum(request_lens)
+    base_scalars = jnp.stack(
+        [tok_index[0]]
+        + [v for j in range(3) for v in (request_ends[j], request_lens[j])]
+    ).astype(jnp.int32)
     rows = per_group * tok_rows
-    state = (
-        jnp.full((KVH, rows, 1), NEG, jnp.float32),
-        jnp.zeros((KVH, rows, 1), jnp.float32),
-        jnp.zeros((KVH, rows, HD), jnp.float32),
-    )
+    state = jnp.zeros((KVH, rows, 128), jnp.float32).at[:, :, HD + 1].set(NEG)
     n_kv = lax.axis_size("kv")
     me = lax.axis_index("kv")
 
     def absorb_block(state, blk, owner):
-        return attention_block(
-            q_heads, blk, qidx - owner * tok_rows, qstart - owner * tok_rows, state, pre_len
-        )
+        scalars = jnp.concatenate([jnp.reshape(owner * tok_rows, (1,)), base_scalars])
+        return attention_block(q_heads, blk, scalars.astype(jnp.int32), state, pre_len)
 
     cw_pairs = [(i, (i + 1) % n_kv) for i in range(n_kv)]
     ccw_pairs = [(i, (i - 1) % n_kv) for i in range(n_kv)]
@@ -198,8 +194,7 @@
         state = absorb_block(state, cw_blk, (me - step) % n_kv)
         if step < n_kv - step:
             state = absorb_block(state, ccw_blk, (me + step) % n_kv)
-    final_max, denom, accumulated = state
-    out_heads = (accumulated / denom).astype(jnp.bfloat16)
+    out_heads = (state[:, :, :HD] / state[:, :, HD:HD + 1]).astype(jnp.bfloat16)
     attended = (
         out_heads.reshape(KVH, per_group, tok_rows, HD)
         .transpose(2, 0, 1, 3)

time: 419 us -> 413 us (0.986)
  Pallas kernels: 110 us -> 100 us
  local copies, waits for them, and re-layouts: 53.5 us -> 59.3 us
    concatenate x0 -> x8, local copies, waits for them, and re-layouts: none -> 31 us  [absorb_block(): jnp.concatenate([jnp.reshape(owner * tok_rows, (1,)), base_scalars])]
    sub x16 -> x0, local copies, waits for them, and re-layouts: 13.8 us -> none  [the longest x8 6.95 us: absorb_block(): qidx - owner * tok_rows]
    unnamed x71 -> x26, local copies, waits for them, and re-layouts: 28.8 us -> 16.8 us
    pallas_call x8, Pallas kernels: 110 us -> 100 us  [attention_block(): pl.pallas_call(kernel, grid=(heads,), in_specs=[pl.BlockSpec(memory_space...]
  transfers between devices with their start and end apart: 9 -> 9, of which waited for: 3 -> 4; matrix products, arithmetic and copies ran while one was open for 6% -> 11% of each run, Pallas kernels for 23% -> 21%
where the time goes in v5:
time: 413 us; the launch traced here: 412 us
  waiting for transfers between devices  178 us (43%)
  Pallas kernels  100 us (24%)
  local copies, waits for them, and re-layouts  59.3 us (14%)
  matrix products  35 us (8%)
  other arithmetic  15.5 us (4%)
  between operations  14.4 us (3%)
  starting transfers between devices  9.58 us (2%)
    pallas_call x8, Pallas kernels, attention_block(): pl.pallas_call(kernel, grid=(heads,), in_specs=[pl.BlockSpec(memory_space...  100 us
    reduce_scatter x1, waiting for transfers between devices, body(): lax.psum_scatter(jnp.dot(activated, w_down, preferred_element_type=jnp.fl...  88.8 us
    all_gather x1, waiting for transfers between devices, body(): shard_piece = lax.all_gather(normed, 'req', axis=0, tiled=True)  81.6 us
    concatenate x8, local copies, waits for them, and re-layouts, absorb_block(): jnp.concatenate([jnp.reshape(owner * tok_rows, (1,)), base_scalars])  31 us
    dot_general x1, matrix products, body(): jnp.dot(activated, w_down, preferred_element_type=jnp.float32)  16.9 us
    unnamed x26, local copies, waits for them, and re-layouts  16.8 us
    dot_general x1, matrix products, body(): gate_proj = jnp.dot(shard_piece, w_gate, preferred_element_type=jnp.float32)  11.3 us
    ppermute x3, starting transfers between devices, body(): ccw_blk = lax.ppermute(ccw_blk, 'kv', ccw_pairs)  9.49 us
  transfers between devices with their start and end apart: 9, of which 4 were waited for; matrix products, arithmetic and copies ran while one was open for 11% of the time, Pallas kernels for 21%

profile of v5, /device:TPU:0, one launch (start us, length us, event | category | flops | bytes accessed | tf_op | source)
XLA Modules:
  0.0 411.8 jit_solution(3540070174188336820)
XLA Ops:
  7.2 0.0 all-gather.2.cloned.1.call-start
  7.3 0.8 broadcast_multiply_fusion
  8.1 0.8 reduce-window.4
  8.9 0.7 select_reduce_fusion
  9.6 0.1 add_bitcast_fusion
  9.7 1.2 copy.37
  10.9 4.5 %copy.40 = bf16[1024,1280]{0,1:T(8,128)(2,1)} copy(bf16[1024,1280]{1,0:T(8,128)(2,1)} %bitcast.57) | data formatting | bytes 5242880 | tf_op jit(solution)/shard_map/reshape | solution.py:150
  15.4 2.0 maximum_bitcast_fusion
  17.5 0.2 fusion.6
  17.7 0.2 convert.21
  17.9 0.7 multiply_cosine_fusion
  18.7 0.4 subtract_convert_fusion
  19.1 0.2 pad_maximum_fusion.1
  19.2 1.9 pad_maximum_fusion.refs_2_.refs_3_
  21.1 3.6 collective-permute-start.1
  24.7 1.4 copy.33
  26.1 0.1 convert.20
  26.2 0.2 multiply_cosine_fusion.1
  26.4 0.2 subtract_convert_fusion.1
  26.5 1.3 copy.35
  27.9 1.4 copy.34
  29.2 3.1 copy.50.refs_4_
  32.3 0.6 fusion.8
  33.0 0.7 fusion.7
  33.6 3.9 concatenate.63.refs_0_
  37.5 2.3 pad_maximum_fusion.2
  39.8 12.5 %shard_map.122.refs_4_ = f32[8,512,128]{2,1,0:T(8,128)S(1)} custom-call(s32[8]{0:T(128)S(1)} %concatenate.63.refs_0_, bf16[8,512,80]{2,1,0:T(8,128)(2,1)S(1)} %bitcast.44, bf16[1280,1152]{1,0:T(8,128)(2,1)} %pad_maximum_fusion.refs_2_.refs_3_, bf16[1280,1152]{1,0:T(8,128)(2,1)} %pad_maximum_fusion.refs_2_.refs_3_, ...), custom_call_target="tpu_custom_call", output_to_operand_aliasing={{}: (4, {})} | custom-call | flops 1509949440 | bytes 7143424 | tf_op jit(solution)/shard_map/pallas_call | solution.py:89
  52.3 1.4 copy-done.2
  53.7 4.0 collective-permute-done.1.refs_2_.refs_3_
  57.7 3.1 collective-permute-done.refs_2_.refs_3_
  60.8 3.0 collective-permute-start.3
  63.8 3.9 concatenate.65.refs_0_
  67.6 3.9 concatenate.64.refs_0_
  71.5 1.6 copy-done.3
  73.1 12.5 %shard_map.123.refs_4_ = f32[8,512,128]{2,1,0:T(8,128)S(1)} custom-call(s32[8]{0:T(128)S(1)} %concatenate.65.refs_0_, bf16[8,512,80]{2,1,0:T(8,128)(2,1)S(1)} %bitcast.45, bf16[1280,1152]{1,0:T(8,128)(2,1)} %collective-permute-done.refs_2_.refs_3_, bf16[1280,1152]{1,0:T(8,128)(2,1)} %collective-permute-done.refs_2_.refs_3_, ...), custom_call_target="tpu_custom_call", output_to_operand_aliasing={{}: (4, {})} | custom-call | flops 1509949440 | bytes 7143424 | tf_op jit(solution)/shard_map/pallas_call | solution.py:89
  85.6 12.5 %shard_map.124.refs_4_ = f32[8,512,128]{2,1,0:T(8,128)S(1)} custom-call(s32[8]{0:T(128)S(1)} %concatenate.64.refs_0_, bf16[8,512,80]{2,1,0:T(8,128)(2,1)S(1)} %bitcast.46, bf16[1280,1152]{1,0:T(8,128)(2,1)} %collective-permute-done.1.refs_2_.refs_3_, bf16[1280,1152]{1,0:T(8,128)(2,1)} %collective-permute-done.1.refs_2_.refs_3_, ...), custom_call_target="tpu_custom_call", output_to_operand_aliasing={{}: (4, {})} | custom-call | flops 1509949440 | bytes 7143424 | tf_op jit(solution)/shard_map/pallas_call | solution.py:89
  98.2 1.4 copy-done.4
  99.6 2.9 collective-permute-start.5
  102.5 3.9 concatenate.67.refs_0_
  106.4 3.9 concatenate.66.refs_0_
  110.3 1.6 copy-done.5
  111.9 12.5 %shard_map.125.refs_4_ = f32[8,512,128]{2,1,0:T(8,128)S(1)} custom-call(s32[8]{0:T(128)S(1)} %concatenate.67.refs_0_, bf16[8,512,80]{2,1,0:T(8,128)(2,1)S(1)} %bitcast.47, bf16[1280,1152]{1,0:T(8,128)(2,1)} %collective-permute-done.2.refs_2_.refs_3_, bf16[1280,1152]{1,0:T(8,128)(2,1)} %collective-permute-done.2.refs_2_.refs_3_, ...), custom_call_target="tpu_custom_call", output_to_operand_aliasing={{}: (4, {})} | custom-call | flops 1509949440 | bytes 7143424 | tf_op jit(solution)/shard_map/pallas_call | solution.py:89
  124.4 12.7 %shard_map.126.refs_4_ = f32[8,512,128]{2,1,0:T(8,128)S(1)} custom-call(s32[8]{0:T(128)S(1)} %concatenate.66.refs_0_, bf16[8,512,80]{2,1,0:T(8,128)(2,1)S(1)} %bitcast.48, bf16[1280,1152]{1,0:T(8,128)(2,1)} %collective-permute-done.3.refs_2_.refs_3_, bf16[1280,1152]{1,0:T(8,128)(2,1)} %collective-permute-done.3.refs_2_.refs_3_, ...), custom_call_target="tpu_custom_call", output_to_operand_aliasing={{}: (4, {})} | custom-call | flops 1509949440 | bytes 7143424 | tf_op jit(solution)/shard_map/pallas_call | solution.py:89
  137.1 1.4 copy-done.6
  138.6 3.9 concatenate.69.refs_0_
  142.5 3.9 concatenate.68.refs_0_
  146.3 3.9 concatenate.56.refs_0_
  150.2 1.6 copy-done.7
  151.8 12.5 %shard_map.127.refs_4_ = f32[8,512,128]{2,1,0:T(8,128)S(1)} custom-call(s32[8]{0:T(128)S(1)} %concatenate.69.refs_0_, bf16[8,512,80]{2,1,0:T(8,128)(2,1)S(1)} %bitcast.49, bf16[1280,1152]{1,0:T(8,128)(2,1)} %collective-permute-done.4.refs_2_.refs_3_, bf16[1280,1152]{1,0:T(8,128)(2,1)} %collective-permute-done.4.refs_2_.refs_3_, ...), custom_call_target="tpu_custom_call", output_to_operand_aliasing={{}: (4, {})} | custom-call | flops 1509949440 | bytes 7143424 | tf_op jit(solution)/shard_map/pallas_call | solution.py:89
  164.3 12.5 %shard_map.128.refs_4_ = f32[8,512,128]{2,1,0:T(8,128)S(1)} custom-call(s32[8]{0:T(128)S(1)} %concatenate.68.refs_0_, bf16[8,512,80]{2,1,0:T(8,128)(2,1)S(1)} %bitcast.50, bf16[1280,1152]{1,0:T(8,128)(2,1)} %collective-permute-done.5.refs_2_.refs_3_, bf16[1280,1152]{1,0:T(8,128)(2,1)} %collective-permute-done.5.refs_2_.refs_3_, ...), custom_call_target="tpu_custom_call", output_to_operand_aliasing={{}: (4, {})} | custom-call | flops 1509949440 | bytes 7143424 | tf_op jit(solution)/shard_map/pallas_call | solution.py:89
  176.9 12.5 %shard_map.129 = f32[8,512,128]{2,1,0:T(8,128)S(1)} custom-call(s32[8]{0:T(128)S(1)} %concatenate.56.refs_0_, bf16[8,512,80]{2,1,0:T(8,128)(2,1)S(1)} %bitcast.51, bf16[1280,1152]{1,0:T(8,128)(2,1)} %collective-permute-done.6.refs_2_.refs_3_, bf16[1280,1152]{1,0:T(8,128)(2,1)} %collective-permute-done.6.refs_2_.refs_3_, ...), custom_call_target="tpu_custom_call", output_to_operand_aliasing={{}: (4, {})} | custom-call | flops 1509949440 | bytes 7143424 | tf_op jit(solution)/shard_map/pallas_call | solution.py:89
  189.4 1.2 slice_reduce_fusion
  190.6 1.5 fusion.2
  192.1 1.5 copy.38
  193.6 6.8 %multiply_reduce_fusion = (f32[128]{0:T(128)S(1)}, f32[128,2560]{1,0:T(8,128)S(1)}) fusion(bf16[128,2560]{0,1:T(8,128)(2,1)S(1)} %bitcast.52, bf16[2560,2560]{1,0:T(8,128)(2,1)} %param.19, bf16[128,2560]{1,0:T(8,128)(2,1)} %param.13), kind=kOutput, calls=%fused_computation.16 | convolution fusion | flops 1679687552 | bytes 15729152 | tf_op jit(solution)/shard_map/dot_general | solution.py:203
  200.4 1.1 copy-done.8
  201.6 1.0 multiply_convert_fusion.1
  202.6 0.0 reduce-scatter.2.cloned.1.call-start
  202.7 81.6 %all-gather.2.cloned.1.call-done = bf16[2048,2560]{1,0:T(8,128)(2,1)} async-done(((bf16[128,2560]{1,0:T(8,128)(2,1)}), bf16[2048,2560]{1,0:T(8,128)(2,1)}) %all-gather.2.cloned.1.call-update) | async-done | bytes 10485776 | tf_op jit(solution)/shard_map/all_gather | solution.py:212
  284.3 11.3 %fusion.9 = f32[2048,448]{0,1:T(8,128)} fusion(bf16[2048,2560]{1,0:T(8,128)(2,1)} %all-gather.2.cloned.1.call-done, bf16[2560,448]{0,1:T(8,128)(2,1)} %param.21), kind=kOutput, calls=%fused_computation.37 | convolution fusion | flops 4697620480 | bytes 16449536 | tf_op jit(solution)/shard_map/dot_general | solution.py:213
  295.7 16.9 %convolution_convert_fusion = bf16[2048,2560]{1,0:T(8,128)(2,1)} fusion(bf16[448,2560]{1,0:T(8,128)(2,1)S(1)} %copy-done, f32[2048,448]{0,1:T(8,128)} %fusion.9, bf16[2048,2560]{1,0:T(8,128)(2,1)} %all-gather.2.cloned.1.call-done, bf16[2560,448]{0,1:T(8,128)(2,1)} %param.22), kind=kOutput, calls=%fused_computation | convolution fusion | flops 9405988864 | bytes 29229056 | tf_op jit(solution)/shard_map/dot_general | solution.py:217
  312.6 1.1 copy.39
  313.6 88.8 %reduce-scatter.2.cloned.1.call-done = bf16[128,2560]{1,0:T(8,128)(2,1)} async-done(((bf16[2048,2560]{1,0:T(8,128)(2,1)}), bf16[128,2560]{1,0:T(8,128)(2,1)}) %reduce-scatter.2.cloned.1.call-update) | async-done | bytes 655376 | tf_op jit(solution)/shard_map/reduce_scatter | solution.py:216
  402.5 2.4 add_convert_fusion.1
  (31 shorter events, 0.1 us)
Async XLA Ops:
  7.2 288.5 %copy-start = (bf16[448,2560]{1,0:T(8,128)(2,1)S(1)}, bf16[448,2560]{1,0:T(8,128)(2,1)}, u32[]{:S(2)}) copy-start(bf16[448,2560]{1,0:T(8,128)(2,1)} %param.23) | copy-start | bytes 6881284
  7.2 277.1 %all-gather.2.cloned.1.call-start = ((), (), s32[]{:S(2)}) async-start(), calls=%async_computation.1 | async-start | bytes 11141120 | tf_op jit(solution)/shard_map/all_gather | solution.py:212
  21.1 36.6 %collective-permute-start.1 = (bf16[1280,1152]{1,0:T(8,128)(2,1)}, bf16[1280,1152]{1,0:T(8,128)(2,1)}, u32[]{:S(2)}, u32[]{:S(2)}) collective-permute-start(bf16[1280,1152]{1,0:T(8,128)(2,1)} %pad_maximum_fusion.refs_2_.refs_3_), channel_id=1, source_target_pairs={{0,7},{1,0},{2,1},{3,2},{4,3},{5,4},{6,5},{7,6},{8,15},{9,8},{10,9... | collective-permute-start | bytes 8847368 | tf_op jit(solution)/shard_map/ppermute | solution.py:193
  24.7 36.1 %collective-permute-start = (bf16[1280,1152]{1,0:T(8,128)(2,1)}, bf16[1280,1152]{1,0:T(8,128)(2,1)}, u32[]{:S(2)}, u32[]{:S(2)}) collective-permute-start(bf16[1280,1152]{1,0:T(8,128)(2,1)} %pad_maximum_fusion.refs_2_.refs_3_), channel_id=1, source_target_pairs={{0,1},{1,2},{2,3},{3,4},{4,5},{5,6},{6,7},{7,0},{8,9},{9,10},{10,1... | collective-permute-start | bytes 8847368 | tf_op jit(solution)/shard_map/ppermute | solution.py:191
  29.2 3.7 copy-start.10
  37.5 2.3 copy-start.1
  52.3 1.4 copy-start.2
  60.8 38.8 %collective-permute-start.2 = (bf16[1280,1152]{1,0:T(8,128)(2,1)}, bf16[1280,1152]{1,0:T(8,128)(2,1)}, u32[]{:S(2)}, u32[]{:S(2)}) collective-permute-start(bf16[1280,1152]{1,0:T(8,128)(2,1)} %collective-permute-done.refs_2_.refs_3_), channel_id=1, source_target_pairs={{0,1},{1,2},{2,3},{3,4},{4,5},{5,6},{6,7},{7,0},{8,9},{9,10},{10,1... | collective-permute-start | bytes 8847368 | tf_op jit(solution)/shard_map/ppermute | solution.py:191
  60.8 38.8 %collective-permute-start.3 = (bf16[1280,1152]{1,0:T(8,128)(2,1)}, bf16[1280,1152]{1,0:T(8,128)(2,1)}, u32[]{:S(2)}, u32[]{:S(2)}) collective-permute-start(bf16[1280,1152]{1,0:T(8,128)(2,1)} %collective-permute-done.1.refs_2_.refs_3_), channel_id=1, source_target_pairs={{0,7},{1,0},{2,1},{3,2},{4,3},{5,4},{6,5},{7,6},{8,15},{9,8},{10,9... | collective-permute-start | bytes 8847368 | tf_op jit(solution)/shard_map/ppermute | solution.py:193
  71.5 1.6 copy-start.3
  98.2 1.4 copy-start.4
  99.6 38.9 %collective-permute-start.4 = (bf16[1280,1152]{1,0:T(8,128)(2,1)}, bf16[1280,1152]{1,0:T(8,128)(2,1)}, u32[]{:S(2)}, u32[]{:S(2)}) collective-permute-start(bf16[1280,1152]{1,0:T(8,128)(2,1)} %collective-permute-done.2.refs_2_.refs_3_), channel_id=1, source_target_pairs={{0,1},{1,2},{2,3},{3,4},{4,5},{5,6},{6,7},{7,0},{8,9},{9,10},{10,1... | collective-permute-start | bytes 8847368 | tf_op jit(solution)/shard_map/ppermute | solution.py:191
  99.6 38.9 %collective-permute-start.5 = (bf16[1280,1152]{1,0:T(8,128)(2,1)}, bf16[1280,1152]{1,0:T(8,128)(2,1)}, u32[]{:S(2)}, u32[]{:S(2)}) collective-permute-start(bf16[1280,1152]{1,0:T(8,128)(2,1)} %collective-permute-done.3.refs_2_.refs_3_), channel_id=1, source_target_pairs={{0,7},{1,0},{2,1},{3,2},{4,3},{5,4},{6,5},{7,6},{8,15},{9,8},{10,9... | collective-permute-start | bytes 8847368 | tf_op jit(solution)/shard_map/ppermute | solution.py:193
  110.3 1.6 copy-start.5
  137.1 1.4 copy-start.6
  138.5 38.3 %collective-permute-start.6 = (bf16[1280,1152]{1,0:T(8,128)(2,1)}, bf16[1280,1152]{1,0:T(8,128)(2,1)}, u32[]{:S(2)}, u32[]{:S(2)}) collective-permute-start(bf16[1280,1152]{1,0:T(8,128)(2,1)} %collective-permute-done.4.refs_2_.refs_3_), channel_id=1, source_target_pairs={{0,1},{1,2},{2,3},{3,4},{4,5},{5,6},{6,7},{7,0},{8,9},{9,10},{10,1... | collective-permute-start | bytes 8847368 | tf_op jit(solution)/shard_map/ppermute | solution.py:191
  150.2 1.6 copy-start.7
  193.6 8.0 %copy-start.9 = (f32[2560]{0:T(1024)S(1)}, f32[2560]{0:T(1024)}, u32[]{:S(2)}) copy-start(f32[2560]{0:T(1024)} %param.20) | copy-start | bytes 30724
  200.4 1.2 copy-start.8
  202.6 199.9 %reduce-scatter.2.cloned.1.call-start = ((), (), s32[]{:S(2)}) async-start(), calls=%async_computation.2 | async-start | bytes 11141120 | tf_op jit(solution)/shard_map/reduce_scatter | solution.py:216
Sparse Core Ops, SparseCore 0:
  202.8 81.5 all-gather.1
  312.7 89.7 reduce-scatter.1

commit v6 on v5

--- a/solution.py
+++ b/solution.py
@@ -40,7 +40,7 @@
     return (request_of, request_start)
 
 
-def attn_kernel(sc_ref, q_ref, k_ref, v_ref, st_in, st_ref, *, pre_len):
+def attn_kernel(off_ref, sc_ref, q_ref, k_ref, v_ref, st_in, st_ref, *, pre_len):
     rows = q_ref.shape[0]
     suf_len = k_ref.shape[1] - pre_len
     scale = HD ** (-0.5)
@@ -53,11 +53,11 @@
     m = st[:, HD + 1:HD + 2]
     s_pre = jnp.dot(q, kt[:, :pre_len], preferred_element_type=jnp.float32) * scale
     s_suf = jnp.dot(q, kt[:, pre_len:], preferred_element_type=jnp.float32) * scale
-    qi = sc_ref[1] + lax.broadcasted_iota(jnp.int32, (rows, 1), 0) % suf_len
+    qi = sc_ref[0] + lax.broadcasted_iota(jnp.int32, (rows, 1), 0) % suf_len
     qs = jnp.zeros((rows, 1), jnp.int32)
     for j in range(3):
-        qs = qs + jnp.where(qi >= sc_ref[2 + 2 * j], sc_ref[3 + 2 * j], 0)
-    kidx = sc_ref[0] + lax.broadcasted_iota(jnp.int32, (rows, suf_len), 1)
+        qs = qs + jnp.where(qi >= sc_ref[1 + 2 * j], sc_ref[2 + 2 * j], 0)
+    kidx = off_ref[0] + lax.broadcasted_iota(jnp.int32, (rows, suf_len), 1)
     mask = (kidx >= qs) & (kidx <= qi)
     s_suf = jnp.where(mask, s_suf, NEG)
     m_new = jnp.maximum(
@@ -81,7 +81,7 @@
     st_ref[:, HD + 1:HD + 2] = m_new
 
 
-def attention_block(q_heads, kv_blk, scalars, state, pre_len):
+def attention_block(q_heads, kv_blk, offset, scalars, state, pre_len):
     heads, rows, _ = q_heads.shape
     width = kv_blk.shape[1]
     kernel = lambda *refs: attn_kernel(*refs, pre_len=pre_len)
@@ -91,6 +91,7 @@
         grid=(heads,),
         in_specs=[
             pl.BlockSpec(memory_space=pltpu.SMEM),
+            pl.BlockSpec(memory_space=pltpu.SMEM),
             pl.BlockSpec((None, rows, HD), lambda h: (h, 0, 0)),
             pl.BlockSpec((HD, width), lambda h: (h, 0)),
             pl.BlockSpec((HD, width), lambda h: (heads + h, 0)),
@@ -98,7 +99,7 @@
         ],
         out_specs=st_spec,
         out_shape=jax.ShapeDtypeStruct(state.shape, jnp.float32),
-        input_output_aliases={4: 0},
+        input_output_aliases={5: 0},
         cost_estimate=pl.CostEstimate(
             flops=4 * heads * rows * width * HD,
             transcendentals=heads * rows * width,
@@ -107,7 +108,7 @@
         compiler_params=pltpu.CompilerParams(
             dimension_semantics=("arbitrary",), vmem_limit_bytes=48 * 1024 * 1024
         ),
-    )(scalars, q_heads, kv_blk, kv_blk, state)
+    )(offset, scalars, q_heads, kv_blk, kv_blk, state)
 
 
 def body(
@@ -175,8 +176,8 @@
     me = lax.axis_index("kv")
 
     def absorb_block(state, blk, owner):
-        scalars = jnp.concatenate([jnp.reshape(owner * tok_rows, (1,)), base_scalars])
-        return attention_block(q_heads, blk, scalars.astype(jnp.int32), state, pre_len)
+        offset = jnp.reshape(owner * tok_rows, (1,)).astype(jnp.int32)
+        return attention_block(q_heads, blk, offset, base_scalars, state, pre_len)
 
     cw_pairs = [(i, (i + 1) % n_kv) for i in range(n_kv)]
     ccw_pairs = [(i, (i - 1) % n_kv) for i in range(n_kv)]

time: 413 us -> 402 us (0.973)
  local copies, waits for them, and re-layouts: 59.3 us -> 32.2 us
  waiting for transfers between devices: 178 us -> 194 us
    concatenate x8 -> x0, local copies, waits for them, and re-layouts: 31 us -> none  [absorb_block(): jnp.concatenate([jnp.reshape(owner * tok_rows, (1,)), base_scalars])]
    ppermute x4, waiting for transfers between devices: 3.12 us -> 22.5 us  [body(): cw_blk = lax.ppermute(cw_blk, 'kv', cw_pairs)]
  transfers between devices with their start and end apart: 9 -> 9, of which waited for: 4 -> 7; matrix products, arithmetic and copies ran while one was open for 11% -> 4% of each run, Pallas kernels for 21% -> 22%
where the time goes in v6:
time: 402 us
  waiting for transfers between devices  194 us (48%)
  Pallas kernels  101 us (25%)
  matrix products  35 us (9%)
  local copies, waits for them, and re-layouts  32.2 us (8%)
  other arithmetic  15.5 us (4%)
  between operations  14.3 us (4%)
  starting transfers between devices  9.59 us (2%)
    pallas_call x8, Pallas kernels, attention_block(): pl.pallas_call(kernel, grid=(heads,), in_specs=[pl.BlockSpec(memory_space...  101 us
    reduce_scatter x1, waiting for transfers between devices, body(): lax.psum_scatter(jnp.dot(activated, w_down, preferred_element_type=jnp.fl...  88.7 us
    all_gather x1, waiting for transfers between devices, body(): shard_piece = lax.all_gather(normed, 'req', axis=0, tiled=True)  79.3 us
    ppermute x4, waiting for transfers between devices, body(): cw_blk = lax.ppermute(cw_blk, 'kv', cw_pairs)  22.5 us
    dot_general x1, matrix products, body(): jnp.dot(activated, w_down, preferred_element_type=jnp.float32)  16.9 us
    unnamed x26, local copies, waits for them, and re-layouts  16.8 us
    dot_general x1, matrix products, body(): gate_proj = jnp.dot(shard_piece, w_gate, preferred_element_type=jnp.float32)  11.3 us
    ppermute x3, starting transfers between devices, body(): ccw_blk = lax.ppermute(ccw_blk, 'kv', ccw_pairs)  9.5 us
  transfers between devices with their start and end apart: 9, of which 7 were waited for; matrix products, arithmetic and copies ran while one was open for 4% of the time, Pallas kernels for 22%

profile of v6, /device:TPU:0, one launch (start us, length us, event | category | flops | bytes accessed | tf_op | source)
XLA Modules:
  0.0 401.6 jit_solution(8123482914518264499)
XLA Ops:
  7.2 0.0 copy-start
  7.2 0.0 all-gather.2.cloned.1.call-start
  7.3 0.8 broadcast_multiply_fusion
  8.1 0.8 reduce-window.4
  8.9 0.7 select_reduce_fusion
  9.6 0.1 add_bitcast_fusion
  9.7 1.2 copy.37
  10.9 4.5 %copy.40 = bf16[1024,1280]{0,1:T(8,128)(2,1)} copy(bf16[1024,1280]{1,0:T(8,128)(2,1)} %bitcast.57) | data formatting | bytes 5242880 | tf_op jit(solution)/shard_map/reshape | solution.py:151
  15.4 2.0 maximum_bitcast_fusion
  17.5 0.2 fusion.6
  17.7 0.2 convert.21
  17.9 0.7 multiply_cosine_fusion
  18.7 0.4 subtract_convert_fusion
  19.1 0.1 pad_maximum_fusion.1
  19.2 1.9 pad_maximum_fusion.refs_3_.refs_4_
  21.1 3.6 collective-permute-start.1
  24.7 1.4 copy.33
  26.1 0.1 convert.20
  26.2 0.2 multiply_cosine_fusion.1
  26.4 0.2 subtract_convert_fusion.1
  26.5 1.3 copy.35
  27.9 1.4 copy.34
  29.2 3.1 copy.50.refs_5_
  32.3 0.7 fusion.8
  33.0 0.6 fusion.7
  33.6 3.9 stack.9.refs_1_
  37.6 2.3 pad_maximum_fusion.2
  39.8 12.6 %shard_map.122.refs_5_ = f32[8,512,128]{2,1,0:T(8,128)S(1)} custom-call(s32[1]{0:T(128)} %bitcast.22.refs_0_, s32[7]{0:T(128)S(1)} %stack.9.refs_1_, bf16[8,512,80]{2,1,0:T(8,128)(2,1)S(1)} %bitcast.44, bf16[1280,1152]{1,0:T(8,128)(2,1)} %pad_maximum_fusion.refs_3_.refs_4_, ...), custom_call_target="tpu_custom_call", output_to_operand_aliasing={{}: (5, {})} | custom-call | flops 1509949440 | bytes 7143424 | tf_op jit(solution)/shard_map/pallas_call | solution.py:89
  52.5 1.4 copy-done.2
  53.8 3.8 collective-permute-done.1.refs_3_.refs_4_
  57.7 3.1 collective-permute-done.refs_3_.refs_4_
  60.8 3.0 collective-permute-start.3
  63.8 1.6 copy-done.3
  65.4 12.6 %shard_map.123.refs_5_ = f32[8,512,128]{2,1,0:T(8,128)S(1)} custom-call(s32[1]{0:T(128)} %bitcast.25.refs_0_, s32[7]{0:T(128)S(1)} %stack.9.refs_1_, bf16[8,512,80]{2,1,0:T(8,128)(2,1)S(1)} %bitcast.45, bf16[1280,1152]{1,0:T(8,128)(2,1)} %collective-permute-done.refs_3_.refs_4_, ...), custom_call_target="tpu_custom_call", output_to_operand_aliasing={{}: (5, {})} | custom-call | flops 1509949440 | bytes 7143424 | tf_op jit(solution)/shard_map/pallas_call | solution.py:89
  77.9 12.6 %shard_map.124.refs_5_ = f32[8,512,128]{2,1,0:T(8,128)S(1)} custom-call(s32[1]{0:T(128)} %bitcast.24.refs_0_, s32[7]{0:T(128)S(1)} %stack.9.refs_1_, bf16[8,512,80]{2,1,0:T(8,128)(2,1)S(1)} %bitcast.46, bf16[1280,1152]{1,0:T(8,128)(2,1)} %collective-permute-done.1.refs_3_.refs_4_, ...), custom_call_target="tpu_custom_call", output_to_operand_aliasing={{}: (5, {})} | custom-call | flops 1509949440 | bytes 7143424 | tf_op jit(solution)/shard_map/pallas_call | solution.py:89
  90.5 1.4 copy-done.4
  91.9 5.0 %collective-permute-done.2.refs_3_.refs_4_ = bf16[1280,1152]{1,0:T(8,128)(2,1)} collective-permute-done((bf16[1280,1152]{1,0:T(8,128)(2,1)}, bf16[1280,1152]{1,0:T(8,128)(2,1)}, u32[]{:S(2)}, u32[]{:S(2)}) %collective-permute-start.2) | collective-permute-done | bytes 2949152 | tf_op jit(solution)/shard_map/ppermute | solution.py:192
  96.9 3.0 collective-permute-start.5
  99.9 1.6 copy-done.5
  101.5 12.6 %shard_map.125.refs_5_ = f32[8,512,128]{2,1,0:T(8,128)S(1)} custom-call(s32[1]{0:T(128)} %bitcast.27.refs_0_, s32[7]{0:T(128)S(1)} %stack.9.refs_1_, bf16[8,512,80]{2,1,0:T(8,128)(2,1)S(1)} %bitcast.47, bf16[1280,1152]{1,0:T(8,128)(2,1)} %collective-permute-done.2.refs_3_.refs_4_, ...), custom_call_target="tpu_custom_call", output_to_operand_aliasing={{}: (5, {})} | custom-call | flops 1509949440 | bytes 7143424 | tf_op jit(solution)/shard_map/pallas_call | solution.py:89
  114.0 12.6 %shard_map.126.refs_5_ = f32[8,512,128]{2,1,0:T(8,128)S(1)} custom-call(s32[1]{0:T(128)} %bitcast.26.refs_0_, s32[7]{0:T(128)S(1)} %stack.9.refs_1_, bf16[8,512,80]{2,1,0:T(8,128)(2,1)S(1)} %bitcast.48, bf16[1280,1152]{1,0:T(8,128)(2,1)} %collective-permute-done.3.refs_3_.refs_4_, ...), custom_call_target="tpu_custom_call", output_to_operand_aliasing={{}: (5, {})} | custom-call | flops 1509949440 | bytes 7143424 | tf_op jit(solution)/shard_map/pallas_call | solution.py:89
  126.7 1.4 copy-done.6
  128.0 5.0 %collective-permute-done.4.refs_3_.refs_4_ = bf16[1280,1152]{1,0:T(8,128)(2,1)} collective-permute-done((bf16[1280,1152]{1,0:T(8,128)(2,1)}, bf16[1280,1152]{1,0:T(8,128)(2,1)}, u32[]{:S(2)}, u32[]{:S(2)}) %collective-permute-start.4) | collective-permute-done | bytes 2949152 | tf_op jit(solution)/shard_map/ppermute | solution.py:192
  133.1 1.6 copy-done.7
  134.6 12.6 %shard_map.127.refs_5_ = f32[8,512,128]{2,1,0:T(8,128)S(1)} custom-call(s32[1]{0:T(128)} %bitcast.29.refs_0_, s32[7]{0:T(128)S(1)} %stack.9.refs_1_, bf16[8,512,80]{2,1,0:T(8,128)(2,1)S(1)} %bitcast.49, bf16[1280,1152]{1,0:T(8,128)(2,1)} %collective-permute-done.4.refs_3_.refs_4_, ...), custom_call_target="tpu_custom_call", output_to_operand_aliasing={{}: (5, {})} | custom-call | flops 1509949440 | bytes 7143424 | tf_op jit(solution)/shard_map/pallas_call | solution.py:89
  147.2 12.6 %shard_map.128.refs_5_ = f32[8,512,128]{2,1,0:T(8,128)S(1)} custom-call(s32[1]{0:T(128)} %bitcast.28.refs_0_, s32[7]{0:T(128)S(1)} %stack.9.refs_1_, bf16[8,512,80]{2,1,0:T(8,128)(2,1)S(1)} %bitcast.50, bf16[1280,1152]{1,0:T(8,128)(2,1)} %collective-permute-done.5.refs_3_.refs_4_, ...), custom_call_target="tpu_custom_call", output_to_operand_aliasing={{}: (5, {})} | custom-call | flops 1509949440 | bytes 7143424 | tf_op jit(solution)/shard_map/pallas_call | solution.py:89
  159.8 9.3 %collective-permute-done.6.refs_3_.refs_4_ = bf16[1280,1152]{1,0:T(8,128)(2,1)} collective-permute-done((bf16[1280,1152]{1,0:T(8,128)(2,1)}, bf16[1280,1152]{1,0:T(8,128)(2,1)}, u32[]{:S(2)}, u32[]{:S(2)}) %collective-permute-start.6) | collective-permute-done | bytes 2949152 | tf_op jit(solution)/shard_map/ppermute | solution.py:192
  169.2 12.6 %shard_map.129 = f32[8,512,128]{2,1,0:T(8,128)S(1)} custom-call(s32[1]{0:T(128)} %bitcast.refs_0_, s32[7]{0:T(128)S(1)} %stack.9.refs_1_, bf16[8,512,80]{2,1,0:T(8,128)(2,1)S(1)} %bitcast.51, bf16[1280,1152]{1,0:T(8,128)(2,1)} %collective-permute-done.6.refs_3_.refs_4_, ...), custom_call_target="tpu_custom_call", output_to_operand_aliasing={{}: (5, {})} | custom-call | flops 1509949440 | bytes 7143424 | tf_op jit(solution)/shard_map/pallas_call | solution.py:89
  181.7 1.2 slice_reduce_fusion
  182.9 1.5 fusion.2
  184.4 1.5 copy.38
  185.9 0.0 copy-start.9
  186.0 6.8 %multiply_reduce_fusion = (f32[128]{0:T(128)S(1)}, f32[128,2560]{1,0:T(8,128)S(1)}) fusion(bf16[128,2560]{0,1:T(8,128)(2,1)S(1)} %bitcast.52, bf16[2560,2560]{1,0:T(8,128)(2,1)} %param.19, bf16[128,2560]{1,0:T(8,128)(2,1)} %param.13), kind=kOutput, calls=%fused_computation.16 | convolution fusion | flops 1679687552 | bytes 15729152 | tf_op jit(solution)/shard_map/dot_general | solution.py:204
  192.8 1.1 copy-done.8
  193.9 1.0 multiply_convert_fusion.1
  194.9 0.0 all-gather.2.cloned.1.call-update
  195.0 0.0 reduce-scatter.2.cloned.1.call-start
  195.0 79.3 %all-gather.2.cloned.1.call-done = bf16[2048,2560]{1,0:T(8,128)(2,1)} async-done(((bf16[128,2560]{1,0:T(8,128)(2,1)}), bf16[2048,2560]{1,0:T(8,128)(2,1)}) %all-gather.2.cloned.1.call-update) | async-done | bytes 10485776 | tf_op jit(solution)/shard_map/all_gather | solution.py:213
  274.3 11.3 %fusion.9 = f32[2048,448]{0,1:T(8,128)} fusion(bf16[2048,2560]{1,0:T(8,128)(2,1)} %all-gather.2.cloned.1.call-done, bf16[2560,448]{0,1:T(8,128)(2,1)} %param.21), kind=kOutput, calls=%fused_computation.37 | convolution fusion | flops 4697620480 | bytes 16449536 | tf_op jit(solution)/shard_map/dot_general | solution.py:214
  285.6 16.9 %convolution_convert_fusion = bf16[2048,2560]{1,0:T(8,128)(2,1)} fusion(bf16[448,2560]{1,0:T(8,128)(2,1)S(1)} %copy-done, f32[2048,448]{0,1:T(8,128)} %fusion.9, bf16[2048,2560]{1,0:T(8,128)(2,1)} %all-gather.2.cloned.1.call-done, bf16[2560,448]{0,1:T(8,128)(2,1)} %param.22), kind=kOutput, calls=%fused_computation | convolution fusion | flops 9405988864 | bytes 29229056 | tf_op jit(solution)/shard_map/dot_general | solution.py:218
  302.5 0.0 reduce-scatter.2.cloned.1.call-update
  302.5 1.1 copy.39
  303.6 88.7 %reduce-scatter.2.cloned.1.call-done = bf16[128,2560]{1,0:T(8,128)(2,1)} async-done(((bf16[2048,2560]{1,0:T(8,128)(2,1)}), bf16[128,2560]{1,0:T(8,128)(2,1)}) %reduce-scatter.2.cloned.1.call-update) | async-done | bytes 655376 | tf_op jit(solution)/shard_map/reduce_scatter | solution.py:217
  392.3 2.4 add_convert_fusion.1
  (24 shorter events, 0.1 us)
Async XLA Ops:
  7.2 278.5 %copy-start = (bf16[448,2560]{1,0:T(8,128)(2,1)S(1)}, bf16[448,2560]{1,0:T(8,128)(2,1)}, u32[]{:S(2)}) copy-start(bf16[448,2560]{1,0:T(8,128)(2,1)} %param.23) | copy-start | bytes 6881284
  7.2 267.1 %all-gather.2.cloned.1.call-start = ((), (), s32[]{:S(2)}) async-start(), calls=%async_computation.1 | async-start | bytes 11141120 | tf_op jit(solution)/shard_map/all_gather | solution.py:213
  21.1 36.6 %collective-permute-start.1 = (bf16[1280,1152]{1,0:T(8,128)(2,1)}, bf16[1280,1152]{1,0:T(8,128)(2,1)}, u32[]{:S(2)}, u32[]{:S(2)}) collective-permute-start(bf16[1280,1152]{1,0:T(8,128)(2,1)} %pad_maximum_fusion.refs_3_.refs_4_), channel_id=1, source_target_pairs={{0,7},{1,0},{2,1},{3,2},{4,3},{5,4},{6,5},{7,6},{8,15},{9,8},{10,9... | collective-permute-start | bytes 8847368 | tf_op jit(solution)/shard_map/ppermute | solution.py:194
  24.7 36.1 %collective-permute-start = (bf16[1280,1152]{1,0:T(8,128)(2,1)}, bf16[1280,1152]{1,0:T(8,128)(2,1)}, u32[]{:S(2)}, u32[]{:S(2)}) collective-permute-start(bf16[1280,1152]{1,0:T(8,128)(2,1)} %pad_maximum_fusion.refs_3_.refs_4_), channel_id=1, source_target_pairs={{0,1},{1,2},{2,3},{3,4},{4,5},{5,6},{6,7},{7,0},{8,9},{9,10},{10,1... | collective-permute-start | bytes 8847368 | tf_op jit(solution)/shard_map/ppermute | solution.py:192
  29.2 3.7 copy-start.10
  37.6 2.3 copy-start.1
  52.4 1.4 copy-start.2
  60.8 36.1 %collective-permute-start.2 = (bf16[1280,1152]{1,0:T(8,128)(2,1)}, bf16[1280,1152]{1,0:T(8,128)(2,1)}, u32[]{:S(2)}, u32[]{:S(2)}) collective-permute-start(bf16[1280,1152]{1,0:T(8,128)(2,1)} %collective-permute-done.refs_3_.refs_4_), channel_id=1, source_target_pairs={{0,1},{1,2},{2,3},{3,4},{4,5},{5,6},{6,7},{7,0},{8,9},{9,10},{10,1... | collective-permute-start | bytes 8847368 | tf_op jit(solution)/shard_map/ppermute | solution.py:192
  60.8 36.1 %collective-permute-start.3 = (bf16[1280,1152]{1,0:T(8,128)(2,1)}, bf16[1280,1152]{1,0:T(8,128)(2,1)}, u32[]{:S(2)}, u32[]{:S(2)}) collective-permute-start(bf16[1280,1152]{1,0:T(8,128)(2,1)} %collective-permute-done.1.refs_3_.refs_4_), channel_id=1, source_target_pairs={{0,7},{1,0},{2,1},{3,2},{4,3},{5,4},{6,5},{7,6},{8,15},{9,8},{10,9... | collective-permute-start | bytes 8847368 | tf_op jit(solution)/shard_map/ppermute | solution.py:194
  63.8 1.6 copy-start.3
  90.5 1.4 copy-start.4
  96.9 36.1 %collective-permute-start.4 = (bf16[1280,1152]{1,0:T(8,128)(2,1)}, bf16[1280,1152]{1,0:T(8,128)(2,1)}, u32[]{:S(2)}, u32[]{:S(2)}) collective-permute-start(bf16[1280,1152]{1,0:T(8,128)(2,1)} %collective-permute-done.2.refs_3_.refs_4_), channel_id=1, source_target_pairs={{0,1},{1,2},{2,3},{3,4},{4,5},{5,6},{6,7},{7,0},{8,9},{9,10},{10,1... | collective-permute-start | bytes 8847368 | tf_op jit(solution)/shard_map/ppermute | solution.py:192
  96.9 36.1 %collective-permute-start.5 = (bf16[1280,1152]{1,0:T(8,128)(2,1)}, bf16[1280,1152]{1,0:T(8,128)(2,1)}, u32[]{:S(2)}, u32[]{:S(2)}) collective-permute-start(bf16[1280,1152]{1,0:T(8,128)(2,1)} %collective-permute-done.3.refs_3_.refs_4_), channel_id=1, source_target_pairs={{0,7},{1,0},{2,1},{3,2},{4,3},{5,4},{6,5},{7,6},{8,15},{9,8},{10,9... | collective-permute-start | bytes 8847368 | tf_op jit(solution)/shard_map/ppermute | solution.py:194
  99.9 1.6 copy-start.5
  126.6 1.4 copy-start.6
  133.0 36.1 %collective-permute-start.6 = (bf16[1280,1152]{1,0:T(8,128)(2,1)}, bf16[1280,1152]{1,0:T(8,128)(2,1)}, u32[]{:S(2)}, u32[]{:S(2)}) collective-permute-start(bf16[1280,1152]{1,0:T(8,128)(2,1)} %collective-permute-done.4.refs_3_.refs_4_), channel_id=1, source_target_pairs={{0,1},{1,2},{2,3},{3,4},{4,5},{5,6},{6,7},{7,0},{8,9},{9,10},{10,1... | collective-permute-start | bytes 8847368 | tf_op jit(solution)/shard_map/ppermute | solution.py:192
  133.0 1.6 copy-start.7
  185.9 8.0 %copy-start.9 = (f32[2560]{0:T(1024)S(1)}, f32[2560]{0:T(1024)}, u32[]{:S(2)}) copy-start(f32[2560]{0:T(1024)} %param.20) | copy-start | bytes 30724
  192.8 1.2 copy-start.8
  195.0 197.3 %reduce-scatter.2.cloned.1.call-start = ((), (), s32[]{:S(2)}) async-start(), calls=%async_computation.2 | async-start | bytes 11141120 | tf_op jit(solution)/shard_map/reduce_scatter | solution.py:217
Sparse Core Ops, SparseCore 0:
  195.1 79.1 all-gather.1
  302.6 89.6 reduce-scatter.1

commit v7 on v6

--- a/solution.py
+++ b/solution.py
@@ -189,7 +189,13 @@
         if step > 1:
             (cw_blk, ccw_blk), unused = lax.optimization_barrier(((cw_blk, ccw_blk), prev_state))
         prev_state = state
-        cw_blk = lax.ppermute(cw_blk, "kv", cw_pairs)
+        if step == n_kv - step:
+            split = 4 * 128
+            cw_part = lax.ppermute(cw_blk[:, :split], "kv", cw_pairs)
+            ccw_part = lax.ppermute(ccw_blk[:, split:], "kv", ccw_pairs)
+            cw_blk = jnp.concatenate([cw_part, ccw_part], axis=1)
+        else:
+            cw_blk = lax.ppermute(cw_blk, "kv", cw_pairs)
         if step < n_kv - step:
             ccw_blk = lax.ppermute(ccw_blk, "kv", ccw_pairs)
         state = absorb_block(state, cw_blk, (me - step) % n_kv)

time: 402 us -> 406 us (level)
  waiting for transfers between devices: 194 us -> 188 us
    ppermute x4 -> x3, waiting for transfers between devices: 22.5 us -> 13.8 us  [body(): cw_blk = lax.ppermute(cw_blk, 'kv', cw_pairs)]
    slice x0 -> x2, local copies, waits for them, and re-layouts: none -> 5.19 us  [the longest x1 2.74 us: body(): ccw_part = lax.ppermute(ccw_blk[:, split:], 'kv', ccw_pairs)]
  transfers between devices with their start and end apart: 9 -> 10, of which waited for: 7 -> 6; matrix products, arithmetic and copies ran while one was open for 4% -> 5% of each run, Pallas kernels for 22% -> 22%
where the time goes in v7:
time: 406 us; the launch traced here: 405 us
  waiting for transfers between devices  188 us (46%)
  Pallas kernels  101 us (25%)
  local copies, waits for them, and re-layouts  36 us (9%)
  matrix products  35 us (9%)
  other arithmetic  17.6 us (4%)
  between operations  14.3 us (4%)
  starting transfers between devices  12.5 us (3%)
    pallas_call x8, Pallas kernels, attention_block(): pl.pallas_call(kernel, grid=(heads,), in_specs=[pl.BlockSpec(memory_space...  101 us
    reduce_scatter x1, waiting for transfers between devices, body(): lax.psum_scatter(jnp.dot(activated, w_down, preferred_element_type=jnp.fl...  88.9 us
    all_gather x1, waiting for transfers between devices, body(): shard_piece = lax.all_gather(normed, 'req', axis=0, tiled=True)  81.7 us
    dot_general x1, matrix products, body(): jnp.dot(activated, w_down, preferred_element_type=jnp.float32)  16.9 us
    unnamed x26, local copies, waits for them, and re-layouts  15.5 us
    ppermute x3, waiting for transfers between devices, body(): cw_blk = lax.ppermute(cw_blk, 'kv', cw_pairs)  13.8 us
    dot_general x1, matrix products, body(): gate_proj = jnp.dot(shard_piece, w_gate, preferred_element_type=jnp.float32)  11.3 us
    ppermute x3, starting transfers between devices, body(): ccw_blk = lax.ppermute(ccw_blk, 'kv', ccw_pairs)  9.5 us
  transfers between devices with their start and end apart: 10, of which 6 were waited for; matrix products, arithmetic and copies ran while one was open for 5% of the time, Pallas kernels for 22%

profile of v7, /device:TPU:0, one launch (start us, length us, event | category | flops | bytes accessed | tf_op | source)
XLA Modules:
  0.0 405.0 jit_solution(931477939092329481)
XLA Ops:
  7.2 0.0 all-gather.2.cloned.1.call-start
  7.3 0.8 broadcast_multiply_fusion
  8.1 0.8 reduce-window.4
  8.9 0.7 select_reduce_fusion
  9.6 0.1 add_bitcast_fusion
  9.7 1.2 copy.37
  10.9 4.5 %copy.40 = bf16[1024,1280]{0,1:T(8,128)(2,1)} copy(bf16[1024,1280]{1,0:T(8,128)(2,1)} %bitcast.57) | data formatting | bytes 5242880 | tf_op jit(solution)/shard_map/reshape | solution.py:151
  15.4 2.0 maximum_bitcast_fusion
  17.5 0.2 fusion.6
  17.7 0.2 convert.21
  17.9 0.7 multiply_cosine_fusion
  18.7 0.4 subtract_convert_fusion
  19.1 0.1 pad_maximum_fusion.2
  19.2 1.9 pad_maximum_fusion.refs_3_.refs_4_
  21.1 3.6 collective-permute-start.1
  24.7 1.4 copy.33
  26.1 0.1 convert.20
  26.2 0.2 multiply_cosine_fusion.1
  26.4 0.2 subtract_convert_fusion.1
  26.6 1.3 copy.35
  27.9 1.4 copy.34
  29.3 3.1 copy.50.refs_5_
  32.3 0.6 fusion.8
  33.0 0.6 fusion.7
  33.6 3.9 stack.9.refs_1_
  37.5 2.3 pad_maximum_fusion.3
  39.8 12.7 %shard_map.122.refs_5_ = f32[8,512,128]{2,1,0:T(8,128)S(1)} custom-call(s32[1]{0:T(128)} %bitcast.22.refs_0_, s32[7]{0:T(128)S(1)} %stack.9.refs_1_, bf16[8,512,80]{2,1,0:T(8,128)(2,1)S(1)} %bitcast.44, bf16[1280,1152]{1,0:T(8,128)(2,1)} %pad_maximum_fusion.refs_3_.refs_4_, ...), custom_call_target="tpu_custom_call", output_to_operand_aliasing={{}: (5, {})} | custom-call | flops 1509949440 | bytes 7143424 | tf_op jit(solution)/shard_map/pallas_call | solution.py:89
  52.5 1.4 copy-done.2
  53.9 3.8 collective-permute-done.1.refs_3_.refs_4_
  57.7 3.1 collective-permute-done.refs_3_.refs_4_
  60.8 3.0 collective-permute-start.3
  63.8 1.6 copy-done.3
  65.4 12.7 %shard_map.123.refs_5_ = f32[8,512,128]{2,1,0:T(8,128)S(1)} custom-call(s32[1]{0:T(128)} %bitcast.25.refs_0_, s32[7]{0:T(128)S(1)} %stack.9.refs_1_, bf16[8,512,80]{2,1,0:T(8,128)(2,1)S(1)} %bitcast.45, bf16[1280,1152]{1,0:T(8,128)(2,1)} %collective-permute-done.refs_3_.refs_4_, ...), custom_call_target="tpu_custom_call", output_to_operand_aliasing={{}: (5, {})} | custom-call | flops 1509949440 | bytes 7143424 | tf_op jit(solution)/shard_map/pallas_call | solution.py:89
  78.1 12.7 %shard_map.124.refs_5_ = f32[8,512,128]{2,1,0:T(8,128)S(1)} custom-call(s32[1]{0:T(128)} %bitcast.24.refs_0_, s32[7]{0:T(128)S(1)} %stack.9.refs_1_, bf16[8,512,80]{2,1,0:T(8,128)(2,1)S(1)} %bitcast.46, bf16[1280,1152]{1,0:T(8,128)(2,1)} %collective-permute-done.1.refs_3_.refs_4_, ...), custom_call_target="tpu_custom_call", output_to_operand_aliasing={{}: (5, {})} | custom-call | flops 1509949440 | bytes 7143424 | tf_op jit(solution)/shard_map/pallas_call | solution.py:89
  90.8 1.4 copy-done.4
  92.2 4.7 %collective-permute-done.2.refs_3_.refs_4_ = bf16[1280,1152]{1,0:T(8,128)(2,1)} collective-permute-done((bf16[1280,1152]{1,0:T(8,128)(2,1)}, bf16[1280,1152]{1,0:T(8,128)(2,1)}, u32[]{:S(2)}, u32[]{:S(2)}) %collective-permute-start.2) | collective-permute-done | bytes 2949152 | tf_op jit(solution)/shard_map/ppermute | solution.py:198
  96.9 3.0 collective-permute-start.5
  99.9 1.6 copy-done.5
  101.5 12.7 %shard_map.125.refs_5_ = f32[8,512,128]{2,1,0:T(8,128)S(1)} custom-call(s32[1]{0:T(128)} %bitcast.27.refs_0_, s32[7]{0:T(128)S(1)} %stack.9.refs_1_, bf16[8,512,80]{2,1,0:T(8,128)(2,1)S(1)} %bitcast.47, bf16[1280,1152]{1,0:T(8,128)(2,1)} %collective-permute-done.2.refs_3_.refs_4_, ...), custom_call_target="tpu_custom_call", output_to_operand_aliasing={{}: (5, {})} | custom-call | flops 1509949440 | bytes 7143424 | tf_op jit(solution)/shard_map/pallas_call | solution.py:89
  114.2 12.9 %shard_map.126.refs_5_ = f32[8,512,128]{2,1,0:T(8,128)S(1)} custom-call(s32[1]{0:T(128)} %bitcast.26.refs_0_, s32[7]{0:T(128)S(1)} %stack.9.refs_1_, bf16[8,512,80]{2,1,0:T(8,128)(2,1)S(1)} %bitcast.48, bf16[1280,1152]{1,0:T(8,128)(2,1)} %collective-permute-done.3.refs_3_.refs_4_, ...), custom_call_target="tpu_custom_call", output_to_operand_aliasing={{}: (5, {})} | custom-call | flops 1509949440 | bytes 7143424 | tf_op jit(solution)/shard_map/pallas_call | solution.py:89
  127.1 5.9 %collective-permute-done.4.refs_3_.refs_4_ = bf16[1280,1152]{1,0:T(8,128)(2,1)} collective-permute-done((bf16[1280,1152]{1,0:T(8,128)(2,1)}, bf16[1280,1152]{1,0:T(8,128)(2,1)}, u32[]{:S(2)}, u32[]{:S(2)}) %collective-permute-start.4) | collective-permute-done | bytes 2949152 | tf_op jit(solution)/shard_map/ppermute | solution.py:198
  133.1 2.7 slice.108
  135.8 3.0 collective-permute-start.7
  138.7 2.5 slice.107
  141.2 1.6 copy-done.7
  142.8 12.7 %shard_map.127.refs_5_ = f32[8,512,128]{2,1,0:T(8,128)S(1)} custom-call(s32[1]{0:T(128)} %bitcast.29.refs_0_, s32[7]{0:T(128)S(1)} %stack.9.refs_1_, bf16[8,512,80]{2,1,0:T(8,128)(2,1)S(1)} %bitcast.49, bf16[1280,1152]{1,0:T(8,128)(2,1)} %collective-permute-done.4.refs_3_.refs_4_, ...), custom_call_target="tpu_custom_call", output_to_operand_aliasing={{}: (5, {})} | custom-call | flops 1509949440 | bytes 7143424 | tf_op jit(solution)/shard_map/pallas_call | solution.py:89
  155.5 12.7 %shard_map.128.refs_5_ = f32[8,512,128]{2,1,0:T(8,128)S(1)} custom-call(s32[1]{0:T(128)} %bitcast.28.refs_0_, s32[7]{0:T(128)S(1)} %stack.9.refs_1_, bf16[8,512,80]{2,1,0:T(8,128)(2,1)S(1)} %bitcast.50, bf16[1280,1152]{1,0:T(8,128)(2,1)} %collective-permute-done.5.refs_3_.refs_4_, ...), custom_call_target="tpu_custom_call", output_to_operand_aliasing={{}: (5, {})} | custom-call | flops 1509949440 | bytes 7143424 | tf_op jit(solution)/shard_map/pallas_call | solution.py:89
  168.3 2.0 pad_maximum_fusion.1.refs_3_.refs_4_
  170.3 12.2 %shard_map.129 = f32[8,512,128]{2,1,0:T(8,128)S(1)} custom-call(s32[1]{0:T(128)} %bitcast.refs_0_, s32[7]{0:T(128)S(1)} %stack.9.refs_1_, bf16[8,512,80]{2,1,0:T(8,128)(2,1)S(1)} %bitcast.51, bf16[1280,1152]{1,0:T(8,128)(2,1)S(1)} %pad_maximum_fusion.1.refs_3_.refs_4_, ...), custom_call_target="tpu_custom_call", output_to_operand_aliasing={{}: (5, {})} | custom-call | flops 1509949440 | bytes 7143424 | tf_op jit(solution)/shard_map/pallas_call | solution.py:89
  182.6 1.2 slice_reduce_fusion
  183.7 1.5 fusion.2
  185.2 1.5 copy.38
  186.8 6.8 %multiply_reduce_fusion = (f32[128]{0:T(128)S(1)}, f32[128,2560]{1,0:T(8,128)S(1)}) fusion(bf16[128,2560]{0,1:T(8,128)(2,1)S(1)} %bitcast.52, bf16[2560,2560]{1,0:T(8,128)(2,1)} %param.19, bf16[128,2560]{1,0:T(8,128)(2,1)} %param.13), kind=kOutput, calls=%fused_computation.17 | convolution fusion | flops 1679687552 | bytes 15729152 | tf_op jit(solution)/shard_map/dot_general | solution.py:210
  193.6 1.1 copy-done.8
  194.8 1.0 multiply_convert_fusion.1
  195.8 0.0 all-gather.2.cloned.1.call-update
  195.8 0.0 reduce-scatter.2.cloned.1.call-start
  195.8 81.7 %all-gather.2.cloned.1.call-done = bf16[2048,2560]{1,0:T(8,128)(2,1)} async-done(((bf16[128,2560]{1,0:T(8,128)(2,1)}), bf16[2048,2560]{1,0:T(8,128)(2,1)}) %all-gather.2.cloned.1.call-update) | async-done | bytes 10485776 | tf_op jit(solution)/shard_map/all_gather | solution.py:219
  277.5 11.3 %fusion.9 = f32[2048,448]{0,1:T(8,128)} fusion(bf16[2048,2560]{1,0:T(8,128)(2,1)} %all-gather.2.cloned.1.call-done, bf16[2560,448]{0,1:T(8,128)(2,1)} %param.21), kind=kOutput, calls=%fused_computation.38 | convolution fusion | flops 4697620480 | bytes 16449536 | tf_op jit(solution)/shard_map/dot_general | solution.py:220
  288.9 16.9 %convolution_convert_fusion = bf16[2048,2560]{1,0:T(8,128)(2,1)} fusion(bf16[448,2560]{1,0:T(8,128)(2,1)S(1)} %copy-done, f32[2048,448]{0,1:T(8,128)} %fusion.9, bf16[2048,2560]{1,0:T(8,128)(2,1)} %all-gather.2.cloned.1.call-done, bf16[2560,448]{0,1:T(8,128)(2,1)} %param.22), kind=kOutput, calls=%fused_computation | convolution fusion | flops 9405988864 | bytes 29229056 | tf_op jit(solution)/shard_map/dot_general | solution.py:224
  305.8 0.0 reduce-scatter.2.cloned.1.call-update
  305.8 1.1 copy.39
  306.9 88.9 %reduce-scatter.2.cloned.1.call-done = bf16[128,2560]{1,0:T(8,128)(2,1)} async-done(((bf16[2048,2560]{1,0:T(8,128)(2,1)}), bf16[128,2560]{1,0:T(8,128)(2,1)}) %reduce-scatter.2.cloned.1.call-update) | async-done | bytes 655376 | tf_op jit(solution)/shard_map/reduce_scatter | solution.py:223
  395.8 2.4 add_convert_fusion.1
  (29 shorter events, 0.1 us)
Async XLA Ops:
  7.2 281.7 %copy-start = (bf16[448,2560]{1,0:T(8,128)(2,1)S(1)}, bf16[448,2560]{1,0:T(8,128)(2,1)}, u32[]{:S(2)}) copy-start(bf16[448,2560]{1,0:T(8,128)(2,1)} %param.23) | copy-start | bytes 6881284
  7.2 270.4 %all-gather.2.cloned.1.call-start = ((), (), s32[]{:S(2)}) async-start(), calls=%async_computation.1 | async-start | bytes 11141120 | tf_op jit(solution)/shard_map/all_gather | solution.py:219
  21.1 36.6 %collective-permute-start.1 = (bf16[1280,1152]{1,0:T(8,128)(2,1)}, bf16[1280,1152]{1,0:T(8,128)(2,1)}, u32[]{:S(2)}, u32[]{:S(2)}) collective-permute-start(bf16[1280,1152]{1,0:T(8,128)(2,1)} %pad_maximum_fusion.refs_3_.refs_4_), channel_id=1, source_target_pairs={{0,7},{1,0},{2,1},{3,2},{4,3},{5,4},{6,5},{7,6},{8,15},{9,8},{10,9... | collective-permute-start | bytes 8847368 | tf_op jit(solution)/shard_map/ppermute | solution.py:200
  24.7 36.1 %collective-permute-start = (bf16[1280,1152]{1,0:T(8,128)(2,1)}, bf16[1280,1152]{1,0:T(8,128)(2,1)}, u32[]{:S(2)}, u32[]{:S(2)}) collective-permute-start(bf16[1280,1152]{1,0:T(8,128)(2,1)} %pad_maximum_fusion.refs_3_.refs_4_), channel_id=1, source_target_pairs={{0,1},{1,2},{2,3},{3,4},{4,5},{5,6},{6,7},{7,0},{8,9},{9,10},{10,1... | collective-permute-start | bytes 8847368 | tf_op jit(solution)/shard_map/ppermute | solution.py:198
  29.3 3.7 copy-start.10
  37.5 2.3 copy-start.1
  52.5 1.4 copy-start.2
  60.8 36.1 %collective-permute-start.2 = (bf16[1280,1152]{1,0:T(8,128)(2,1)}, bf16[1280,1152]{1,0:T(8,128)(2,1)}, u32[]{:S(2)}, u32[]{:S(2)}) collective-permute-start(bf16[1280,1152]{1,0:T(8,128)(2,1)} %collective-permute-done.refs_3_.refs_4_), channel_id=1, source_target_pairs={{0,1},{1,2},{2,3},{3,4},{4,5},{5,6},{6,7},{7,0},{8,9},{9,10},{10,1... | collective-permute-start | bytes 8847368 | tf_op jit(solution)/shard_map/ppermute | solution.py:198
  60.8 36.1 %collective-permute-start.3 = (bf16[1280,1152]{1,0:T(8,128)(2,1)}, bf16[1280,1152]{1,0:T(8,128)(2,1)}, u32[]{:S(2)}, u32[]{:S(2)}) collective-permute-start(bf16[1280,1152]{1,0:T(8,128)(2,1)} %collective-permute-done.1.refs_3_.refs_4_), channel_id=1, source_target_pairs={{0,7},{1,0},{2,1},{3,2},{4,3},{5,4},{6,5},{7,6},{8,15},{9,8},{10,9... | collective-permute-start | bytes 8847368 | tf_op jit(solution)/shard_map/ppermute | solution.py:200
  63.8 1.6 copy-start.3
  90.8 1.4 copy-start.4
  96.9 36.1 %collective-permute-start.4 = (bf16[1280,1152]{1,0:T(8,128)(2,1)}, bf16[1280,1152]{1,0:T(8,128)(2,1)}, u32[]{:S(2)}, u32[]{:S(2)}) collective-permute-start(bf16[1280,1152]{1,0:T(8,128)(2,1)} %collective-permute-done.2.refs_3_.refs_4_), channel_id=1, source_target_pairs={{0,1},{1,2},{2,3},{3,4},{4,5},{5,6},{6,7},{7,0},{8,9},{9,10},{10,1... | collective-permute-start | bytes 8847368 | tf_op jit(solution)/shard_map/ppermute | solution.py:198
  96.9 36.1 %collective-permute-start.5 = (bf16[1280,1152]{1,0:T(8,128)(2,1)}, bf16[1280,1152]{1,0:T(8,128)(2,1)}, u32[]{:S(2)}, u32[]{:S(2)}) collective-permute-start(bf16[1280,1152]{1,0:T(8,128)(2,1)} %collective-permute-done.3.refs_3_.refs_4_), channel_id=1, source_target_pairs={{0,7},{1,0},{2,1},{3,2},{4,3},{5,4},{6,5},{7,6},{8,15},{9,8},{10,9... | collective-permute-start | bytes 8847368 | tf_op jit(solution)/shard_map/ppermute | solution.py:200
  99.9 1.6 copy-start.5
  127.1 14.1 %copy-start.6 = (f32[8,512,128]{2,1,0:T(8,128)}, f32[8,512,128]{2,1,0:T(8,128)S(1)}, u32[]{:S(2)}) copy-start(f32[8,512,128]{2,1,0:T(8,128)S(1)} %shard_map.126.refs_5_) | copy-start | bytes 6291460
  135.8 32.5 %collective-permute-start.7 = (bf16[1280,640]{1,0:T(8,128)(2,1)}, bf16[1280,640]{1,0:T(8,128)(2,1)}, u32[]{:S(2)}, u32[]{:S(2)}) collective-permute-start(bf16[1280,640]{1,0:T(8,128)(2,1)} %slice.108), channel_id=1, source_target_pairs={{0,7},{1,0},{2,1},{3,2},{4,3},{5,4},{6,5},{7,6},{8,15},{9,8},{10,9... | collective-permute-start | bytes 4915208 | tf_op jit(solution)/shard_map/ppermute | solution.py:195
  141.2 27.1 %collective-permute-start.6 = (bf16[1280,512]{1,0:T(8,128)(2,1)}, bf16[1280,512]{1,0:T(8,128)(2,1)}, u32[]{:S(2)}, u32[]{:S(2)}) collective-permute-start(bf16[1280,512]{1,0:T(8,128)(2,1)} %slice.107), channel_id=1, source_target_pairs={{0,1},{1,2},{2,3},{3,4},{4,5},{5,6},{6,7},{7,0},{8,9},{9,10},{10,1... | collective-permute-start | bytes 3932168 | tf_op jit(solution)/shard_map/ppermute | solution.py:194
  141.2 1.6 copy-start.7
  186.8 8.0 %copy-start.9 = (f32[2560]{0:T(1024)S(1)}, f32[2560]{0:T(1024)}, u32[]{:S(2)}) copy-start(f32[2560]{0:T(1024)} %param.20) | copy-start | bytes 30724
  193.6 1.2 copy-start.8
  195.8 200.0 %reduce-scatter.2.cloned.1.call-start = ((), (), s32[]{:S(2)}) async-start(), calls=%async_computation.2 | async-start | bytes 11141120 | tf_op jit(solution)/shard_map/reduce_scatter | solution.py:223
Sparse Core Ops, SparseCore 0:
  195.9 81.5 all-gather.1
  305.9 89.8 reduce-scatter.1

commit v8 on v6

--- a/solution.py
+++ b/solution.py
@@ -214,6 +214,7 @@
     gate_proj = jnp.dot(shard_piece, w_gate, preferred_element_type=jnp.float32)
     up_proj = jnp.dot(shard_piece, w_up, preferred_element_type=jnp.float32)
     activated = (jax.nn.silu(gate_proj) * up_proj).astype(jnp.bfloat16)
+    activated = lax.optimization_barrier(activated)
     summed = lax.psum_scatter(
         jnp.dot(activated, w_down, preferred_element_type=jnp.float32).astype(jnp.bfloat16),
         "req",

time: 402 us -> 396 us (0.985)
  matrix products: 35 us -> 29.1 us
    dot_general x1, matrix products: 16.9 us -> 8.46 us  [body(): jnp.dot(activated, w_down, preferred_element_type=jnp.float32)]
    dot_general x0 -> x1, matrix products: none -> 5.12 us  [body(): up_proj = jnp.dot(shard_piece, w_up, preferred_element_type=jnp.float32)]
    unnamed x26 -> x30, local copies, waits for them, and re-layouts: 16.8 us -> 16.8 us
where the time goes in v8:
time: 396 us
  waiting for transfers between devices  194 us (49%)
  Pallas kernels  101 us (26%)
  local copies, waits for them, and re-layouts  32.1 us (8%)
  matrix products  29.1 us (7%)
  other arithmetic  15.5 us (4%)
  between operations  14.3 us (4%)
  starting transfers between devices  9.59 us (2%)
    pallas_call x8, Pallas kernels, attention_block(): pl.pallas_call(kernel, grid=(heads,), in_specs=[pl.BlockSpec(memory_space...  101 us
    reduce_scatter x1, waiting for transfers between devices, body(): lax.psum_scatter(jnp.dot(activated, w_down, preferred_element_type=jnp.fl...  88.6 us
    all_gather x1, waiting for transfers between devices, body(): shard_piece = lax.all_gather(normed, 'req', axis=0, tiled=True)  79.3 us
    ppermute x4, waiting for transfers between devices, body(): cw_blk = lax.ppermute(cw_blk, 'kv', cw_pairs)  22.4 us
    unnamed x30, local copies, waits for them, and re-layouts  16.8 us
    ppermute x3, starting transfers between devices, body(): ccw_blk = lax.ppermute(ccw_blk, 'kv', ccw_pairs)  9.5 us
    dot_general x1, matrix products, body(): gate_proj = jnp.dot(shard_piece, w_gate, preferred_element_type=jnp.float32)  8.71 us
    dot_general x1, matrix products, body(): jnp.dot(activated, w_down, preferred_element_type=jnp.float32)  8.46 us
  transfers between devices with their start and end apart: 9, of which 7 were waited for; matrix products, arithmetic and copies ran while one was open for 4% of the time, Pallas kernels for 22%

profile of v8, /device:TPU:0, one launch (start us, length us, event | category | flops | bytes accessed | tf_op | source)
XLA Modules:
  0.0 395.6 jit_solution(13929101791133476635)
XLA Ops:
  7.2 0.0 copy-start
  7.2 0.0 all-gather.2.cloned.1.call-start
  7.3 0.8 broadcast_multiply_fusion
  8.1 0.8 reduce-window.4
  8.9 0.7 select_reduce_fusion
  9.6 0.1 add_bitcast_fusion
  9.7 1.2 copy.37
  10.9 4.5 %copy.40 = bf16[1024,1280]{0,1:T(8,128)(2,1)} copy(bf16[1024,1280]{1,0:T(8,128)(2,1)} %bitcast.58) | data formatting | bytes 5242880 | tf_op jit(solution)/shard_map/reshape | solution.py:151
  15.4 2.0 maximum_bitcast_fusion
  17.5 0.2 fusion.4
  17.7 0.2 convert.21
  17.9 0.7 multiply_cosine_fusion
  18.7 0.4 subtract_convert_fusion
  19.1 0.1 pad_maximum_fusion.1
  19.2 1.9 pad_maximum_fusion.refs_3_.refs_4_
  21.1 3.6 collective-permute-start.1
  24.7 1.4 copy.33
  26.1 0.1 convert.20
  26.2 0.2 multiply_cosine_fusion.1
  26.4 0.2 subtract_convert_fusion.1
  26.5 1.3 copy.35
  27.9 1.4 copy.34
  29.3 3.1 copy.50.refs_5_
  32.3 0.6 fusion.6
  33.0 0.7 fusion.5
  33.6 3.9 stack.9.refs_1_
  37.5 2.3 pad_maximum_fusion.2
  39.8 12.6 %shard_map.122.refs_5_ = f32[8,512,128]{2,1,0:T(8,128)S(1)} custom-call(s32[1]{0:T(128)} %bitcast.22.refs_0_, s32[7]{0:T(128)S(1)} %stack.9.refs_1_, bf16[8,512,80]{2,1,0:T(8,128)(2,1)S(1)} %bitcast.45, bf16[1280,1152]{1,0:T(8,128)(2,1)} %pad_maximum_fusion.refs_3_.refs_4_, ...), custom_call_target="tpu_custom_call", output_to_operand_aliasing={{}: (5, {})} | custom-call | flops 1509949440 | bytes 7143424 | tf_op jit(solution)/shard_map/pallas_call | solution.py:89
  52.4 1.4 copy-done.2
  53.8 3.9 collective-permute-done.1.refs_3_.refs_4_
  57.7 3.1 collective-permute-done.refs_3_.refs_4_
  60.8 3.0 collective-permute-start.3
  63.8 1.6 copy-done.3
  65.4 12.6 %shard_map.123.refs_5_ = f32[8,512,128]{2,1,0:T(8,128)S(1)} custom-call(s32[1]{0:T(128)} %bitcast.25.refs_0_, s32[7]{0:T(128)S(1)} %stack.9.refs_1_, bf16[8,512,80]{2,1,0:T(8,128)(2,1)S(1)} %bitcast.46, bf16[1280,1152]{1,0:T(8,128)(2,1)} %collective-permute-done.refs_3_.refs_4_, ...), custom_call_target="tpu_custom_call", output_to_operand_aliasing={{}: (5, {})} | custom-call | flops 1509949440 | bytes 7143424 | tf_op jit(solution)/shard_map/pallas_call | solution.py:89
  77.9 12.6 %shard_map.124.refs_5_ = f32[8,512,128]{2,1,0:T(8,128)S(1)} custom-call(s32[1]{0:T(128)} %bitcast.24.refs_0_, s32[7]{0:T(128)S(1)} %stack.9.refs_1_, bf16[8,512,80]{2,1,0:T(8,128)(2,1)S(1)} %bitcast.47, bf16[1280,1152]{1,0:T(8,128)(2,1)} %collective-permute-done.1.refs_3_.refs_4_, ...), custom_call_target="tpu_custom_call", output_to_operand_aliasing={{}: (5, {})} | custom-call | flops 1509949440 | bytes 7143424 | tf_op jit(solution)/shard_map/pallas_call | solution.py:89
  90.5 1.4 copy-done.4
  91.9 5.0 %collective-permute-done.2.refs_3_.refs_4_ = bf16[1280,1152]{1,0:T(8,128)(2,1)} collective-permute-done((bf16[1280,1152]{1,0:T(8,128)(2,1)}, bf16[1280,1152]{1,0:T(8,128)(2,1)}, u32[]{:S(2)}, u32[]{:S(2)}) %collective-permute-start.2) | collective-permute-done | bytes 2949152 | tf_op jit(solution)/shard_map/ppermute | solution.py:192
  96.9 3.0 collective-permute-start.5
  99.9 1.6 copy-done.5
  101.5 12.6 %shard_map.125.refs_5_ = f32[8,512,128]{2,1,0:T(8,128)S(1)} custom-call(s32[1]{0:T(128)} %bitcast.27.refs_0_, s32[7]{0:T(128)S(1)} %stack.9.refs_1_, bf16[8,512,80]{2,1,0:T(8,128)(2,1)S(1)} %bitcast.48, bf16[1280,1152]{1,0:T(8,128)(2,1)} %collective-permute-done.2.refs_3_.refs_4_, ...), custom_call_target="tpu_custom_call", output_to_operand_aliasing={{}: (5, {})} | custom-call | flops 1509949440 | bytes 7143424 | tf_op jit(solution)/shard_map/pallas_call | solution.py:89
  114.0 12.6 %shard_map.126.refs_5_ = f32[8,512,128]{2,1,0:T(8,128)S(1)} custom-call(s32[1]{0:T(128)} %bitcast.26.refs_0_, s32[7]{0:T(128)S(1)} %stack.9.refs_1_, bf16[8,512,80]{2,1,0:T(8,128)(2,1)S(1)} %bitcast.49, bf16[1280,1152]{1,0:T(8,128)(2,1)} %collective-permute-done.3.refs_3_.refs_4_, ...), custom_call_target="tpu_custom_call", output_to_operand_aliasing={{}: (5, {})} | custom-call | flops 1509949440 | bytes 7143424 | tf_op jit(solution)/shard_map/pallas_call | solution.py:89
  126.7 1.4 copy-done.6
  128.0 5.0 %collective-permute-done.4.refs_3_.refs_4_ = bf16[1280,1152]{1,0:T(8,128)(2,1)} collective-permute-done((bf16[1280,1152]{1,0:T(8,128)(2,1)}, bf16[1280,1152]{1,0:T(8,128)(2,1)}, u32[]{:S(2)}, u32[]{:S(2)}) %collective-permute-start.4) | collective-permute-done | bytes 2949152 | tf_op jit(solution)/shard_map/ppermute | solution.py:192
  133.0 1.6 copy-done.7
  134.6 12.6 %shard_map.127.refs_5_ = f32[8,512,128]{2,1,0:T(8,128)S(1)} custom-call(s32[1]{0:T(128)} %bitcast.29.refs_0_, s32[7]{0:T(128)S(1)} %stack.9.refs_1_, bf16[8,512,80]{2,1,0:T(8,128)(2,1)S(1)} %bitcast.50, bf16[1280,1152]{1,0:T(8,128)(2,1)} %collective-permute-done.4.refs_3_.refs_4_, ...), custom_call_target="tpu_custom_call", output_to_operand_aliasing={{}: (5, {})} | custom-call | flops 1509949440 | bytes 7143424 | tf_op jit(solution)/shard_map/pallas_call | solution.py:89
  147.2 12.6 %shard_map.128.refs_5_ = f32[8,512,128]{2,1,0:T(8,128)S(1)} custom-call(s32[1]{0:T(128)} %bitcast.28.refs_0_, s32[7]{0:T(128)S(1)} %stack.9.refs_1_, bf16[8,512,80]{2,1,0:T(8,128)(2,1)S(1)} %bitcast.51, bf16[1280,1152]{1,0:T(8,128)(2,1)} %collective-permute-done.5.refs_3_.refs_4_, ...), custom_call_target="tpu_custom_call", output_to_operand_aliasing={{}: (5, {})} | custom-call | flops 1509949440 | bytes 7143424 | tf_op jit(solution)/shard_map/pallas_call | solution.py:89
  159.8 9.3 %collective-permute-done.6.refs_3_.refs_4_ = bf16[1280,1152]{1,0:T(8,128)(2,1)} collective-permute-done((bf16[1280,1152]{1,0:T(8,128)(2,1)}, bf16[1280,1152]{1,0:T(8,128)(2,1)}, u32[]{:S(2)}, u32[]{:S(2)}) %collective-permute-start.6) | collective-permute-done | bytes 2949152 | tf_op jit(solution)/shard_map/ppermute | solution.py:192
  169.2 12.6 %shard_map.129 = f32[8,512,128]{2,1,0:T(8,128)S(1)} custom-call(s32[1]{0:T(128)} %bitcast.refs_0_, s32[7]{0:T(128)S(1)} %stack.9.refs_1_, bf16[8,512,80]{2,1,0:T(8,128)(2,1)S(1)} %bitcast.52, bf16[1280,1152]{1,0:T(8,128)(2,1)} %collective-permute-done.6.refs_3_.refs_4_, ...), custom_call_target="tpu_custom_call", output_to_operand_aliasing={{}: (5, {})} | custom-call | flops 1509949440 | bytes 7143424 | tf_op jit(solution)/shard_map/pallas_call | solution.py:89
  181.7 1.2 slice_reduce_fusion
  182.9 1.5 fusion.2
  184.5 1.5 copy.38
  186.0 6.8 %multiply_reduce_fusion = (f32[128]{0:T(128)S(1)}, f32[128,2560]{1,0:T(8,128)S(1)}) fusion(bf16[128,2560]{0,1:T(8,128)(2,1)S(1)} %bitcast.53, bf16[2560,2560]{1,0:T(8,128)(2,1)} %param.19, bf16[128,2560]{1,0:T(8,128)(2,1)} %param.13), kind=kOutput, calls=%fused_computation.15 | convolution fusion | flops 1679687552 | bytes 15729152 | tf_op jit(solution)/shard_map/dot_general | solution.py:204
  192.8 1.1 copy-done.8
  193.9 1.0 multiply_convert_fusion.1
  194.9 0.0 all-gather.2.cloned.1.call-update
  194.9 0.0 reduce-scatter.2.cloned.1.call-start
  194.9 79.3 %all-gather.2.cloned.1.call-done = bf16[2048,2560]{1,0:T(8,128)(2,1)} async-done(((bf16[128,2560]{1,0:T(8,128)(2,1)}), bf16[2048,2560]{1,0:T(8,128)(2,1)}) %all-gather.2.cloned.1.call-update) | async-done | bytes 10485776 | tf_op jit(solution)/shard_map/all_gather | solution.py:213
  274.2 8.7 %fusion.7 = f32[2048,448]{0,1:T(8,128)S(1)} fusion(bf16[2048,2560]{1,0:T(8,128)(2,1)} %all-gather.2.cloned.1.call-done, bf16[2560,448]{0,1:T(8,128)(2,1)} %param.21), kind=kOutput, calls=%fused_computation.35 | convolution fusion | flops 4697620480 | bytes 16449536 | tf_op jit(solution)/shard_map/dot_general | solution.py:214
  282.9 5.1 %multiply_convert_fusion = bf16[2048,448]{0,1:T(8,128)(2,1)S(1)} fusion(f32[2048,448]{0,1:T(8,128)S(1)} %fusion.7, bf16[2048,2560]{1,0:T(8,128)(2,1)S(1)} %copy-done.11, bf16[2560,448]{0,1:T(8,128)(2,1)S(1)} %copy-done.12), kind=kOutput, calls=%fused_computation.1 | convolution fusion | flops 4703125504 | bytes 18284544 | tf_op jit(solution)/shard_map/dot_general | solution.py:215
  288.1 8.5 %convolution_convert_fusion = bf16[2048,2560]{1,0:T(8,128)(2,1)} fusion(bf16[2048,448]{0,1:T(8,128)(2,1)S(1)} %multiply_convert_fusion, bf16[448,2560]{1,0:T(8,128)(2,1)S(1)} %copy-done), kind=kOutput, calls=%fused_computation | convolution fusion | flops 4702863360 | bytes 14614528 | tf_op jit(solution)/shard_map/dot_general | solution.py:219
  296.6 0.0 reduce-scatter.2.cloned.1.call-update
  296.6 1.1 copy.39
  297.7 88.6 %reduce-scatter.2.cloned.1.call-done = bf16[128,2560]{1,0:T(8,128)(2,1)} async-done(((bf16[2048,2560]{1,0:T(8,128)(2,1)}), bf16[128,2560]{1,0:T(8,128)(2,1)}) %reduce-scatter.2.cloned.1.call-update) | async-done | bytes 655376 | tf_op jit(solution)/shard_map/reduce_scatter | solution.py:218
  386.3 2.4 add_convert_fusion.1
  (29 shorter events, 0.1 us)
Async XLA Ops:
  7.2 280.9 %copy-start = (bf16[448,2560]{1,0:T(8,128)(2,1)S(1)}, bf16[448,2560]{1,0:T(8,128)(2,1)}, u32[]{:S(2)}) copy-start(bf16[448,2560]{1,0:T(8,128)(2,1)} %param.23) | copy-start | bytes 6881284
  7.2 267.0 %all-gather.2.cloned.1.call-start = ((), (), s32[]{:S(2)}) async-start(), calls=%async_computation.1 | async-start | bytes 11141120 | tf_op jit(solution)/shard_map/all_gather | solution.py:213
  21.1 36.6 %collective-permute-start.1 = (bf16[1280,1152]{1,0:T(8,128)(2,1)}, bf16[1280,1152]{1,0:T(8,128)(2,1)}, u32[]{:S(2)}, u32[]{:S(2)}) collective-permute-start(bf16[1280,1152]{1,0:T(8,128)(2,1)} %pad_maximum_fusion.refs_3_.refs_4_), channel_id=1, source_target_pairs={{0,7},{1,0},{2,1},{3,2},{4,3},{5,4},{6,5},{7,6},{8,15},{9,8},{10,9... | collective-permute-start | bytes 8847368 | tf_op jit(solution)/shard_map/ppermute | solution.py:194
  24.7 36.1 %collective-permute-start = (bf16[1280,1152]{1,0:T(8,128)(2,1)}, bf16[1280,1152]{1,0:T(8,128)(2,1)}, u32[]{:S(2)}, u32[]{:S(2)}) collective-permute-start(bf16[1280,1152]{1,0:T(8,128)(2,1)} %pad_maximum_fusion.refs_3_.refs_4_), channel_id=1, source_target_pairs={{0,1},{1,2},{2,3},{3,4},{4,5},{5,6},{6,7},{7,0},{8,9},{9,10},{10,1... | collective-permute-start | bytes 8847368 | tf_op jit(solution)/shard_map/ppermute | solution.py:192
  29.3 3.7 copy-start.10
  37.5 2.3 copy-start.1
  52.4 1.4 copy-start.2
  60.8 36.1 %collective-permute-start.2 = (bf16[1280,1152]{1,0:T(8,128)(2,1)}, bf16[1280,1152]{1,0:T(8,128)(2,1)}, u32[]{:S(2)}, u32[]{:S(2)}) collective-permute-start(bf16[1280,1152]{1,0:T(8,128)(2,1)} %collective-permute-done.refs_3_.refs_4_), channel_id=1, source_target_pairs={{0,1},{1,2},{2,3},{3,4},{4,5},{5,6},{6,7},{7,0},{8,9},{9,10},{10,1... | collective-permute-start | bytes 8847368 | tf_op jit(solution)/shard_map/ppermute | solution.py:192
  60.8 36.1 %collective-permute-start.3 = (bf16[1280,1152]{1,0:T(8,128)(2,1)}, bf16[1280,1152]{1,0:T(8,128)(2,1)}, u32[]{:S(2)}, u32[]{:S(2)}) collective-permute-start(bf16[1280,1152]{1,0:T(8,128)(2,1)} %collective-permute-done.1.refs_3_.refs_4_), channel_id=1, source_target_pairs={{0,7},{1,0},{2,1},{3,2},{4,3},{5,4},{6,5},{7,6},{8,15},{9,8},{10,9... | collective-permute-start | bytes 8847368 | tf_op jit(solution)/shard_map/ppermute | solution.py:194
  63.8 1.6 copy-start.3
  90.5 1.4 copy-start.4
  96.9 36.1 %collective-permute-start.4 = (bf16[1280,1152]{1,0:T(8,128)(2,1)}, bf16[1280,1152]{1,0:T(8,128)(2,1)}, u32[]{:S(2)}, u32[]{:S(2)}) collective-permute-start(bf16[1280,1152]{1,0:T(8,128)(2,1)} %collective-permute-done.2.refs_3_.refs_4_), channel_id=1, source_target_pairs={{0,1},{1,2},{2,3},{3,4},{4,5},{5,6},{6,7},{7,0},{8,9},{9,10},{10,1... | collective-permute-start | bytes 8847368 | tf_op jit(solution)/shard_map/ppermute | solution.py:192
  96.9 36.1 %collective-permute-start.5 = (bf16[1280,1152]{1,0:T(8,128)(2,1)}, bf16[1280,1152]{1,0:T(8,128)(2,1)}, u32[]{:S(2)}, u32[]{:S(2)}) collective-permute-start(bf16[1280,1152]{1,0:T(8,128)(2,1)} %collective-permute-done.3.refs_3_.refs_4_), channel_id=1, source_target_pairs={{0,7},{1,0},{2,1},{3,2},{4,3},{5,4},{6,5},{7,6},{8,15},{9,8},{10,9... | collective-permute-start | bytes 8847368 | tf_op jit(solution)/shard_map/ppermute | solution.py:194
  99.9 1.6 copy-start.5
  126.6 1.4 copy-start.6
  133.0 36.1 %collective-permute-start.6 = (bf16[1280,1152]{1,0:T(8,128)(2,1)}, bf16[1280,1152]{1,0:T(8,128)(2,1)}, u32[]{:S(2)}, u32[]{:S(2)}) collective-permute-start(bf16[1280,1152]{1,0:T(8,128)(2,1)} %collective-permute-done.4.refs_3_.refs_4_), channel_id=1, source_target_pairs={{0,1},{1,2},{2,3},{3,4},{4,5},{5,6},{6,7},{7,0},{8,9},{9,10},{10,1... | collective-permute-start | bytes 8847368 | tf_op jit(solution)/shard_map/ppermute | solution.py:192
  133.0 1.6 copy-start.7
  186.0 7.9 %copy-start.9 = (f32[2560]{0:T(1024)S(1)}, f32[2560]{0:T(1024)}, u32[]{:S(2)}) copy-start(f32[2560]{0:T(1024)} %param.20) | copy-start | bytes 30724
  192.8 1.1 copy-start.8
  194.9 191.4 %reduce-scatter.2.cloned.1.call-start = ((), (), s32[]{:S(2)}) async-start(), calls=%async_computation.2 | async-start | bytes 11141120 | tf_op jit(solution)/shard_map/reduce_scatter | solution.py:218
  274.2 8.7 %copy-start.11 = (bf16[2048,2560]{1,0:T(8,128)(2,1)S(1)}, bf16[2048,2560]{1,0:T(8,128)(2,1)}, u32[]{:S(2)}) copy-start(bf16[2048,2560]{1,0:T(8,128)(2,1)} %all-gather.2.cloned.1.call-done) | copy-start | bytes 31457284
  274.2 8.7 %copy-start.12 = (bf16[2560,448]{0,1:T(8,128)(2,1)S(1)}, bf16[2560,448]{0,1:T(8,128)(2,1)}, u32[]{:S(2)}) copy-start(bf16[2560,448]{0,1:T(8,128)(2,1)} %param.22) | copy-start | bytes 6881284
Sparse Core Ops, SparseCore 0:
  195.0 79.1 all-gather.1
  296.7 89.5 reduce-scatter.1

commit v9 on v8

--- a/solution.py
+++ b/solution.py
@@ -106,7 +106,7 @@
             bytes_accessed=2 * kv_blk.size + 8 * state.size,
         ),
         compiler_params=pltpu.CompilerParams(
-            dimension_semantics=("arbitrary",), vmem_limit_bytes=48 * 1024 * 1024
+            dimension_semantics=("arbitrary",), vmem_limit_bytes=63 * 1024 * 1024
         ),
     )(offset, scalars, q_heads, kv_blk, kv_blk, state)
 

time: 396 us -> 392 us (0.990)
  local copies, waits for them, and re-layouts: 32.1 us -> 19.1 us
  Pallas kernels: 101 us -> 108 us
  waiting for transfers between devices: 194 us -> 200 us
    unnamed x30 -> x20, local copies, waits for them, and re-layouts: 16.8 us -> 5.77 us
    pallas_call x8, Pallas kernels: 101 us -> 108 us  [attention_block(): pl.pallas_call(kernel, grid=(heads,), in_specs=[pl.BlockSpec(memory_space...]
  transfers between devices with their start and end apart: 9 -> 9, of which waited for: 7 -> 7; matrix products, arithmetic and copies ran while one was open for 4% -> 3% of each run, Pallas kernels for 22% -> 24%
where the time goes in v9:
time: 392 us
  waiting for transfers between devices  200 us (51%)
  Pallas kernels  108 us (28%)
  matrix products  29 us (7%)
  local copies, waits for them, and re-layouts  19.1 us (5%)
  between operations  14.3 us (4%)
  other arithmetic  11.8 us (3%)
  starting transfers between devices  9.59 us (2%)
    pallas_call x8, Pallas kernels, attention_block(): pl.pallas_call(kernel, grid=(heads,), in_specs=[pl.BlockSpec(memory_space...  108 us
    reduce_scatter x1, waiting for transfers between devices, body(): lax.psum_scatter(jnp.dot(activated, w_down, preferred_element_type=jnp.fl...  88.6 us
    all_gather x1, waiting for transfers between devices, body(): shard_piece = lax.all_gather(normed, 'req', axis=0, tiled=True)  79.3 us
    ppermute x4, waiting for transfers between devices, body(): cw_blk = lax.ppermute(cw_blk, 'kv', cw_pairs)  24.5 us
    ppermute x3, starting transfers between devices, body(): ccw_blk = lax.ppermute(ccw_blk, 'kv', ccw_pairs)  9.5 us
    dot_general x1, matrix products, body(): gate_proj = jnp.dot(shard_piece, w_gate, preferred_element_type=jnp.float32)  8.74 us
    dot_general x1, matrix products, body(): jnp.dot(activated, w_down, preferred_element_type=jnp.float32)  8.44 us
  transfers between devices with their start and end apart: 9, of which 7 were waited for; matrix products, arithmetic and copies ran while one was open for 3% of the time, Pallas kernels for 24%

profile of v9, /device:TPU:0, one launch (start us, length us, event | category | flops | bytes accessed | tf_op | source)
XLA Modules:
  0.0 391.5 jit_solution(6599060879404685099)
XLA Ops:
  7.2 0.0 all-gather.2.cloned.1.call-start
  7.2 0.7 broadcast_multiply_fusion
  7.9 0.8 reduce-window.4
  8.7 0.7 select_reduce_fusion
  9.5 0.1 add_bitcast_fusion
  9.6 1.2 copy.37
  10.7 3.0 copy.40
  13.7 0.3 maximum_bitcast_fusion
  14.0 0.2 fusion.4
  14.3 0.2 convert.21
  14.5 0.7 multiply_cosine_fusion
  15.2 0.4 subtract_convert_fusion
  15.7 0.1 pad_maximum_fusion.1
  15.8 0.0 copy-start.2
  15.8 1.9 pad_maximum_fusion.refs_3_.refs_4_
  17.7 3.6 collective-permute-start.1
  21.3 0.0 collective-permute-start
  21.3 0.3 copy.33
  21.6 0.1 convert.20
  21.7 0.2 multiply_cosine_fusion.1
  21.9 0.2 subtract_convert_fusion.1
  22.1 0.5 copy.35
  22.6 0.5 copy.34
  23.1 0.0 copy-start.4
  23.1 3.1 copy.50.refs_5_
  26.2 0.6 fusion.6
  26.9 0.6 fusion.5
  27.5 4.4 %stack.9.refs_1_ = s32[7]{0:T(128)} concatenate(s32[1]{0:T(128)S(1)} %bitcast.65, s32[1]{0:T(128)} %bitcast.2, s32[1]{0:T(128)} %bitcast.3, s32[1]{0:T(128)} %bitcast.4, s32[1]{0:T(128)} %bitcast.5, s32[1]{0:T(128)} %bitcast.6, s32[1]{0:T(128)} %bitcast.7), dimensions={0} | concatenate | bytes 56 | tf_op jit(solution)/shard_map/stack | solution.py:169
  31.9 1.6 pad_maximum_fusion.2
  33.5 13.5 %shard_map.122.refs_5_ = f32[8,512,128]{2,1,0:T(8,128)} custom-call(s32[1]{0:T(128)} %bitcast.22.refs_0_, s32[7]{0:T(128)} %stack.9.refs_1_, bf16[8,512,80]{2,1,0:T(8,128)(2,1)} %bitcast.45, bf16[1280,1152]{1,0:T(8,128)(2,1)} %pad_maximum_fusion.refs_3_.refs_4_, bf16[1280,1152]{1,0:T(8,128)(2,1)} %pad_maximum_fusion.refs_3_.refs_4_, ...), custom_call_target="tpu_custom_call", output_to_operand_aliasing={{}: (5, {})} | custom-call | flops 1509949440 | bytes 7143424 | tf_op jit(solution)/shard_map/pallas_call | solution.py:89
  46.9 7.4 %collective-permute-done.1.refs_3_.refs_4_ = bf16[1280,1152]{1,0:T(8,128)(2,1)} collective-permute-done((bf16[1280,1152]{1,0:T(8,128)(2,1)}, bf16[1280,1152]{1,0:T(8,128)(2,1)}, u32[]{:S(2)}, u32[]{:S(2)}) %collective-permute-start.1) | collective-permute-done | bytes 2949152 | tf_op jit(solution)/shard_map/ppermute | solution.py:194
  54.3 3.1 collective-permute-done.refs_3_.refs_4_
  57.4 0.0 collective-permute-start.2
  57.4 3.0 collective-permute-start.3
  60.4 13.5 %shard_map.123.refs_5_ = f32[8,512,128]{2,1,0:T(8,128)} custom-call(s32[1]{0:T(128)} %bitcast.25.refs_0_, s32[7]{0:T(128)} %stack.9.refs_1_, bf16[8,512,80]{2,1,0:T(8,128)(2,1)} %bitcast.46, bf16[1280,1152]{1,0:T(8,128)(2,1)} %collective-permute-done.refs_3_.refs_4_, ...), custom_call_target="tpu_custom_call", output_to_operand_aliasing={{}: (5, {})} | custom-call | flops 1509949440 | bytes 7143424 | tf_op jit(solution)/shard_map/pallas_call | solution.py:89
  73.9 13.5 %shard_map.124.refs_5_ = f32[8,512,128]{2,1,0:T(8,128)} custom-call(s32[1]{0:T(128)} %bitcast.24.refs_0_, s32[7]{0:T(128)} %stack.9.refs_1_, bf16[8,512,80]{2,1,0:T(8,128)(2,1)} %bitcast.47, bf16[1280,1152]{1,0:T(8,128)(2,1)} %collective-permute-done.1.refs_3_.refs_4_, ...), custom_call_target="tpu_custom_call", output_to_operand_aliasing={{}: (5, {})} | custom-call | flops 1509949440 | bytes 7143424 | tf_op jit(solution)/shard_map/pallas_call | solution.py:89
  87.3 6.2 %collective-permute-done.2.refs_3_.refs_4_ = bf16[1280,1152]{1,0:T(8,128)(2,1)} collective-permute-done((bf16[1280,1152]{1,0:T(8,128)(2,1)}, bf16[1280,1152]{1,0:T(8,128)(2,1)}, u32[]{:S(2)}, u32[]{:S(2)}) %collective-permute-start.2) | collective-permute-done | bytes 2949152 | tf_op jit(solution)/shard_map/ppermute | solution.py:192
  93.5 0.0 collective-permute-done.3.refs_3_.refs_4_
  93.5 3.0 collective-permute-start.5
  96.5 13.5 %shard_map.125.refs_5_ = f32[8,512,128]{2,1,0:T(8,128)} custom-call(s32[1]{0:T(128)} %bitcast.27.refs_0_, s32[7]{0:T(128)} %stack.9.refs_1_, bf16[8,512,80]{2,1,0:T(8,128)(2,1)} %bitcast.48, bf16[1280,1152]{1,0:T(8,128)(2,1)} %collective-permute-done.2.refs_3_.refs_4_, ...), custom_call_target="tpu_custom_call", output_to_operand_aliasing={{}: (5, {})} | custom-call | flops 1509949440 | bytes 7143424 | tf_op jit(solution)/shard_map/pallas_call | solution.py:89
  110.0 13.5 %shard_map.126.refs_5_ = f32[8,512,128]{2,1,0:T(8,128)} custom-call(s32[1]{0:T(128)} %bitcast.26.refs_0_, s32[7]{0:T(128)} %stack.9.refs_1_, bf16[8,512,80]{2,1,0:T(8,128)(2,1)} %bitcast.49, bf16[1280,1152]{1,0:T(8,128)(2,1)} %collective-permute-done.3.refs_3_.refs_4_, ...), custom_call_target="tpu_custom_call", output_to_operand_aliasing={{}: (5, {})} | custom-call | flops 1509949440 | bytes 7143424 | tf_op jit(solution)/shard_map/pallas_call | solution.py:89
  123.4 6.2 %collective-permute-done.4.refs_3_.refs_4_ = bf16[1280,1152]{1,0:T(8,128)(2,1)} collective-permute-done((bf16[1280,1152]{1,0:T(8,128)(2,1)}, bf16[1280,1152]{1,0:T(8,128)(2,1)}, u32[]{:S(2)}, u32[]{:S(2)}) %collective-permute-start.4) | collective-permute-done | bytes 2949152 | tf_op jit(solution)/shard_map/ppermute | solution.py:192
  129.7 13.7 %shard_map.127.refs_5_ = f32[8,512,128]{2,1,0:T(8,128)} custom-call(s32[1]{0:T(128)} %bitcast.29.refs_0_, s32[7]{0:T(128)} %stack.9.refs_1_, bf16[8,512,80]{2,1,0:T(8,128)(2,1)} %bitcast.50, bf16[1280,1152]{1,0:T(8,128)(2,1)} %collective-permute-done.4.refs_3_.refs_4_, ...), custom_call_target="tpu_custom_call", output_to_operand_aliasing={{}: (5, {})} | custom-call | flops 1509949440 | bytes 7143424 | tf_op jit(solution)/shard_map/pallas_call | solution.py:89
  143.3 13.5 %shard_map.128.refs_5_ = f32[8,512,128]{2,1,0:T(8,128)} custom-call(s32[1]{0:T(128)} %bitcast.28.refs_0_, s32[7]{0:T(128)} %stack.9.refs_1_, bf16[8,512,80]{2,1,0:T(8,128)(2,1)} %bitcast.51, bf16[1280,1152]{1,0:T(8,128)(2,1)} %collective-permute-done.5.refs_3_.refs_4_, ...), custom_call_target="tpu_custom_call", output_to_operand_aliasing={{}: (5, {})} | custom-call | flops 1509949440 | bytes 7143424 | tf_op jit(solution)/shard_map/pallas_call | solution.py:89
  156.8 9.0 %collective-permute-done.6.refs_3_.refs_4_ = bf16[1280,1152]{1,0:T(8,128)(2,1)} collective-permute-done((bf16[1280,1152]{1,0:T(8,128)(2,1)}, bf16[1280,1152]{1,0:T(8,128)(2,1)}, u32[]{:S(2)}, u32[]{:S(2)}) %collective-permute-start.6) | collective-permute-done | bytes 2949152 | tf_op jit(solution)/shard_map/ppermute | solution.py:192
  165.8 13.5 %shard_map.129 = f32[8,512,128]{2,1,0:T(8,128)} custom-call(s32[1]{0:T(128)} %bitcast.refs_0_, s32[7]{0:T(128)} %stack.9.refs_1_, bf16[8,512,80]{2,1,0:T(8,128)(2,1)} %bitcast.52, bf16[1280,1152]{1,0:T(8,128)(2,1)} %collective-permute-done.6.refs_3_.refs_4_, ...), custom_call_target="tpu_custom_call", output_to_operand_aliasing={{}: (5, {})} | custom-call | flops 1509949440 | bytes 7143424 | tf_op jit(solution)/shard_map/pallas_call | solution.py:89
  179.2 2.9 slice_reduce_fusion
  182.2 0.0 copy-start.1
  182.2 0.7 fusion.2
  182.9 0.6 copy.38
  183.5 0.0 copy-start.3
  183.5 6.7 %multiply_reduce_fusion = (f32[128]{0:T(128)S(1)}, f32[128,2560]{1,0:T(8,128)S(1)}) fusion(bf16[128,2560]{0,1:T(8,128)(2,1)S(1)} %bitcast.53, bf16[2560,2560]{1,0:T(8,128)(2,1)} %param.19, bf16[128,2560]{1,0:T(8,128)(2,1)S(1)} %copy-done.1), kind=kOutput, calls=%fused_computation.15 | convolution fusion | flops 1679687552 | bytes 15729152 | tf_op jit(solution)/shard_map/dot_general | solution.py:204
  190.2 1.0 multiply_convert_fusion.1
  191.3 0.0 all-gather.2.cloned.1.call-update
  191.3 0.0 reduce-scatter.2.cloned.1.call-start
  191.3 79.3 %all-gather.2.cloned.1.call-done = bf16[2048,2560]{1,0:T(8,128)(2,1)} async-done(((bf16[128,2560]{1,0:T(8,128)(2,1)}), bf16[2048,2560]{1,0:T(8,128)(2,1)}) %all-gather.2.cloned.1.call-update) | async-done | bytes 10485776 | tf_op jit(solution)/shard_map/all_gather | solution.py:213
  270.6 8.7 %fusion.7 = f32[2048,448]{0,1:T(8,128)S(1)} fusion(bf16[2048,2560]{1,0:T(8,128)(2,1)} %all-gather.2.cloned.1.call-done, bf16[2560,448]{0,1:T(8,128)(2,1)} %param.21), kind=kOutput, calls=%fused_computation.35 | convolution fusion | flops 4697620480 | bytes 16449536 | tf_op jit(solution)/shard_map/dot_general | solution.py:214
  279.4 0.0 copy-start.7
  279.4 5.1 %multiply_convert_fusion = bf16[2048,448]{0,1:T(8,128)(2,1)S(1)} fusion(f32[2048,448]{0,1:T(8,128)S(1)} %fusion.7, bf16[2048,2560]{1,0:T(8,128)(2,1)S(1)} %copy-done.5, bf16[2560,448]{0,1:T(8,128)(2,1)S(1)} %copy-done.6), kind=kOutput, calls=%fused_computation.1 | convolution fusion | flops 4703125504 | bytes 18284544 | tf_op jit(solution)/shard_map/dot_general | solution.py:215
  284.5 8.4 %convolution_convert_fusion = bf16[2048,2560]{1,0:T(8,128)(2,1)} fusion(bf16[2048,448]{0,1:T(8,128)(2,1)S(1)} %multiply_convert_fusion, bf16[448,2560]{1,0:T(8,128)(2,1)S(1)} %copy-done.7), kind=kOutput, calls=%fused_computation | convolution fusion | flops 4702863360 | bytes 14614528 | tf_op jit(solution)/shard_map/dot_general | solution.py:219
  293.0 0.0 reduce-scatter.2.cloned.1.call-update
  293.0 1.1 copy.39
  294.1 88.6 %reduce-scatter.2.cloned.1.call-done = bf16[128,2560]{1,0:T(8,128)(2,1)} async-done(((bf16[2048,2560]{1,0:T(8,128)(2,1)}), bf16[128,2560]{1,0:T(8,128)(2,1)}) %reduce-scatter.2.cloned.1.call-update) | async-done | bytes 655376 | tf_op jit(solution)/shard_map/reduce_scatter | solution.py:218
  382.7 2.0 add_convert_fusion.1
  (19 shorter events, 0.1 us)
Async XLA Ops:
  7.2 263.4 %all-gather.2.cloned.1.call-start = ((), (), s32[]{:S(2)}) async-start(), calls=%async_computation.1 | async-start | bytes 11141120 | tf_op jit(solution)/shard_map/all_gather | solution.py:213
  15.8 5.5 %copy-start.2 = (bf16[128,2560]{1,0:T(8,128)(2,1)S(1)}, bf16[128,2560]{1,0:T(8,128)(2,1)}, u32[]{:S(2)}) copy-start(bf16[128,2560]{1,0:T(8,128)(2,1)} %param.14) | copy-start | bytes 1966084
  17.7 36.6 %collective-permute-start.1 = (bf16[1280,1152]{1,0:T(8,128)(2,1)}, bf16[1280,1152]{1,0:T(8,128)(2,1)}, u32[]{:S(2)}, u32[]{:S(2)}) collective-permute-start(bf16[1280,1152]{1,0:T(8,128)(2,1)} %pad_maximum_fusion.refs_3_.refs_4_), channel_id=1, source_target_pairs={{0,7},{1,0},{2,1},{3,2},{4,3},{5,4},{6,5},{7,6},{8,15},{9,8},{10,9... | collective-permute-start | bytes 8847368 | tf_op jit(solution)/shard_map/ppermute | solution.py:194
  21.3 36.1 %collective-permute-start = (bf16[1280,1152]{1,0:T(8,128)(2,1)}, bf16[1280,1152]{1,0:T(8,128)(2,1)}, u32[]{:S(2)}, u32[]{:S(2)}) collective-permute-start(bf16[1280,1152]{1,0:T(8,128)(2,1)} %pad_maximum_fusion.refs_3_.refs_4_), channel_id=1, source_target_pairs={{0,1},{1,2},{2,3},{3,4},{4,5},{5,6},{6,7},{7,0},{8,9},{9,10},{10,1... | collective-permute-start | bytes 8847368 | tf_op jit(solution)/shard_map/ppermute | solution.py:192
  23.1 3.8 copy-start.4
  57.4 36.1 %collective-permute-start.2 = (bf16[1280,1152]{1,0:T(8,128)(2,1)}, bf16[1280,1152]{1,0:T(8,128)(2,1)}, u32[]{:S(2)}, u32[]{:S(2)}) collective-permute-start(bf16[1280,1152]{1,0:T(8,128)(2,1)} %collective-permute-done.refs_3_.refs_4_), channel_id=1, source_target_pairs={{0,1},{1,2},{2,3},{3,4},{4,5},{5,6},{6,7},{7,0},{8,9},{9,10},{10,1... | collective-permute-start | bytes 8847368 | tf_op jit(solution)/shard_map/ppermute | solution.py:192
  57.4 36.1 %collective-permute-start.3 = (bf16[1280,1152]{1,0:T(8,128)(2,1)}, bf16[1280,1152]{1,0:T(8,128)(2,1)}, u32[]{:S(2)}, u32[]{:S(2)}) collective-permute-start(bf16[1280,1152]{1,0:T(8,128)(2,1)} %collective-permute-done.1.refs_3_.refs_4_), channel_id=1, source_target_pairs={{0,7},{1,0},{2,1},{3,2},{4,3},{5,4},{6,5},{7,6},{8,15},{9,8},{10,9... | collective-permute-start | bytes 8847368 | tf_op jit(solution)/shard_map/ppermute | solution.py:194
  93.5 36.1 %collective-permute-start.4 = (bf16[1280,1152]{1,0:T(8,128)(2,1)}, bf16[1280,1152]{1,0:T(8,128)(2,1)}, u32[]{:S(2)}, u32[]{:S(2)}) collective-permute-start(bf16[1280,1152]{1,0:T(8,128)(2,1)} %collective-permute-done.2.refs_3_.refs_4_), channel_id=1, source_target_pairs={{0,1},{1,2},{2,3},{3,4},{4,5},{5,6},{6,7},{7,0},{8,9},{9,10},{10,1... | collective-permute-start | bytes 8847368 | tf_op jit(solution)/shard_map/ppermute | solution.py:192
  93.5 36.1 %collective-permute-start.5 = (bf16[1280,1152]{1,0:T(8,128)(2,1)}, bf16[1280,1152]{1,0:T(8,128)(2,1)}, u32[]{:S(2)}, u32[]{:S(2)}) collective-permute-start(bf16[1280,1152]{1,0:T(8,128)(2,1)} %collective-permute-done.3.refs_3_.refs_4_), channel_id=1, source_target_pairs={{0,7},{1,0},{2,1},{3,2},{4,3},{5,4},{6,5},{7,6},{8,15},{9,8},{10,9... | collective-permute-start | bytes 8847368 | tf_op jit(solution)/shard_map/ppermute | solution.py:194
  129.7 36.1 %collective-permute-start.6 = (bf16[1280,1152]{1,0:T(8,128)(2,1)}, bf16[1280,1152]{1,0:T(8,128)(2,1)}, u32[]{:S(2)}, u32[]{:S(2)}) collective-permute-start(bf16[1280,1152]{1,0:T(8,128)(2,1)} %collective-permute-done.4.refs_3_.refs_4_), channel_id=1, source_target_pairs={{0,1},{1,2},{2,3},{3,4},{4,5},{5,6},{6,7},{7,0},{8,9},{9,10},{10,1... | collective-permute-start | bytes 8847368 | tf_op jit(solution)/shard_map/ppermute | solution.py:192
  179.2 2.9 copy-start
  182.2 1.3 copy-start.1
  183.5 6.7 %copy-start.3 = (f32[2560]{0:T(1024)S(1)}, f32[2560]{0:T(1024)}, u32[]{:S(2)}) copy-start(f32[2560]{0:T(1024)} %param.20) | copy-start | bytes 30724
  191.3 191.4 %reduce-scatter.2.cloned.1.call-start = ((), (), s32[]{:S(2)}) async-start(), calls=%async_computation.2 | async-start | bytes 11141120 | tf_op jit(solution)/shard_map/reduce_scatter | solution.py:218
  270.6 8.8 %copy-start.5 = (bf16[2048,2560]{1,0:T(8,128)(2,1)S(1)}, bf16[2048,2560]{1,0:T(8,128)(2,1)}, u32[]{:S(2)}) copy-start(bf16[2048,2560]{1,0:T(8,128)(2,1)} %all-gather.2.cloned.1.call-done) | copy-start | bytes 31457284
  270.6 8.8 %copy-start.6 = (bf16[2560,448]{0,1:T(8,128)(2,1)S(1)}, bf16[2560,448]{0,1:T(8,128)(2,1)}, u32[]{:S(2)}) copy-start(bf16[2560,448]{0,1:T(8,128)(2,1)} %param.22) | copy-start | bytes 6881284
  279.4 5.1 %copy-start.7 = (bf16[448,2560]{1,0:T(8,128)(2,1)S(1)}, bf16[448,2560]{1,0:T(8,128)(2,1)}, u32[]{:S(2)}) copy-start(bf16[448,2560]{1,0:T(8,128)(2,1)} %param.23) | copy-start | bytes 6881284
Sparse Core Ops, SparseCore 0:
  191.4 79.1 all-gather.1
  293.1 89.5 reduce-scatter.1
